TPU v7x, 32 devices: a whole 2x2x4 slice. The times are simulated.
32 devices in a mesh: grp: 2 (over x), row: 8 (over z, y), col: 2 (over core).
Axes of the slice: x: 2, y: 2, z: 4, core: 2. Of those that a mesh axis runs over, the one named last changes fastest.
Arguments:
- green: float32 [4, 256, 256, 256], P('grp', None, 'row', 'col'), parts along dimension 0, may hold values from -6 to 6
- hamiltonian: float32 [4, 256, 256], P('grp'), parts along dimension 0
- onebody: float32 [4, 256, 256], P('grp'), parts along dimension 0, may hold values from -5 to 5
- site_map: int32 [256], replicated, may hold values from 0 to 31
- onsite_u: float32 [32], replicated, may hold values from 0.5 to 2
- pair_first: int32 [4096], replicated, may hold values from 0 to 255
- pair_second: int32 [4096], replicated, may hold values from 0 to 255
Outputs:
- advanced: float32 [4, 256, 256, 256], P('grp', None, 'row', 'col'), parts along dimension 0
There are 2 independent parts, one for each index of `grp`. A program takes and returns all parts, laid end to end along the dimension named above; an argument that names none is the same for every part. Nothing has to cross between parts.
All inputs are finite; a program needn't handle non-finite values.
Results may differ from a plain program's by a relative error of at most 0.00005.
Values sent between devices are 32-bit elements; how exact they have to be, the bound alone decides.
No kernel may reach another device: no remote copies, remote signals or barrier semaphores. Data moves between devices by JAX's collectives and lax.ppermute only.
A program may use at most 192 MiB of HBM per device.

v0:
```python
import jax
import jax.numpy as jnp
from jax import lax
from jax.sharding import PartitionSpec as P

time_step = 0.1
highest = lax.Precision.HIGHEST


def along_rows(hamiltonian, field):
    hre = hamiltonian[0]
    him = hamiltonian[1]
    out_re = jnp.einsum("ia,kaj->kij", hre, field[0], precision=highest) - jnp.einsum(
        "ia,kaj->kij", him, field[1], precision=highest
    )
    out_im = jnp.einsum("ia,kaj->kij", hre, field[1], precision=highest) + jnp.einsum(
        "ia,kaj->kij", him, field[0], precision=highest
    )
    return jnp.stack([out_re, out_im])


def along_cols(hamiltonian, field):
    hre = hamiltonian[0]
    him = hamiltonian[1]
    out_re = jnp.einsum("ja,kia->kij", hre, field[0], precision=highest) - jnp.einsum(
        "ja,kia->kij", him, field[1], precision=highest
    )
    out_im = jnp.einsum("ja,kia->kij", hre, field[1], precision=highest) + jnp.einsum(
        "ja,kia->kij", him, field[0], precision=highest
    )
    return jnp.stack([out_re, out_im])


def on_device(green, hamiltonian, onebody, site_map, onsite_u, pair_first, pair_second):
    orbs = green.shape[1]
    nrows = green.shape[2]
    ncols = green.shape[3]
    row_start = lax.axis_index("row") * nrows
    col_start = lax.axis_index("col") * ncols
    sites_i = lax.dynamic_slice_in_dim(site_map, row_start, nrows)
    sites_j = lax.dynamic_slice_in_dim(site_map, col_start, ncols)
    levels = jnp.arange(onsite_u.shape[0], dtype=jnp.int32)
    u_rows = jnp.sum(jnp.where(sites_i[:, None] == levels[None, :], onsite_u[None, :], 0.0), axis=1)
    ladder = u_rows[:, None] * (sites_i[:, None] == sites_j[None, :]).astype(jnp.float32)
    first_hot = (
        pair_first[:, None] == (row_start + jnp.arange(nrows, dtype=jnp.int32))[None, :]
    ).astype(jnp.float32)
    second_hot = (
        pair_second[:, None] == (col_start + jnp.arange(ncols, dtype=jnp.int32))[None, :]
    ).astype(jnp.float32)
    counts = jnp.einsum("pi,pj->ij", first_hot, second_hot, precision=highest)
    pauli = u_rows[:, None] * counts
    left = lax.dynamic_slice_in_dim(onebody, row_start, nrows, 2)
    right = lax.dynamic_slice_in_dim(onebody, col_start, ncols, 2)
    source_re = pauli * (
        left[0][:, :, None] * right[0][:, None, :] - left[1][:, :, None] * right[1][:, None, :]
    )
    source_im = pauli * (
        left[0][:, :, None] * right[1][:, None, :] + left[1][:, :, None] * right[0][:, None, :]
    )
    hre = hamiltonian[0]
    him = hamiltonian[1]

    def row_apply(field):
        return along_rows(hamiltonian, field)

    def col_apply(field):
        return along_cols(hamiltonian, field)

    def force(field):
        flat_re = field[0].reshape(orbs, nrows * ncols)
        flat_im = field[1].reshape(orbs, nrows * ncols)
        k_re = (
            jnp.dot(hre, flat_re, precision=highest) - jnp.dot(him, flat_im, precision=highest)
        ).reshape(orbs, nrows, ncols)
        k_im = (
            jnp.dot(hre, flat_im, precision=highest) + jnp.dot(him, flat_re, precision=highest)
        ).reshape(orbs, nrows, ncols)
        moved_rows = row_apply(
            lax.all_to_all(field, "row", split_axis=1, concat_axis=2, tiled=True)
        )
        by_rows = lax.all_to_all(moved_rows, "row", split_axis=2, concat_axis=1, tiled=True)
        moved_cols = col_apply(
            lax.all_to_all(field, "col", split_axis=1, concat_axis=3, tiled=True)
        )
        by_cols = lax.all_to_all(moved_cols, "col", split_axis=3, concat_axis=1, tiled=True)
        cross = by_rows + by_cols
        total_re = k_re + cross[0] + ladder * field[0] + source_re
        total_im = k_im + cross[1] + ladder * field[1] + source_im
        return jnp.stack([total_im, -total_re])

    half = green + 0.5 * time_step * force(green)
    return green + time_step * force(half)


def solution(mesh):
    placed = (
        P("grp", None, "row", "col"),
        P("grp", None, None),
        P("grp", None, None),
        P(),
        P(),
        P(),
        P(),
    )
    return jax.shard_map(
        on_device,
        mesh=mesh,
        in_specs=placed,
        out_specs=P("grp", None, "row", "col"),
        check_vma=False,
    )
```

profile of v0, /device:TPU:13, one launch (start us, length us, event | category | flops | bytes accessed | tf_op | source)
XLA Modules:
  0.0 987.4 jit_solution(16488565198921307543)
XLA Ops:
  7.8 12.1 %all_to_all.132 = f32[2,256,32,128]{3,2,0,1:T(8,128)} all-to-all(f32[2,256,32,128]{3,2,0,1:T(8,128)S(1)} %copy.88), channel_id=1, replica_groups=mesh['grp'=2,'row'=8,'col'=2] {'col'}, dimensions={1} | all-to-all | bytes 16777216 | tf_op jit(solution)/shard_map/all_to_all | solution.py:84
  25.6 15.3 %copy.175 = f32[2,2,128,32,128]{4,1,2,3,0:T(2,128)} copy(f32[2,2,128,32,128]{4,3,0,2,1:T(8,128)} %bitcast.225) | data formatting | bytes 16777216 | tf_op jit(solution)/shard_map/all_to_all | solution.py:84
  81.8 10.3 %copy.101 = f32[2,128,32,256]{1,2,0,3:T(8,128)} copy(f32[2,128,32,256]{3,1,2,0:T(8,128)} %pad_maximum_fusion.1) | data formatting | bytes 16777216 | tf_op jit(solution)/shard_map/stack | solution.py:31
  92.0 114.1 %all-to-all-done = f32[2,256,32,128]{3,2,0,1:T(8,128)} async-done(((f32[2,256,32,128]{3,2,0,1:T(8,128)}), f32[2,256,32,128]{3,2,0,1:T(8,128)}, u32[]{:S(2)}, u32[]{:S(2)}) %all-to-all-start) | async-done | bytes 8388640 | tf_op jit(solution)/shard_map/all_to_all | solution.py:80
  252.6 10.3 %copy.96 = f32[2,32,256,128]{3,1,0,2:T(8,128)} copy(f32[2,32,256,128]{2,3,1,0:T(8,128)} %pad_maximum_fusion) | data formatting | bytes 16777216 | tf_op jit(solution)/shard_map/stack | solution.py:19
  271.1 11.3 %copy.102 = f32[2,128,32,2,128]{4,2,1,3,0:T(8,128)} copy(f32[2,128,32,2,128]{1,2,0,4,3:T(8,128)} %bitcast.21) | data formatting | bytes 16777216 | tf_op jit(solution)/shard_map/all_to_all | solution.py:86
  317.8 133.8 %all-to-all-done.1 = f32[2,32,256,128]{3,1,0,2:T(8,128)} async-done(((f32[2,32,256,128]{3,1,0,2:T(8,128)}), f32[2,32,256,128]{3,1,0,2:T(8,128)}, u32[]{:S(2)}, u32[]{:S(2)}) %all-to-all-start.1) | async-done | bytes 8388640 | tf_op jit(solution)/shard_map/all_to_all | solution.py:82
  451.6 13.3 %copy.98 = f32[2,8,32,32,128]{4,3,2,1,0:T(8,128)} copy(f32[2,8,32,32,128]{4,2,0,3,1:T(8,128)} %bitcast.15) | data formatting | bytes 16777216 | tf_op jit(solution)/shard_map/all_to_all | solution.py:82
  464.8 11.8 %add.130 = f32[2,256,32,128]{3,2,1,0:T(8,128)} add(f32[2,256,32,128]{3,2,1,0:T(8,128)} %bitcast.223, f32[2,256,32,128]{3,2,1,0:T(8,128)} %bitcast.221) | non-fusion elementwise | flops 2097152 | bytes 25165824 | tf_op jit(solution)/shard_map/add | solution.py:87
  476.7 13.6 %fusion.12 = (f32[1,256,32,128]{3,2,1,0:T(8,128)S(1)}, f32[1,256,32,128]{3,2,1,0:T(8,128)}) fusion(f32[2,256,32,128]{3,2,1,0:T(8,128)} %add.130, f32[256,128]{1,0:T(8,128)S(1)} %get-tuple-element.24, f32[256,32]{1,0:T(8,128)S(1)} %get-tuple-element.22, f32[256,128]{1,0:T(8,128)S(1)} %get-tuple-element.23, f32[256,32]{1,0:T(8,128)S(1)} %get-tuple-element.21, ...), kind=kLoop, calls=%fused_computation.26 | loop fusion | flops 17825792 | bytes 33914880 | tf_op jit(solution)/shard_map/add | solution.py:89
  501.3 11.9 %all_to_all.133 = f32[2,256,32,128]{3,2,0,1:T(8,128)} all-to-all(f32[2,256,32,128]{3,2,0,1:T(8,128)S(1)} %copy.103), channel_id=1, replica_groups=mesh['grp'=2,'row'=8,'col'=2] {'col'}, dimensions={1} | all-to-all | bytes 16777216 | tf_op jit(solution)/shard_map/all_to_all | solution.py:84
  521.2 15.4 %copy.174 = f32[2,2,128,32,128]{4,1,2,3,0:T(2,128)} copy(f32[2,2,128,32,128]{4,3,0,2,1:T(8,128)} %bitcast.226) | data formatting | bytes 16777216 | tf_op jit(solution)/shard_map/all_to_all | solution.py:84
  577.3 10.3 %copy.116 = f32[2,128,32,256]{1,2,0,3:T(8,128)} copy(f32[2,128,32,256]{3,1,2,0:T(8,128)} %pad_maximum_fusion.3) | data formatting | bytes 16777216 | tf_op jit(solution)/shard_map/stack | solution.py:31
  587.6 114.1 %all-to-all-done.4 = f32[2,256,32,128]{3,2,0,1:T(8,128)} async-done(((f32[2,256,32,128]{3,2,0,1:T(8,128)}), f32[2,256,32,128]{3,2,0,1:T(8,128)}, u32[]{:S(2)}, u32[]{:S(2)}) %all-to-all-start.4) | async-done | bytes 8388640 | tf_op jit(solution)/shard_map/all_to_all | solution.py:80
  748.1 10.3 %copy.111 = f32[2,32,256,128]{3,1,0,2:T(8,128)} copy(f32[2,32,256,128]{2,3,1,0:T(8,128)} %pad_maximum_fusion.2) | data formatting | bytes 16777216 | tf_op jit(solution)/shard_map/stack | solution.py:19
  758.4 8.4 all-to-all-start.5
  766.8 10.9 %copy.117 = f32[2,128,32,2,128]{4,2,1,3,0:T(8,128)} copy(f32[2,128,32,2,128]{1,2,0,4,3:T(8,128)} %bitcast.47) | data formatting | bytes 16777216 | tf_op jit(solution)/shard_map/all_to_all | solution.py:86
  790.6 11.8 %convolution_add_fusion = f32[4096,256]{1,0:T(8,128)} fusion(f32[4096,256]{1,0:T(8,128)S(1)} %fusion.6, f32[32,8,32,128]{3,2,1,0:T(8,128)S(1)} %bitcast.207, f32[2,256,256]{2,1,0:T(8,128)S(1)} %copy-done.1), kind=kOutput, calls=%fused_computation.11 | convolution fusion | flops 3222274048 | bytes 12845056 | tf_op jit(solution)/shard_map/dot_general | solution.py:77
  807.9 9.8 fusion.2
  817.8 11.6 %convolution_subtract_fusion = f32[4096,256]{1,0:T(8,128)} fusion(f32[4096,256]{1,0:T(8,128)S(1)} %fusion.2, f32[32,8,32,128]{3,2,1,0:T(8,128)S(1)} %bitcast.206, f32[2,256,256]{2,1,0:T(8,128)S(1)} %copy-done.1), kind=kOutput, calls=%fused_computation.10 | convolution fusion | flops 3222274048 | bytes 12845056 | tf_op jit(solution)/shard_map/dot_general | solution.py:74
  835.1 112.3 %all-to-all-done.5 = f32[2,32,256,128]{3,1,0,2:T(8,128)} async-done(((f32[2,32,256,128]{3,1,0,2:T(8,128)}), f32[2,32,256,128]{3,1,0,2:T(8,128)}, u32[]{:S(2)}, u32[]{:S(2)}) %all-to-all-start.5) | async-done | bytes 8388640 | tf_op jit(solution)/shard_map/all_to_all | solution.py:82
  947.4 13.1 %copy.113 = f32[2,8,32,32,128]{4,3,2,1,0:T(8,128)} copy(f32[2,8,32,32,128]{4,2,0,3,1:T(8,128)} %bitcast.41) | data formatting | bytes 16777216 | tf_op jit(solution)/shard_map/all_to_all | solution.py:82
  960.5 11.3 %add.150 = f32[2,256,32,128]{3,2,1,0:T(8,128)} add(f32[2,256,32,128]{3,2,1,0:T(8,128)} %bitcast.224, f32[2,256,32,128]{3,2,1,0:T(8,128)} %bitcast.222) | non-fusion elementwise | flops 2097152 | bytes 25165824 | tf_op jit(solution)/shard_map/add | solution.py:87
  971.8 10.9 %fusion.23 = (f32[1,256,32,128]{3,2,1,0:T(8,128)S(1)}, f32[1,256,32,128]{3,2,1,0:T(8,128)S(1)}) fusion(f32[1,256,32,128]{3,2,1,0:T(8,128)} %copy.118, f32[2,256,32,128]{3,2,1,0:T(8,128)} %add.150, f32[256,128]{1,0:T(8,128)S(1)} %get-tuple-element.24, f32[256,32]{1,0:T(8,128)S(1)} %get-tuple-element.22, f32[256,128]{1,0:T(8,128)S(1)} %get-tuple-element.23, ...), kind=kLoop, calls=%fused_computation.39 | loop fusion | flops 17825792 | bytes 33914880 | tf_op jit(solution)/shard_map/add | solution.py:89
  (109 shorter events, 278.5 us)
Async XLA Ops:
  4.4 3.4 copy-start.2
  19.9 186.2 %all-to-all-start = ((f32[2,256,32,128]{3,2,0,1:T(8,128)}), f32[2,256,32,128]{3,2,0,1:T(8,128)}, u32[]{:S(2)}, u32[]{:S(2)}) async-start(f32[2,256,32,128]{3,2,0,1:T(8,128)} %copy-done.2), calls=%async_computation | async-start | bytes 16777216 | tf_op jit(solution)/shard_map/all_to_all | solution.py:80
  55.2 6.5 copy-start.1
  61.6 5.6 copy-start.7
  70.9 3.5 copy-start.9
  206.1 56.8 %all-to-all-start.3 = ((f32[2,128,32,256]{1,2,0,3:T(8,128)}), f32[2,128,32,256]{1,2,0,3:T(8,128)}, u32[]{:S(2)}, u32[]{:S(2)}) async-start(f32[2,128,32,256]{1,2,0,3:T(8,128)} %copy.101), calls=%async_computation.3 | async-start | bytes 16777216 | tf_op jit(solution)/shard_map/all_to_all | solution.py:86
  262.9 8.1 copy-start.15
  262.9 188.6 %all-to-all-start.1 = ((f32[2,32,256,128]{3,1,0,2:T(8,128)}), f32[2,32,256,128]{3,1,0,2:T(8,128)}, u32[]{:S(2)}, u32[]{:S(2)}) async-start(f32[2,32,256,128]{3,1,0,2:T(8,128)} %copy.96), calls=%async_computation.1 | async-start | bytes 16777216 | tf_op jit(solution)/shard_map/all_to_all | solution.py:82
  313.8 3.2 copy-start.13
  464.8 11.8 %copy-start.11 = (f32[32,8,32,128]{3,2,1,0:T(8,128)S(1)}, f32[32,8,32,128]{3,2,1,0:T(8,128)}, u32[]{:S(2)}) copy-start(f32[32,8,32,128]{3,2,1,0:T(8,128)} %copy.132) | copy-start | bytes 12582916
  476.7 13.6 %slice-start = ((s8[8388608]{0:T(1024)(128)(4,1)}), s8[4194304]{0:T(1024)(128)(4,1)S(1)}, s32[]{:S(2)}) async-start(s8[8388608]{0:T(1024)(128)(4,1)} %bitcast.201), calls=%async_computation.8 | async-start | bytes 8388608
  476.7 13.6 %slice-start.1 = ((s8[8388608]{0:T(1024)(128)(4,1)}), s8[4194304]{0:T(1024)(128)(4,1)S(1)}, s32[]{:S(2)}) async-start(s8[8388608]{0:T(1024)(128)(4,1)} %bitcast.201), calls=%async_computation.9 | async-start | bytes 8388608
  494.0 4.0 copy-start
  498.0 3.3 copy-start.3
  513.2 188.5 %all-to-all-start.4 = ((f32[2,256,32,128]{3,2,0,1:T(8,128)}), f32[2,256,32,128]{3,2,0,1:T(8,128)}, u32[]{:S(2)}, u32[]{:S(2)}) async-start(f32[2,256,32,128]{3,2,0,1:T(8,128)} %copy-done.3), calls=%async_computation.4 | async-start | bytes 16777216 | tf_op jit(solution)/shard_map/all_to_all | solution.py:80
  557.2 5.6 copy-start.8
  566.4 3.5 copy-start.10
  701.7 56.7 %all-to-all-start.7 = ((f32[2,128,32,256]{1,2,0,3:T(8,128)}), f32[2,128,32,256]{1,2,0,3:T(8,128)}, u32[]{:S(2)}, u32[]{:S(2)}) async-start(f32[2,128,32,256]{1,2,0,3:T(8,128)} %copy.116), calls=%async_computation.7 | async-start | bytes 16777216 | tf_op jit(solution)/shard_map/all_to_all | solution.py:86
  758.4 188.9 %all-to-all-start.5 = ((f32[2,32,256,128]{3,1,0,2:T(8,128)}), f32[2,32,256,128]{3,1,0,2:T(8,128)}, u32[]{:S(2)}, u32[]{:S(2)}) async-start(f32[2,32,256,128]{3,1,0,2:T(8,128)} %copy.111), calls=%async_computation.5 | async-start | bytes 16777216 | tf_op jit(solution)/shard_map/all_to_all | solution.py:82
  782.2 8.4 copy-start.4
  782.2 8.4 copy-start.6
  807.9 9.8 copy-start.5
  960.5 22.3 %slice-start.2 = ((s8[8388608]{0:T(1024)(128)(4,1)}), s8[4194304]{0:T(1024)(128)(4,1)S(1)}, s32[]{:S(2)}) async-start(s8[8388608]{0:T(1024)(128)(4,1)} %bitcast.203), calls=%async_computation.10 | async-start | bytes 8388608
  971.8 10.9 %slice-start.3 = ((s8[8388608]{0:T(1024)(128)(4,1)}), s8[4194304]{0:T(1024)(128)(4,1)S(1)}, s32[]{:S(2)}) async-start(s8[8388608]{0:T(1024)(128)(4,1)} %bitcast.203), calls=%async_computation.11 | async-start | bytes 8388608
  (3 other events, 8.9 us)
where the time goes:
time: 1000 us; the launch traced here: 987 us
  waiting for transfers between devices  474 us (47%)
  local copies, waits for them, and re-layouts  216 us (22%)
  matrix products  155 us (16%)
  other arithmetic  71.4 us (7%)
  starting transfers between devices  45.8 us (5%)
  blocking collectives  24 us (2%)
    all_to_all x2, waiting for transfers between devices, force(): lax.all_to_all(moved_rows, 'row', split_axis=2, concat_axis=1, tiled=True)  246 us
    all_to_all x2, waiting for transfers between devices, force(): lax.all_to_all(field, 'row', split_axis=1, concat_axis=2, tiled=True)  228 us
    all_to_all x2, local copies, waits for them, and re-layouts, force(): lax.all_to_all(field, 'col', split_axis=1, concat_axis=3, tiled=True)  30.8 us
    all_to_all x2, local copies, waits for them, and re-layouts, force(): lax.all_to_all(moved_rows, 'row', split_axis=2, concat_axis=1, tiled=True)  26.4 us
    add x2, other arithmetic, force(): total_im = k_im + cross[1] + ladder * field[1] + source_im  24.5 us
    all_to_all x2, blocking collectives, force(): lax.all_to_all(field, 'col', split_axis=1, concat_axis=3, tiled=True)  24 us
    add x2, other arithmetic, force(): cross = by_rows + by_cols  23.2 us
    all_to_all x2, local copies, waits for them, and re-layouts, force(): lax.all_to_all(moved_cols, 'col', split_axis=3, concat_axis=1, tiled=True)  22.2 us
  transfers between devices with their start and end apart: 6, of which 4 were waited for; matrix products, arithmetic and copies ran while one was open for 35% of the time, Pallas kernels for 0%

commit v1 on v0

v1 whole, which is shorter than its diff:
```python
import jax
import jax.numpy as jnp
from jax import lax
from jax.sharding import PartitionSpec as P

time_step = 0.1
highest = lax.Precision.HIGHEST


def dot(a, b):
    return jnp.dot(a, b, precision=highest)


def neg_i(x, scale):
    return jnp.stack([scale * x[1], -scale * x[0]])


def make_on_device(nrow):
    def on_device(green, hamiltonian, onebody, site_map, onsite_u, pair_first, pair_second):
        orbs = green.shape[1]
        nrows = green.shape[2]
        ncols = green.shape[3]
        jb = ncols // nrow
        r = lax.axis_index("row")
        c = lax.axis_index("col")
        row_start = r * nrows
        col_start = c * ncols
        sub_start = col_start + r * jb
        levels = jnp.arange(onsite_u.shape[0], dtype=jnp.int32)
        orb_ids = jnp.arange(orbs, dtype=jnp.int32)
        u_all = jnp.sum(jnp.where(site_map[:, None] == levels[None, :], onsite_u[None, :], 0.0), axis=1)
        first_hot = (pair_first[:, None] == orb_ids[None, :]).astype(jnp.float32)
        second_hot = (pair_second[:, None] == orb_ids[None, :]).astype(jnp.float32)
        hre = hamiltonian[0]
        him = hamiltonian[1]

        sites_i = lax.dynamic_slice_in_dim(site_map, row_start, nrows)
        sites_j = lax.dynamic_slice_in_dim(site_map, col_start, ncols)
        u_i = lax.dynamic_slice_in_dim(u_all, row_start, nrows)
        lad_a = u_i[:, None] * (sites_i[:, None] == sites_j[None, :]).astype(jnp.float32)
        fh_a = lax.dynamic_slice_in_dim(first_hot, row_start, nrows, 1)
        sh_a = lax.dynamic_slice_in_dim(second_hot, col_start, ncols, 1)
        pauli_a = u_i[:, None] * jnp.einsum("pi,pj->ij", fh_a, sh_a, precision=highest)
        left = lax.dynamic_slice_in_dim(onebody, row_start, nrows, 2)
        right = lax.dynamic_slice_in_dim(onebody, col_start, ncols, 2)
        src_a = jnp.stack([
            pauli_a * (left[0][:, :, None] * right[0][:, None, :] - left[1][:, :, None] * right[1][:, None, :]),
            pauli_a * (left[0][:, :, None] * right[1][:, None, :] + left[1][:, :, None] * right[0][:, None, :]),
        ])

        sites_s = lax.dynamic_slice_in_dim(site_map, sub_start, jb)
        lad_b = u_all[None, :] * (sites_s[:, None] == site_map[None, :]).astype(jnp.float32)
        sh_b = lax.dynamic_slice_in_dim(second_hot, sub_start, jb, 1)
        pauli_b = u_all[None, :] * jnp.einsum("pj,pi->ji", sh_b, first_hot, precision=highest)
        g_s = lax.dynamic_slice_in_dim(onebody, sub_start, jb, 2)
        g_all = onebody
        src_b = jnp.stack([
            pauli_b * (g_s[0][:, :, None] * g_all[0][:, None, :] - g_s[1][:, :, None] * g_all[1][:, None, :]),
            pauli_b * (g_s[1][:, :, None] * g_all[0][:, None, :] + g_s[0][:, :, None] * g_all[1][:, None, :]),
        ])

        h_own = lax.dynamic_slice_in_dim(hamiltonian, col_start, ncols, 1)
        hre_own_t = h_own[0].T
        him_own_t = h_own[1].T

        def apply_j(x):
            full = lax.all_gather(x, "col", axis=3, tiled=True)
            fr = full[0].reshape(orbs * nrows, orbs)
            fi = full[1].reshape(orbs * nrows, orbs)
            out_re = dot(fr, hre_own_t) - dot(fi, him_own_t)
            out_im = dot(fi, hre_own_t) + dot(fr, him_own_t)
            return jnp.stack([out_re, out_im]).reshape(2, orbs, nrows, ncols)

        def apply_ki(x):
            xr = x[0]
            xi = x[1]
            kr = xr.reshape(orbs, jb * orbs)
            ki = xi.reshape(orbs, jb * orbs)
            k_re = (dot(hre, kr) - dot(him, ki)).reshape(orbs, jb, orbs)
            k_im = (dot(hre, ki) + dot(him, kr)).reshape(orbs, jb, orbs)
            ir = xr.reshape(orbs * jb, orbs)
            ii = xi.reshape(orbs * jb, orbs)
            i_re = (dot(ir, hre.T) - dot(ii, him.T)).reshape(orbs, jb, orbs)
            i_im = (dot(ii, hre.T) + dot(ir, him.T)).reshape(orbs, jb, orbs)
            return jnp.stack([k_re + i_re, k_im + i_im])

        def to_split(x):
            send = x.reshape(2, orbs, nrows, nrow, jb).transpose(3, 0, 1, 4, 2)
            send = send.reshape(nrow, 2, orbs, jb * nrows)
            got = lax.all_to_all(send, "row", 0, 0, tiled=True)
            got = got.reshape(nrow, 2, orbs, jb, nrows).transpose(1, 2, 3, 0, 4)
            return got.reshape(2, orbs, jb, nrow * nrows)

        def from_split(y):
            send = y.reshape(2, orbs, jb, nrow, nrows).transpose(3, 0, 1, 2, 4)
            send = send.reshape(nrow, 2, orbs, jb * nrows)
            got = lax.all_to_all(send, "row", 0, 0, tiled=True)
            got = got.reshape(nrow, 2, orbs, jb, nrows).transpose(1, 2, 4, 0, 3)
            return got.reshape(2, orbs, nrows, ncols)

        dt = time_step
        dt2 = 0.5 * time_step * time_step
        g = green
        g_b = to_split(g)
        p = apply_j(g)
        p_b = to_split(p)
        q = apply_ki(g_b) + lad_b * g_b
        e = p_b + q + src_b
        w = e + p_b
        part_b = neg_i(q, dt) - dt2 * (apply_ki(w) + lad_b * e)
        part_b_a = from_split(part_b)
        e2 = p + lad_a * g + src_a
        part_a = g + neg_i(p + src_a, dt) - dt2 * apply_j(e2)
        return part_a + part_b_a

    return on_device


def solution(mesh):
    placed = (
        P("grp", None, "row", "col"),
        P("grp", None, None),
        P("grp", None, None),
        P(),
        P(),
        P(),
        P(),
    )
    return jax.shard_map(
        make_on_device(mesh.shape["row"]),
        mesh=mesh,
        in_specs=placed,
        out_specs=P("grp", None, "row", "col"),
        check_vma=False,
    )
```

time: 1000 us -> 913 us (0.913)
  waiting for transfers between devices: 474 us -> 202 us
  local copies, waits for them, and re-layouts: 216 us -> 348 us
  other arithmetic: 71.4 us -> 153 us
  starting transfers between devices: 45.8 us -> 18.1 us
  blocking collectives: 24 us -> 0 us
  between operations: 0.78 us -> 14.3 us
    all_to_all x6 -> x3, waiting for transfers between devices: 474 us -> 201 us  [the longest x1 135 us: from_split(): got = lax.all_to_all(send, 'row', 0, 0, tiled=True)]
    reshape x2 -> x13, local copies, waits for them, and re-layouts: 11.2 us -> 129 us  [the longest x5 54.1 us: apply_ki(): i_im = (dot(ii, hre.T) + dot(ir, him.T)).reshape(orbs, jb, orbs)]
    all_to_all x8 -> x0, local copies, waits for them, and re-layouts: 88.1 us -> none  [the longest x2 30.8 us: force(): lax.all_to_all(field, 'col', split_axis=1, concat_axis=3, tiled=True)]
    transpose x0 -> x5, local copies, waits for them, and re-layouts: none -> 67.1 us  [the longest x2 38.8 us: to_split(): send = x.reshape(2, orbs, nrows, nrow, jb).transpose(3, 0, 1, 4, 2)]
    slice x10 -> x11, local copies, waits for them, and re-layouts: 29 us -> 79.5 us  [the longest x5 40.9 us: apply_ki(): xr = x[0]]
    mul x1 -> x8, other arithmetic: 0.07 us -> 30.3 us  [the longest x2 15.7 us: neg_i(): return jnp.stack([scale * x[1], -scale * x[0]])]
    all_to_all x6 -> x3, starting transfers between devices: 45.8 us -> 18.1 us  [the longest x2 12.7 us: to_split(): got = lax.all_to_all(send, 'row', 0, 0, tiled=True)]
    squeeze x4 -> x0, local copies, waits for them, and re-layouts: 25.9 us -> none  [the longest x2 13 us: along_cols(): field[1]]
  transfers between devices with their start and end apart: 6 -> 5, of which waited for: 4 -> 2; matrix products, arithmetic and copies ran while one was open for 35% -> 69% of each run, Pallas kernels for 0% -> 0%
where the time goes in v1:
time: 913 us; the launch traced here: 899 us
  local copies, waits for them, and re-layouts  348 us (38%)
  waiting for transfers between devices  202 us (22%)
  matrix products  163 us (18%)
  other arithmetic  153 us (17%)
  starting transfers between devices  18.1 us (2%)
  between operations  14.3 us (2%)
    dot_general x24, matrix products, dot(): return jnp.dot(a, b, precision=highest)  159 us
    all_to_all x1, waiting for transfers between devices, from_split(): got = lax.all_to_all(send, 'row', 0, 0, tiled=True)  135 us
    all_to_all x2, waiting for transfers between devices, to_split(): got = lax.all_to_all(send, 'row', 0, 0, tiled=True)  66.7 us
    reshape x5, local copies, waits for them, and re-layouts, apply_ki(): i_im = (dot(ii, hre.T) + dot(ir, him.T)).reshape(orbs, jb, orbs)  54.1 us
    reshape x5, local copies, waits for them, and re-layouts, apply_ki(): i_re = (dot(ir, hre.T) - dot(ii, him.T)).reshape(orbs, jb, orbs)  53.6 us
    slice x5, local copies, waits for them, and re-layouts, apply_ki(): xr = x[0]  40.9 us
    transpose x2, local copies, waits for them, and re-layouts, to_split(): send = x.reshape(2, orbs, nrows, nrow, jb).transpose(3, 0, 1, 4, 2)  38.8 us
    slice x3, local copies, waits for them, and re-layouts, apply_ki(): xi = x[1]  24.8 us
  transfers between devices with their start and end apart: 5, of which 2 were waited for; matrix products, arithmetic and copies ran while one was open for 69% of the time, Pallas kernels for 0%

profile of v1, /device:TPU:13, one launch (start us, length us, event | category | flops | bytes accessed | tf_op | source)
XLA Modules:
  0.0 898.9 jit_solution(4371925586831101845)
XLA Ops:
  17.2 17.1 %copy.129 = f32[8,2,256,16,32]{2,4,3,1,0:T(8,128)} copy(f32[8,2,256,16,32]{2,3,0,4,1:T(8,128)} %bitcast.187) | data formatting | bytes 16777216 | tf_op jit(solution)/shard_map/transpose | solution.py:88
  66.0 11.0 %stack.74 = f32[1,256,32,8,16]{2,1,4,3,0:T(8,128)} reshape(f32[8192,128]{0,1:T(8,128)} %fusion.1) | data formatting | bytes 8388608 | tf_op jit(solution)/shard_map/stack | solution.py:72
  77.0 11.0 %fusion.66 = f32[128,8192]{1,0:T(8,128)S(1)} fusion(f32[8192,256]{1,0:T(8,128)} %bitcast.163, f32[2,256,256]{2,1,0:T(8,128)S(1)} %copy-done.5, s32[]{:T(128)S(6)} %select_n.10), kind=kOutput, calls=%fused_computation.109 | convolution fusion | flops 3221225472 | bytes 12713988 | tf_op jit(solution)/shard_map/dot_general | solution.py:11
  109.0 23.1 %maximum_bitcast_fusion = f32[8,2,256,16,32]{4,2,3,0,1:T(8,128)} fusion(f32[1,256,32,8,16]{2,1,4,3,0:T(8,128)} %stack.75, f32[1,256,32,8,16]{2,1,4,3,0:T(8,128)} %stack.74), kind=kLoop, calls=%fused_computation | loop fusion | flops 2097152 | bytes 16777216 | tf_op jit(solution)/shard_map/transpose | solution.py:88
  132.1 21.7 %copy.141 = f32[8,2,256,16,32]{2,4,3,1,0:T(8,128)} copy(f32[8,2,256,16,32]{4,2,3,0,1:T(8,128)} %maximum_bitcast_fusion) | data formatting | bytes 16777216 | tf_op jit(solution)/shard_map/transpose | solution.py:88
  153.8 66.7 %all-to-all-done = f32[8,2,256,512]{2,3,1,0:T(8,128)} async-done(((f32[8,2,256,512]{2,3,1,0:T(8,128)}), f32[8,2,256,512]{2,3,1,0:T(8,128)}, u32[]{:S(2)}, u32[]{:S(2)}) %all-to-all-start) | async-done | bytes 8388640 | tf_op jit(solution)/shard_map/all_to_all | solution.py:90
  258.9 14.5 %copy.132 = f32[1,256,16,8,32]{4,3,2,1,0:T(8,128)} copy(f32[1,256,16,8,32]{1,4,2,0,3:T(8,128)} %get-tuple-element.19) | data formatting | bytes 8388608 | tf_op jit(solution)/shard_map/slice | solution.py:75
  278.3 14.5 %copy.133 = f32[1,256,16,8,32]{4,3,2,1,0:T(8,128)} copy(f32[1,256,16,8,32]{1,4,2,0,3:T(8,128)} %get-tuple-element.20) | data formatting | bytes 8388608 | tf_op jit(solution)/shard_map/slice | solution.py:76
  305.8 12.2 %reshape_squeeze.42 = f32[4096,256]{1,0:T(8,128)} reshape(f32[1,256,16,8,32]{4,3,2,1,0:T(8,128)} %copy.132) | data formatting | bytes 8388608 | tf_op jit(solution)/shard_map/reshape;squeeze | solution.py:81
  318.0 12.3 %reshape_squeeze.43 = f32[4096,256]{1,0:T(8,128)} reshape(f32[1,256,16,8,32]{4,3,2,1,0:T(8,128)} %copy.133) | data formatting | bytes 8388608 | tf_op jit(solution)/shard_map/reshape;squeeze | solution.py:82
  384.4 10.9 %reshape.391 = f32[1,256,16,8,32]{4,3,2,1,0:T(8,128)} reshape(f32[4096,256]{1,0:T(8,128)} %convolution_add_fusion.4) | data formatting | bytes 8388608 | tf_op jit(solution)/shard_map/reshape | solution.py:84
  417.2 13.3 %copy.155 = f32[1,256,16,8,32]{1,4,2,0,3:T(8,128)} copy(f32[1,256,16,8,32]{4,3,2,1,0:T(8,128)} %reshape.389) | data formatting | bytes 8388608 | tf_op jit(solution)/shard_map/reshape | solution.py:83
  430.5 13.6 %copy.158 = f32[1,256,16,8,32]{1,4,2,0,3:T(8,128)} copy(f32[1,256,16,8,32]{4,3,2,1,0:T(8,128)} %reshape.391) | data formatting | bytes 8388608 | tf_op jit(solution)/shard_map/reshape | solution.py:84
  454.2 12.2 %copy_add_fusion = (f32[1,256,16,8,32]{1,4,2,0,3:T(8,128)}, f32[1,256,16,8,32]{1,4,2,0,3:T(8,128)}) fusion(f32[1,256,16,8,32]{1,4,2,0,3:T(8,128)} %copy.158, f32[1,256,16,8,32]{1,4,3,2,0:T(8,128)} %bitcast.180, f32[1,256,16,8,32]{1,4,2,0,3:T(8,128)} %copy.155, f32[1,256,16,8,32]{1,4,3,2,0:T(8,128)} %bitcast.179), kind=kLoop, calls=%fused_computation.40 | loop fusion | flops 2097152 | bytes 25165824 | tf_op jit(solution)/shard_map/add | solution.py:85
  477.6 15.9 %add_add_fusion = (f32[2,256,32,128]{3,2,1,0:T(8,128)}, f32[2,256,32,128]{3,2,1,0:T(8,128)}) fusion(f32[2,256,32,128]{3,2,1,0:T(8,128)} %param.7, f32[1,256,32,128]{3,2,1,0:T(8,128)} %get-tuple-element.26, f32[1,256,32,128]{3,2,1,0:T(8,128)} %get-tuple-element.25, f32[1,256,32,128]{3,2,1,0:T(8,128)} %bitcast.192, f32[1,256,32,128]{3,2,1,0:T(8,128)} %bitcast.191, ...), kind=kLoop, calls=%fused_computation.26 | loop fusion | flops 12582912 | bytes 41959424 | tf_op jit(solution)/shard_map/add | solution.py:112
  502.0 24.8 %fusion.4 = (f32[2,256,16,256]{1,3,2,0:T(8,128)}, f32[2,256,16,256]{1,3,2,0:T(8,128)}) fusion(f32[1,256,16,256]{1,3,2,0:T(8,128)} %get-tuple-element.24, f32[1,256,16,256]{1,3,2,0:T(8,128)} %get-tuple-element.23, f32[2,256,16,8,32]{1,4,3,2,0:T(8,128)} %copy.142, f32[2,256,16,8,32]{1,4,3,2,0:T(8,128)} %copy.138, f32[16,256]{1,0:T(8,128)S(1)} %compare_select_fusion.1, ...), kind=kLoop, calls=%fused_computation.16 | loop fusion | flops 14680064 | bytes 50348032 | tf_op jit(solution)/shard_map/add | solution.py:109
  569.0 10.9 %reshape.385 = f32[1,256,16,8,32]{4,3,2,1,0:T(8,128)} reshape(f32[4096,256]{1,0:T(8,128)} %convolution_subtract_fusion.2) | data formatting | bytes 8388608 | tf_op jit(solution)/shard_map/reshape | solution.py:83
  579.8 13.2 %copy.150 = f32[1,256,16,8,32]{1,4,2,0,3:T(8,128)} copy(f32[1,256,16,8,32]{4,3,2,1,0:T(8,128)} %reshape.385) | data formatting | bytes 8388608 | tf_op jit(solution)/shard_map/reshape | solution.py:83
  593.1 10.9 %reshape.387 = f32[1,256,16,8,32]{4,3,2,1,0:T(8,128)} reshape(f32[4096,256]{1,0:T(8,128)} %convolution_add_fusion.2) | data formatting | bytes 8388608 | tf_op jit(solution)/shard_map/reshape | solution.py:84
  604.0 13.4 %copy.152 = f32[1,256,16,8,32]{1,4,2,0,3:T(8,128)} copy(f32[1,256,16,8,32]{4,3,2,1,0:T(8,128)} %reshape.387) | data formatting | bytes 8388608 | tf_op jit(solution)/shard_map/reshape | solution.py:84
  651.0 16.5 %fusion.6 = f32[2,256,16,8,32]{1,4,2,0,3:T(8,128)} fusion(f32[1,256,16,8,32]{1,4,2,0,3:T(8,128)S(1)} %copy_add_fusion.2, f32[1,256,16,8,32]{1,4,2,0,3:T(8,128)S(1)} %copy_add_fusion.3, f32[2,256,16,8,32]{1,4,2,0,3:T(8,128)} %bitcast.36, f32[1,256,16,8,32]{1,4,2,0,3:T(8,128)} %get-tuple-element.37, f32[1,256,16,8,32]{1,4,2,0,3:T(8,128)} %get-tuple-element.38, ...), kind=kLoop, calls=%fused_computation.19 | loop fusion | flops 25165824 | bytes 58736640 | tf_op jit(solution)/shard_map/sub | solution.py:110
  718.7 134.7 %all-to-all-done.2 = f32[8,2,256,512]{2,3,1,0:T(8,128)} async-done(((f32[8,2,256,512]{2,3,1,0:T(8,128)}), f32[8,2,256,512]{2,3,1,0:T(8,128)}, u32[]{:S(2)}, u32[]{:S(2)}) %all-to-all-start.2) | async-done | bytes 8388640 | tf_op jit(solution)/shard_map/all_to_all | solution.py:97
  853.5 11.6 %copy.162 = f32[2,256,32,8,16]{1,4,3,2,0:T(8,128)} copy(f32[2,256,32,8,16]{1,2,4,0,3:T(8,128)} %bitcast.58) | data formatting | bytes 16777216 | tf_op jit(solution)/shard_map/transpose | solution.py:98
  875.3 16.3 %fusion.3 = f32[2,256,32,128]{3,2,1,0:T(8,128)} fusion(f32[2,256,32,128]{3,2,1,0:T(8,128)} %copy.163, f32[2,256,32,128]{3,2,1,0:T(8,128)} %param.7, f32[1,256,32,128]{3,2,1,0:T(8,128)} %get-tuple-element.14, f32[1,256,32,128]{3,2,1,0:T(8,128)} %get-tuple-element.13, f32[1,256,32,128]{3,2,1,0:T(8,128)} %bitcast.183, f32[1,256,32,128]{3,2,1,0:T(8,128)} %bitcast.182), kind=kLoop, calls=%fused_computation.11 | loop fusion | flops 12582912 | bytes 41943040 | tf_op jit(solution)/shard_map/add | solution.py:114
  (133 shorter events, 362.3 us)
Async XLA Ops:
  6.5 33.6 %all-gather.3.cloned.1.call-start = ((), (), s32[]{:S(2)}) async-start(), calls=%async_computation.3 | async-start | bytes 25165824 | tf_op jit(solution)/shard_map/all_gather | solution.py:67
  34.2 186.3 %all-to-all-start = ((f32[8,2,256,512]{2,3,1,0:T(8,128)}), f32[8,2,256,512]{2,3,1,0:T(8,128)}, u32[]{:S(2)}, u32[]{:S(2)}) async-start(f32[8,2,256,512]{2,3,1,0:T(8,128)} %bitcast.185), calls=%async_computation | async-start | bytes 16777216 | tf_op jit(solution)/shard_map/all_to_all | solution.py:90
  40.1 6.9 copy-start.5
  46.9 8.9 copy-start
  46.9 8.9 copy-start.2
  77.0 11.0 %copy-start.1 = (f32[1,256,32,256]{3,2,1,0:T(8,128)S(1)}, f32[1,256,32,256]{3,2,1,0:T(8,128)}, u32[]{:S(2)}) copy-start(f32[1,256,32,256]{3,2,1,0:T(8,128)} %copy-done) | copy-start | bytes 25165828
  220.5 6.9 copy-start.22
  220.5 7.0 copy-start.23
  220.5 7.4 copy-start.18
  220.5 8.0 copy-start.20
  220.5 8.0 copy-start.21
  220.5 273.0 %all-to-all-start.1 = ((f32[8,2,256,512]{2,3,1,0:T(8,128)}), f32[8,2,256,512]{2,3,1,0:T(8,128)}, u32[]{:S(2)}, u32[]{:S(2)}) async-start(f32[8,2,256,512]{2,3,1,0:T(8,128)} %bitcast.184), calls=%async_computation.1 | async-start | bytes 16777216 | tf_op jit(solution)/shard_map/all_to_all | solution.py:90
  227.4 453.3 %all-gather.5.cloned.1.call-start = ((), (), s32[]{:S(2)}) async-start(), calls=%async_computation.4 | async-start | bytes 25165824 | tf_op jit(solution)/shard_map/all_gather | solution.py:67
  330.4 5.5 copy-start.7
  357.1 5.6 copy-start.9
  373.7 5.6 copy-start.6
  400.6 5.6 copy-start.8
  444.1 6.4 copy-start.12
  444.1 7.4 copy-start.16
  553.1 5.7 copy-start.11
  553.1 5.7 copy-start.17
  617.4 7.9 copy-start.4
  636.9 6.2 copy-start.14
  667.5 186.0 %all-to-all-start.2 = ((f32[8,2,256,512]{2,3,1,0:T(8,128)}), f32[8,2,256,512]{2,3,1,0:T(8,128)}, u32[]{:S(2)}, u32[]{:S(2)}) async-start(f32[8,2,256,512]{2,3,1,0:T(8,128)} %bitcast.188), calls=%async_computation.2 | async-start | bytes 16777216 | tf_op jit(solution)/shard_map/all_to_all | solution.py:97
  (5 other events, 15.2 us)
Sparse Core Ops, SparseCore 0:
  8.9 31.0 all-gather.2
  493.6 32.1 all-gather.4

commit v2 on v1

v2 whole, which is shorter than its diff:
```python
import jax
import jax.numpy as jnp
from jax import lax
from jax.sharding import PartitionSpec as P

time_step = 0.1
highest = lax.Precision.HIGHEST


def neg_i(x, scale):
    return jnp.stack([scale * x[1], -scale * x[0]])


def make_on_device(nrow, ncol):
    ndev = nrow * ncol

    def on_device(green, hamiltonian, onebody, site_map, onsite_u, pair_first, pair_second):
        orbs = green.shape[1]
        nrows = green.shape[2]
        ncols = green.shape[3]
        kb = orbs // ndev
        r = lax.axis_index("row")
        c = lax.axis_index("col")
        row_start = r * nrows
        col_start = c * ncols
        k_start = (r * ncol + c) * kb
        levels = jnp.arange(onsite_u.shape[0], dtype=jnp.int32)
        orb_ids = jnp.arange(orbs, dtype=jnp.int32)
        u_all = jnp.sum(jnp.where(site_map[:, None] == levels[None, :], onsite_u[None, :], 0.0), axis=1)
        first_hot = (pair_first[:, None] == orb_ids[None, :]).astype(jnp.float32)
        second_hot = (pair_second[:, None] == orb_ids[None, :]).astype(jnp.float32)
        hre = hamiltonian[0]
        him = hamiltonian[1]
        h_big = jnp.concatenate(
            [jnp.concatenate([hre, -him], axis=1), jnp.concatenate([him, hre], axis=1)], axis=0
        )
        hre_t = hre.T
        him_t = him.T

        sites_i = lax.dynamic_slice_in_dim(site_map, row_start, nrows)
        sites_j = lax.dynamic_slice_in_dim(site_map, col_start, ncols)
        u_i = lax.dynamic_slice_in_dim(u_all, row_start, nrows)
        lad_a = u_i[:, None] * (sites_i[:, None] == sites_j[None, :]).astype(jnp.float32)
        fh_a = lax.dynamic_slice_in_dim(first_hot, row_start, nrows, 1)
        sh_a = lax.dynamic_slice_in_dim(second_hot, col_start, ncols, 1)
        pauli_a = u_i[:, None] * jnp.einsum("pi,pj->ij", fh_a, sh_a, precision=highest)
        left = lax.dynamic_slice_in_dim(onebody, row_start, nrows, 2)
        right = lax.dynamic_slice_in_dim(onebody, col_start, ncols, 2)
        src_a = jnp.stack([
            pauli_a * (left[0][:, :, None] * right[0][:, None, :] - left[1][:, :, None] * right[1][:, None, :]),
            pauli_a * (left[0][:, :, None] * right[1][:, None, :] + left[1][:, :, None] * right[0][:, None, :]),
        ])

        lad_k = u_all[:, None] * (site_map[:, None] == site_map[None, :]).astype(jnp.float32)
        pauli_k = u_all[:, None] * jnp.einsum("pi,pj->ij", first_hot, second_hot, precision=highest)
        gk = lax.dynamic_slice_in_dim(onebody, k_start, kb, 1)
        gi_r = gk[0].T[:, :, None]
        gi_i = gk[1].T[:, :, None]
        gj_r = gk[0][None, :, :]
        gj_i = gk[1][None, :, :]
        pk = pauli_k[:, None, :]
        src_k = jnp.stack([pk * (gi_r * gj_r - gi_i * gj_i), pk * (gi_r * gj_i + gi_i * gj_r)])
        lad_kb = lad_k[:, None, :]

        def left_mul(x):
            shp = x.shape
            flat = x.reshape(2 * shp[1], shp[2], shp[3])
            out = jnp.einsum("ab,bmn->amn", h_big, flat, precision=highest)
            return out.reshape(shp)

        def right_mul(x):
            xr = x[0]
            xi = x[1]
            out_re = jnp.einsum("ikj,nj->ikn", xr, hre, precision=highest) - jnp.einsum(
                "ikj,nj->ikn", xi, him, precision=highest
            )
            out_im = jnp.einsum("ikj,nj->ikn", xr, him, precision=highest) + jnp.einsum(
                "ikj,nj->ikn", xi, hre, precision=highest
            )
            return jnp.stack([out_re, out_im])

        def apply_ij(x):
            return left_mul(x) + right_mul(x)

        def to_k(x):
            xs = x.reshape(2, ndev, kb, nrows, ncols)
            got = lax.all_to_all(xs, ("row", "col"), 1, 1, tiled=True)
            got = got.reshape(2, nrow, ncol, kb, nrows, ncols).transpose(0, 1, 4, 3, 2, 5)
            return got.reshape(2, nrow * nrows, kb, ncol * ncols)

        def from_k(y):
            ys = y.reshape(2, nrow, nrows, kb, ncol, ncols).transpose(0, 1, 4, 3, 2, 5)
            ys = ys.reshape(2, ndev, kb, nrows, ncols)
            got = lax.all_to_all(ys, ("row", "col"), 1, 1, tiled=True)
            return got.reshape(2, orbs, nrows, ncols)

        dt = time_step
        dt2 = 0.5 * time_step * time_step
        g = green
        g_k = to_k(g)
        p = left_mul(g)
        p_k = to_k(p)
        q = apply_ij(g_k) + lad_kb * g_k
        e = p_k + q + src_k
        w = e + p_k
        part_k = neg_i(q, dt) - dt2 * (apply_ij(w) + lad_kb * e)
        part_k_a = from_k(part_k)
        e2 = p + lad_a * g + src_a
        part_a = g + neg_i(p + src_a, dt) - dt2 * left_mul(e2)
        return part_a + part_k_a

    return on_device


def solution(mesh):
    placed = (
        P("grp", None, "row", "col"),
        P("grp", None, None),
        P("grp", None, None),
        P(),
        P(),
        P(),
        P(),
    )
    return jax.shard_map(
        make_on_device(mesh.shape["row"], mesh.shape["col"]),
        mesh=mesh,
        in_specs=placed,
        out_specs=P("grp", None, "row", "col"),
        check_vma=False,
    )
```

time: 913 us -> 858 us (0.940)
  waiting for transfers between devices: 202 us -> 412 us
  local copies, waits for them, and re-layouts: 348 us -> 194 us
  other arithmetic: 153 us -> 32 us
  matrix products: 163 us -> 193 us
  between operations: 14.3 us -> 0.49 us
    all_to_all x3, waiting for transfers between devices: 201 us -> 412 us  [the longest x2 266 us: to_k(): got = lax.all_to_all(xs, ('row', 'col'), 1, 1, tiled=True)]
    reshape x13 -> x5, local copies, waits for them, and re-layouts: 129 us -> 57.5 us  [the longest x2 23.1 us: to_k(): return got.reshape(2, nrow * nrows, kb, ncol * ncols)]
    add x7 -> x0, other arithmetic: 64.6 us -> none  [the longest x1 24.8 us: on_device(): w = e + p_b]
    slice x11 -> x3, local copies, waits for them, and re-layouts: 79.5 us -> 17.6 us  [the longest x2 11.4 us: right_mul(): xi = x[1]]
    dot_general x25 -> x13, matrix products: 161 us -> 191 us  [the longest x4 140 us: left_mul(): out = jnp.einsum('ab,bmn->amn', h_big, flat, precision=highest)]
    another operation x4 -> x2, local copies, waits for them, and re-layouts: 46.3 us -> 15.9 us  [the longest x1 11.6 us: left_mul(): flat = x.reshape(2 * shp[1], shp[2], shp[3])]
    add x1 -> x3, local copies, waits for them, and re-layouts: 5.59 us -> 31.3 us  [the longest x1 11.6 us: on_device(): return part_a + part_k_a]
    transpose x5 -> x4, local copies, waits for them, and re-layouts: 67.1 us -> 42.7 us  [the longest x2 31.2 us: to_k(): got.reshape(2, nrow, ncol, kb, nrows, ncols).transpose(0, 1, 4, 3, 2, 5)]
  transfers between devices with their start and end apart: 5 -> 3, of which waited for: 2 -> 3; matrix products, arithmetic and copies ran while one was open for 69% -> 16% of each run, Pallas kernels for 0% -> 0%
where the time goes in v2:
time: 858 us; the launch traced here: 848 us
  waiting for transfers between devices  412 us (48%)
  local copies, waits for them, and re-layouts  194 us (23%)
  matrix products  193 us (22%)
  other arithmetic  32 us (4%)
  starting transfers between devices  16.8 us (2%)
    all_to_all x2, waiting for transfers between devices, to_k(): got = lax.all_to_all(xs, ('row', 'col'), 1, 1, tiled=True)  266 us
    all_to_all x1, waiting for transfers between devices, from_k(): got = lax.all_to_all(ys, ('row', 'col'), 1, 1, tiled=True)  146 us
    dot_general x4, matrix products, left_mul(): out = jnp.einsum('ab,bmn->amn', h_big, flat, precision=highest)  140 us
    transpose x2, local copies, waits for them, and re-layouts, to_k(): got.reshape(2, nrow, ncol, kb, nrows, ncols).transpose(0, 1, 4, 3, 2, 5)  31.2 us
    reshape x2, local copies, waits for them, and re-layouts, to_k(): return got.reshape(2, nrow * nrows, kb, ncol * ncols)  23.1 us
  transfers between devices with their start and end apart: 3, of which 3 were waited for; matrix products, arithmetic and copies ran while one was open for 16% of the time, Pallas kernels for 0%

profile of v2, /device:TPU:13, one launch (start us, length us, event | category | flops | bytes accessed | tf_op | source)
XLA Modules:
  0.0 848.1 jit_solution(17480973424403162283)
XLA Ops:
  0.0 8.2 copy.89
  15.0 19.3 %fusion.11 = f32[512,32,128]{2,0,1:T(8,128)S(1)} fusion(f32[512,32,128]{2,1,0:T(8,128)} %bitcast.122, f32[256,256]{1,0:T(8,128)S(1)} %get-tuple-element.22, f32[256,256]{1,0:T(8,128)S(1)} %get-tuple-element.21, f32[256,256]{1,0:T(8,128)S(1)} %fusion.50), kind=kOutput, calls=%fused_computation.18 | convolution fusion | flops 12885688320 | bytes 17563648 | tf_op jit(solution)/shard_map/ab,bmn->amn/dot_general | solution.py:68
  42.1 155.2 %all-to-all-done = f32[2,16,16,32,128]{4,3,2,0,1:T(8,128)} async-done(((f32[2,16,16,32,128]{4,3,2,0,1:T(8,128)}), f32[2,16,16,32,128]{4,3,2,0,1:T(8,128)}, u32[]{:S(2)}, u32[]{:S(2)}) %all-to-all-start) | async-done | bytes 8388640 | tf_op jit(solution)/shard_map/all_to_all | solution.py:87
  209.6 15.5 %copy.94 = f32[2,8,32,16,2,128]{5,4,2,1,3,0:T(2,128)} copy(f32[2,8,32,16,2,128]{5,2,3,0,4,1:T(8,128)} %bitcast.19) | data formatting | bytes 16777216 | tf_op jit(solution)/shard_map/transpose | solution.py:88
  225.0 15.8 %copy.91 = f32[2,8,32,16,2,128]{5,4,2,1,0,3:T(2,128)} copy(f32[2,8,32,16,2,128]{5,2,3,0,4,1:T(8,128)} %bitcast.19) | data formatting | bytes 16777216 | tf_op jit(solution)/shard_map/transpose | solution.py:88
  260.9 7.9 fusion.33
  273.9 110.8 %all-to-all-done.1 = f32[2,16,16,32,128]{4,2,0,3,1:T(8,128)} async-done(((f32[2,16,16,32,128]{4,2,0,3,1:T(8,128)}), f32[2,16,16,32,128]{4,2,0,3,1:T(8,128)}, u32[]{:S(2)}, u32[]{:S(2)}) %all-to-all-start.1) | async-done | bytes 8388640 | tf_op jit(solution)/shard_map/all_to_all | solution.py:87
  384.7 15.4 %copy.124 = f32[2,8,2,16,32,128]{5,2,4,1,3,0:T(2,128)} copy(f32[2,8,2,16,32,128]{5,3,0,4,2,1:T(8,128)} %bitcast.27) | data formatting | bytes 16777216 | tf_op jit(solution)/shard_map/reshape | solution.py:88
  400.1 11.6 %reshape.199 = f32[2,256,16,256]{3,1,2,0:T(8,128)} reshape(f32[2,8,32,16,2,128]{5,4,2,1,3,0:T(2,128)} %bitcast.131) | data formatting | bytes 16777216 | tf_op jit(solution)/shard_map/reshape | solution.py:89
  411.7 11.5 %reshape.197 = f32[2,256,16,256]{3,1,2,0:T(8,128)} reshape(f32[2,8,32,16,2,128]{5,4,2,1,3,0:T(2,128)} %copy.94) | data formatting | bytes 16777216 | tf_op jit(solution)/shard_map/reshape | solution.py:89
  423.2 11.6 %reshape.207 = f32[512,16,256,1]{2,0,1,3:T(8,128)} reshape(f32[2,8,32,16,2,128]{5,4,2,1,0,3:T(2,128)} %copy.91) | data formatting | bytes 16777216 | tf_op jit(solution)/shard_map/reshape;reshape | solution.py:67
  434.8 8.3 copy.93
  449.8 9.1 %subtract_bitcast_fusion.1 = f32[1,256,16,256]{3,1,2,0:T(8,128)} fusion(f32[256,16,256]{2,0,1:T(8,128)} %fusion.39, f32[256,16,256]{2,0,1:T(8,128)} %squeeze.31, f32[2,256,256]{2,1,0:T(8,128)S(1)} %copy-done.7), kind=kOutput, calls=%fused_computation.33 | convolution fusion | flops 3222274048 | bytes 12845056 | tf_op jit(solution)/shard_map/ikj,nj->ikn/dot_general | solution.py:74
  463.8 27.2 %fusion.24 = (f32[2,256,16,256]{3,1,2,0:T(8,128)}, f32[2,256,16,256]{3,1,2,0:T(8,128)}) fusion(f32[2,256,16,256]{3,1,2,0:T(8,128)} %reshape.199, f32[1,256,16,256]{3,1,2,0:T(8,128)} %get-tuple-element.26, f32[1,256,16,256]{3,1,2,0:T(8,128)} %get-tuple-element.25, f32[2,256,16,256]{3,1,2,0:T(8,128)} %reshape.197, f32[256,256]{1,0:T(8,128)S(1)} %compare_select_fusion, ...), kind=kOutput, calls=%fused_computation.45 | convolution fusion | flops 12901679104 | bytes 60030976 | tf_op jit(solution)/shard_map/ab,bmn->amn/dot_general | solution.py:68
  502.2 8.1 copy.97
  524.7 45.7 %maximum_subtract_fusion = f32[2,256,16,256]{3,1,2,0:T(8,128)} fusion(f32[1,256,16,256]{3,1,2,0:T(8,128)} %get-tuple-element.8, f32[1,256,16,256]{3,1,2,0:T(8,128)} %get-tuple-element.7, f32[1,256,16,256]{3,1,2,0:T(8,128)} %add_bitcast_fusion, f32[1,256,16,256]{3,1,2,0:T(8,128)} %subtract_bitcast_fusion, f32[256,256]{1,0:T(8,128)S(1)} %compare_select_fusion, ...), kind=kOutput, calls=%fused_computation.6 | convolution fusion | flops 12905873408 | bytes 60030976 | tf_op jit(solution)/shard_map/ab,bmn->amn/dot_general | solution.py:68
  570.5 10.8 %reshape.201 = f32[2,8,32,16,2,128]{5,4,2,1,3,0:T(2,128)} reshape(f32[2,256,16,256]{3,1,2,0:T(8,128)} %maximum_subtract_fusion) | data formatting | bytes 16777216 | tf_op jit(solution)/shard_map/reshape | solution.py:92
  581.3 11.4 %copy.99 = f32[2,8,2,16,32,128]{5,3,4,0,2,1:T(8,128)} copy(f32[2,8,2,16,32,128]{5,2,4,1,3,0:T(2,128)} %bitcast.132) | data formatting | bytes 16777216 | tf_op jit(solution)/shard_map/transpose | solution.py:92
  605.6 13.3 %add_add_fusion = (f32[2,256,32,128]{3,1,2,0:T(8,128)}, f32[2,256,32,128]{3,1,2,0:T(8,128)S(1)}) fusion(f32[2,256,32,128]{3,2,1,0:T(8,128)} %param.7, f32[2,256,32,128]{3,1,0,2:T(8,128)} %bitcast.124, f32[1,256,32,128]{3,1,2,0:T(8,128)} %get-tuple-element.24, f32[1,256,32,128]{3,1,2,0:T(8,128)} %get-tuple-element.23, f32[32,128]{1,0:T(8,128)S(1)} %compare_select_fusion.1), kind=kLoop, calls=%fused_computation.20 | loop fusion | flops 10485760 | bytes 41959424 | tf_op jit(solution)/shard_map/add | solution.py:108
  618.8 11.5 %copy.87 = f32[2,256,32,128]{3,2,1,0:T(8,128)} copy(f32[2,256,32,128]{3,1,2,0:T(8,128)} %get-tuple-element.5) | data formatting | bytes 16777216 | tf_op jit(solution)/shard_map/add | solution.py:108
  634.4 145.5 %all-to-all-done.2 = f32[2,16,16,32,128]{4,2,3,0,1:T(8,128)} async-done(((f32[2,16,16,32,128]{4,2,3,0,1:T(8,128)}), f32[2,16,16,32,128]{4,2,3,0,1:T(8,128)}, u32[]{:S(2)}, u32[]{:S(2)}) %all-to-all-start.2) | async-done | bytes 8388640 | tf_op jit(solution)/shard_map/all_to_all | solution.py:94
  779.9 8.2 copy.100
  788.1 48.1 %fusion.1 = f32[2,256,32,128]{3,1,2,0:T(8,128)} fusion(f32[1,256,32,128]{3,1,2,0:T(8,128)} %get-tuple-element.12, f32[1,256,32,128]{3,1,2,0:T(8,128)S(1)} %copy-done.6, f32[2,16,16,32,128]{4,2,1,3,0:T(8,128)} %copy.100, f32[2,256,32,128]{3,2,1,0:T(8,128)} %param.7, f32[2,256,512,1]{2,1,3,0:T(8,128)S(1)} %bitcast.135, f32[512,32,128]{2,1,0:T(8,128)} %bitcast.127), kind=kOutput, calls=%fused_computation.3 | convolution fusion | flops 12895387648 | bytes 42991616 | tf_op jit(solution)/shard_map/ab,bmn->amn/dot_general | solution.py:68
  836.2 11.6 %copy.101 = f32[2,256,32,128]{3,2,1,0:T(8,128)} copy(f32[2,256,32,128]{3,1,2,0:T(8,128)} %fusion.1) | data formatting | bytes 16777216 | tf_op jit(solution)/shard_map/add | solution.py:110
  (67 shorter events, 106.0 us)
Async XLA Ops:
  8.2 6.7 copy-start.7
  8.2 189.0 %all-to-all-start = ((f32[2,16,16,32,128]{4,3,2,0,1:T(8,128)}), f32[2,16,16,32,128]{4,3,2,0,1:T(8,128)}, u32[]{:S(2)}, u32[]{:S(2)}) async-start(f32[2,16,16,32,128]{4,3,2,0,1:T(8,128)} %copy.89), calls=%async_computation | async-start | bytes 16777216 | tf_op jit(solution)/shard_map/all_to_all | solution.py:87
  34.3 3.4 copy-start.1
  42.0 160.5 %copy-start.11 = (s32[256]{0:T(256)S(1)}, s32[256]{0:T(256)}, u32[]{:S(2)}) copy-start(s32[256]{0:T(256)} %param.10) | copy-start | bytes 3076
  42.0 160.5 %copy-start.12 = (f32[32]{0:T(128)S(1)}, f32[32]{0:T(128)}, u32[]{:S(2)}) copy-start(f32[32]{0:T(128)} %param.11) | copy-start | bytes 388
  42.1 160.6 %copy-start.8 = (f32[2,256,256]{2,1,0:T(8,128)S(1)}, f32[2,256,256]{2,1,0:T(8,128)}, u32[]{:S(2)}) copy-start(f32[2,256,256]{2,1,0:T(8,128)} %param.9) | copy-start | bytes 1572868
  42.1 160.9 %copy-start.9 = (s32[4096]{0:T(1024)S(1)}, s32[4096]{0:T(1024)}, u32[]{:S(2)}) copy-start(s32[4096]{0:T(1024)} %param.13) | copy-start | bytes 49156
  42.1 160.9 %copy-start.10 = (s32[4096]{0:T(1024)S(1)}, s32[4096]{0:T(1024)}, u32[]{:S(2)}) copy-start(s32[4096]{0:T(1024)} %param.12) | copy-start | bytes 49156
  197.3 187.5 %all-to-all-start.1 = ((f32[2,16,16,32,128]{4,2,0,3,1:T(8,128)}), f32[2,16,16,32,128]{4,2,0,3,1:T(8,128)}, u32[]{:S(2)}, u32[]{:S(2)}) async-start(f32[2,16,16,32,128]{4,2,0,3,1:T(8,128)} %copy.95), calls=%async_computation.1 | async-start | bytes 16777216 | tf_op jit(solution)/shard_map/all_to_all | solution.py:87
  260.9 7.9 copy-start.3
  449.7 9.1 %copy-start.2 = (f32[256,16,256]{2,0,1:T(8,128)S(1)}, f32[256,16,256]{2,0,1:T(8,128)}, u32[]{:S(2)}) copy-start(f32[256,16,256]{2,0,1:T(8,128)} %squeeze.31) | copy-start | bytes 12582916
  449.7 9.1 %copy-start.4 = (f32[256,16,256]{2,0,1:T(8,128)S(1)}, f32[256,16,256]{2,0,1:T(8,128)}, u32[]{:S(2)}) copy-start(f32[256,16,256]{2,0,1:T(8,128)} %fusion.33) | copy-start | bytes 12582916
  491.1 6.1 copy-start
  510.3 5.1 copy-start.5
  510.3 10.3 %slice-start = ((s8[8388608]{0:T(1024)(128)(4,1)}), s8[4194304]{0:T(1024)(128)(4,1)S(1)}, s32[]{:S(2)}) async-start(s8[8388608]{0:T(1024)(128)(4,1)} %bitcast.125), calls=%async_computation.3 | async-start | bytes 8388608
  515.5 5.2 slice-start.1
  592.7 187.2 %all-to-all-start.2 = ((f32[2,16,16,32,128]{4,2,3,0,1:T(8,128)}), f32[2,16,16,32,128]{4,2,3,0,1:T(8,128)}, u32[]{:S(2)}, u32[]{:S(2)}) async-start(f32[2,16,16,32,128]{4,2,3,0,1:T(8,128)} %bitcast.129), calls=%async_computation.2 | async-start | bytes 16777216 | tf_op jit(solution)/shard_map/all_to_all | solution.py:94
  779.9 8.2 copy-start.6

commit v3 on v2

--- a/solution.py
+++ b/solution.py
@@ -34,8 +34,6 @@
         h_big = jnp.concatenate(
             [jnp.concatenate([hre, -him], axis=1), jnp.concatenate([him, hre], axis=1)], axis=0
         )
-        hre_t = hre.T
-        him_t = him.T
 
         sites_i = lax.dynamic_slice_in_dim(site_map, row_start, nrows)
         sites_j = lax.dynamic_slice_in_dim(site_map, col_start, ncols)
@@ -54,13 +52,13 @@
         lad_k = u_all[:, None] * (site_map[:, None] == site_map[None, :]).astype(jnp.float32)
         pauli_k = u_all[:, None] * jnp.einsum("pi,pj->ij", first_hot, second_hot, precision=highest)
         gk = lax.dynamic_slice_in_dim(onebody, k_start, kb, 1)
-        gi_r = gk[0].T[:, :, None]
-        gi_i = gk[1].T[:, :, None]
-        gj_r = gk[0][None, :, :]
-        gj_i = gk[1][None, :, :]
-        pk = pauli_k[:, None, :]
+        gi_r = gk[0][:, :, None]
+        gi_i = gk[1][:, :, None]
+        gj_r = gk[0][:, None, :]
+        gj_i = gk[1][:, None, :]
+        pk = pauli_k[None, :, :]
         src_k = jnp.stack([pk * (gi_r * gj_r - gi_i * gj_i), pk * (gi_r * gj_i + gi_i * gj_r)])
-        lad_kb = lad_k[:, None, :]
+        lad_kb = lad_k[None, :, :]
 
         def left_mul(x):
             shp = x.shape
@@ -68,29 +66,38 @@
             out = jnp.einsum("ab,bmn->amn", h_big, flat, precision=highest)
             return out.reshape(shp)
 
-        def right_mul(x):
+        def apply_ij(x):
             xr = x[0]
             xi = x[1]
-            out_re = jnp.einsum("ikj,nj->ikn", xr, hre, precision=highest) - jnp.einsum(
-                "ikj,nj->ikn", xi, him, precision=highest
-            )
-            out_im = jnp.einsum("ikj,nj->ikn", xr, him, precision=highest) + jnp.einsum(
-                "ikj,nj->ikn", xi, hre, precision=highest
-            )
+
+            def li(hm, xm):
+                return jnp.einsum("ia,kaj->kij", hm, xm, precision=highest)
+
+            def lj(xm, hm):
+                return jnp.einsum("kia,ja->kij", xm, hm, precision=highest)
+
+            out_re = li(hre, xr) - li(him, xi) + lj(xr, hre) - lj(xi, him)
+            out_im = li(hre, xi) + li(him, xr) + lj(xi, hre) + lj(xr, him)
             return jnp.stack([out_re, out_im])
-
-        def apply_ij(x):
-            return left_mul(x) + right_mul(x)
 
         def to_k(x):
             xs = x.reshape(2, ndev, kb, nrows, ncols)
             got = lax.all_to_all(xs, ("row", "col"), 1, 1, tiled=True)
-            got = got.reshape(2, nrow, ncol, kb, nrows, ncols).transpose(0, 1, 4, 3, 2, 5)
-            return got.reshape(2, nrow * nrows, kb, ncol * ncols)
+            rows = [
+                jnp.concatenate([got[:, a * ncol + b] for b in range(ncol)], axis=-1)
+                for a in range(nrow)
+            ]
+            return jnp.concatenate(rows, axis=-2)
 
         def from_k(y):
-            ys = y.reshape(2, nrow, nrows, kb, ncol, ncols).transpose(0, 1, 4, 3, 2, 5)
-            ys = ys.reshape(2, ndev, kb, nrows, ncols)
+            ys = jnp.stack(
+                [
+                    y[:, :, a * nrows:(a + 1) * nrows, b * ncols:(b + 1) * ncols]
+                    for a in range(nrow)
+                    for b in range(ncol)
+                ],
+                axis=1,
+            )
             got = lax.all_to_all(ys, ("row", "col"), 1, 1, tiled=True)
             return got.reshape(2, orbs, nrows, ncols)
 

time: 858 us -> 808 us (0.942)
  local copies, waits for them, and re-layouts: 194 us -> 99.2 us
  other arithmetic: 32 us -> 77.6 us
  matrix products: 193 us -> 176 us
  waiting for transfers between devices: 412 us -> 429 us
    dot_general x4 -> x2, matrix products: 140 us -> 67.8 us  [left_mul(): out = jnp.einsum('ab,bmn->amn', h_big, flat, precision=highest)]
    dot_general x8 -> x16, matrix products: 48.5 us -> 104 us  [the longest x8 52.8 us: li(): return jnp.einsum('ia,kaj->kij', hm, xm, precision=highest)]
    reshape x4 -> x0, local copies, waits for them, and re-layouts: 49.2 us -> none  [the longest x2 23.1 us: to_k(): return got.reshape(2, nrow * nrows, kb, ncol * ncols)]
    transpose x4 -> x0, local copies, waits for them, and re-layouts: 42.7 us -> none  [the longest x2 31.2 us: to_k(): got.reshape(2, nrow, ncol, kb, nrows, ncols).transpose(0, 1, 4, 3, 2, 5)]
    unnamed x30 -> x67, local copies, waits for them, and re-layouts: 3.45 us -> 34.5 us
    add x0 -> x1, other arithmetic: none -> 19.3 us  [on_device(): w = e + p_k]
    sub x0 -> x1, other arithmetic: none -> 19.2 us  [on_device(): part_k = neg_i(q, dt) - dt2 * (apply_ij(w) + lad_kb * e)]
    slice x3 -> x0, local copies, waits for them, and re-layouts: 17.6 us -> none  [the longest x2 11.4 us: right_mul(): xi = x[1]]
  transfers between devices with their start and end apart: 3 -> 3, of which waited for: 3 -> 3; matrix products, arithmetic and copies ran while one was open for 16% -> 14% of each run, Pallas kernels for 0% -> 0%
where the time goes in v3:
time: 808 us; the launch traced here: 800 us
  waiting for transfers between devices  429 us (53%)
  matrix products  176 us (22%)
  local copies, waits for them, and re-layouts  99.2 us (12%)
  other arithmetic  77.6 us (10%)
  starting transfers between devices  16.6 us (2%)
    all_to_all x2, waiting for transfers between devices, to_k(): got = lax.all_to_all(xs, ('row', 'col'), 1, 1, tiled=True)  282 us
    all_to_all x1, waiting for transfers between devices, from_k(): got = lax.all_to_all(ys, ('row', 'col'), 1, 1, tiled=True)  148 us
    dot_general x2, matrix products, left_mul(): out = jnp.einsum('ab,bmn->amn', h_big, flat, precision=highest)  67.8 us
    dot_general x8, matrix products, li(): return jnp.einsum('ia,kaj->kij', hm, xm, precision=highest)  52.8 us
    dot_general x8, matrix products, lj(): return jnp.einsum('kia,ja->kij', xm, hm, precision=highest)  51.6 us
    unnamed x67, local copies, waits for them, and re-layouts  34.5 us
    add x1, other arithmetic, on_device(): w = e + p_k  19.3 us
    sub x1, other arithmetic, on_device(): part_k = neg_i(q, dt) - dt2 * (apply_ij(w) + lad_kb * e)  19.2 us
  transfers between devices with their start and end apart: 3, of which 3 were waited for; matrix products, arithmetic and copies ran while one was open for 14% of the time, Pallas kernels for 0%

profile of v3, /device:TPU:13, one launch (start us, length us, event | category | flops | bytes accessed | tf_op | source)
XLA Modules:
  0.0 799.5 jit_solution(3665114845267354506)
XLA Ops:
  0.0 8.2 %copy.40 = f32[2,16,16,32,128]{4,3,2,0,1:T(8,128)} copy(f32[2,16,16,32,128]{4,3,2,1,0:T(8,128)} %bitcast.265) | data formatting | bytes 16777216 | tf_op jit(solution)/shard_map/reshape | solution.py:84
  8.3 6.7 all-to-all-start
  15.0 19.6 %fusion.6 = f32[512,32,128]{2,0,1:T(8,128)S(1)} fusion(f32[512,32,128]{2,1,0:T(8,128)} %bitcast.266, f32[256,256]{1,0:T(8,128)S(1)} %get-tuple-element.52, f32[256,256]{1,0:T(8,128)S(1)} %get-tuple-element.51, f32[256,256]{1,0:T(8,128)S(1)} %fusion.93), kind=kOutput, calls=%fused_computation.12 | convolution fusion | flops 12885688320 | bytes 17563648 | tf_op jit(solution)/shard_map/ab,bmn->amn/dot_general | solution.py:66
  38.0 8.1 %copy.41 = f32[2,16,16,32,128]{4,3,2,0,1:T(8,128)} copy(f32[2,16,16,32,128]{4,2,1,0,3:T(8,128)S(1)} %bitcast.267) | data formatting | bytes 16777216 | tf_op jit(solution)/shard_map/reshape;reshape | solution.py:84
  46.1 151.2 %all-to-all-done = f32[2,16,16,32,128]{4,3,2,0,1:T(8,128)} async-done(((f32[2,16,16,32,128]{4,3,2,0,1:T(8,128)}), f32[2,16,16,32,128]{4,3,2,0,1:T(8,128)}, u32[]{:S(2)}, u32[]{:S(2)}) %all-to-all-start) | async-done | bytes 8388640 | tf_op jit(solution)/shard_map/all_to_all | solution.py:85
  220.0 5.4 fusion.19
  230.4 13.3 %fusion.16 = f32[16,256,256]{2,1,0:T(8,128)} fusion(f32[2,16,256,256]{3,2,1,0:T(8,128)S(1)} %maximum_dynamic-update-slice_fusion, f32[2,256,256]{2,1,0:T(8,128)S(1)} %copy-done.4), kind=kOutput, calls=%fused_computation.42 | convolution fusion | flops 3221225472 | bytes 8650752 | tf_op jit(solution)/shard_map/kia,ja->kij/dot_general | solution.py:77
  254.2 130.4 %all-to-all-done.1 = f32[2,16,16,32,128]{4,3,2,0,1:T(8,128)} async-done(((f32[2,16,16,32,128]{4,3,2,0,1:T(8,128)}), f32[2,16,16,32,128]{4,3,2,0,1:T(8,128)}, u32[]{:S(2)}, u32[]{:S(2)}) %all-to-all-start.1) | async-done | bytes 8388640 | tf_op jit(solution)/shard_map/all_to_all | solution.py:85
  384.5 5.8 slice_bitcast_fusion.45
  392.1 8.9 %fusion.15 = f32[1,16,256,256]{3,2,1,0:T(8,128)} fusion(f32[16,256,256]{2,1,0:T(8,128)} %fusion.22, f32[16,256,256]{2,1,0:T(8,128)} %fusion.18, f32[16,256,256]{1,2,0:T(8,128)} %fusion.19, f32[2,16,256,256]{3,2,1,0:T(8,128)S(1)} %copy-done.1, f32[2,256,256]{2,1,0:T(8,128)S(1)} %copy-done.4), kind=kOutput, calls=%fused_computation.35 | convolution fusion | flops 3224371200 | bytes 21233664 | tf_op jit(solution)/shard_map/ia,kaj->kij/dot_general | solution.py:74
  402.0 6.6 fusion.13
  416.5 19.3 %fusion.37 = (f32[2,16,256,256]{3,2,1,0:T(8,128)}, f32[2,16,256,256]{3,2,1,0:T(8,128)}) fusion(f32[2,16,256,256]{3,2,1,0:T(8,128)} %maximum_dynamic-update-slice_fusion.8, f32[1,16,256,256]{3,2,1,0:T(8,128)} %get-tuple-element.56, f32[1,16,256,256]{3,2,1,0:T(8,128)} %get-tuple-element.55, f32[2,16,256,256]{3,2,1,0:T(8,128)} %copy-done, ...), kind=kLoop, calls=%fused_computation.61 | loop fusion | flops 14680064 | bytes 50593792 | tf_op jit(solution)/shard_map/add | solution.py:112
  435.8 7.8 fusion.26
  443.6 5.4 fusion.27
  459.1 5.8 fusion.25
  474.1 8.9 %fusion.11 = f32[1,16,256,256]{3,2,1,0:T(8,128)} fusion(f32[16,256,256]{2,1,0:T(8,128)} %fusion.30, f32[16,256,256]{2,1,0:T(8,128)} %fusion.26, f32[16,256,256]{1,2,0:T(8,128)} %fusion.27, f32[2,16,256,256]{3,2,1,0:T(8,128)S(1)} %copy-done.2, f32[2,256,256]{2,1,0:T(8,128)S(1)} %copy-done.4), kind=kOutput, calls=%fused_computation.29 | convolution fusion | flops 3224371200 | bytes 21233664 | tf_op jit(solution)/shard_map/ia,kaj->kij/dot_general | solution.py:74
  483.9 6.5 fusion.9
  490.4 19.2 %maximum_subtract_fusion = f32[2,16,256,256]{3,2,1,0:T(8,128)} fusion(f32[1,16,256,256]{3,2,1,0:T(8,128)} %get-tuple-element.10, f32[1,16,256,256]{3,2,1,0:T(8,128)} %get-tuple-element.9, f32[1,16,256,256]{3,2,1,0:T(8,128)} %fusion.9, f32[1,16,256,256]{3,2,1,0:T(8,128)} %fusion.11, f32[256,256]{1,0:T(8,128)S(1)} %compare_select_fusion, ...), kind=kLoop, calls=%fused_computation.5 | loop fusion | flops 18874368 | bytes 50593792 | tf_op jit(solution)/shard_map/sub | solution.py:113
  552.4 11.5 %add_add_fusion = (f32[2,256,32,128]{3,1,2,0:T(8,128)}, f32[2,256,32,128]{3,1,2,0:T(8,128)S(1)}) fusion(f32[2,256,32,128]{3,2,1,0:T(8,128)} %param.7, f32[2,256,32,128]{3,1,0,2:T(8,128)} %bitcast.268, f32[1,256,32,128]{3,1,2,0:T(8,128)} %get-tuple-element.54, f32[1,256,32,128]{3,1,2,0:T(8,128)S(1)} %get-tuple-element.53, f32[32,128]{1,0:T(8,128)S(1)} %compare_select_fusion.1), kind=kLoop, calls=%fused_computation.14 | loop fusion | flops 10485760 | bytes 41959424 | tf_op jit(solution)/shard_map/add | solution.py:115
  563.9 11.5 %copy.38 = f32[2,256,32,128]{3,2,1,0:T(8,128)} copy(f32[2,256,32,128]{3,1,2,0:T(8,128)} %get-tuple-element.7) | data formatting | bytes 16777216 | tf_op jit(solution)/shard_map/add | solution.py:115
  579.6 147.9 %all-to-all-done.2 = f32[2,16,16,32,128]{4,3,2,0,1:T(8,128)} async-done(((f32[2,16,16,32,128]{4,3,2,0,1:T(8,128)}), f32[2,16,16,32,128]{4,3,2,0,1:T(8,128)}, u32[]{:S(2)}, u32[]{:S(2)}) %all-to-all-start.2) | async-done | bytes 8388640 | tf_op jit(solution)/shard_map/all_to_all | solution.py:101
  727.5 11.8 %copy.42 = f32[2,16,16,32,128]{4,2,1,3,0:T(8,128)} copy(f32[2,16,16,32,128]{4,3,2,0,1:T(8,128)} %all-to-all-done.2) | data formatting | bytes 16777216 | tf_op jit(solution)/shard_map/all_to_all | solution.py:101
  739.2 48.2 %fusion.1 = f32[2,256,32,128]{3,1,2,0:T(8,128)} fusion(f32[1,256,32,128]{3,1,2,0:T(8,128)} %get-tuple-element.44, f32[1,256,32,128]{3,1,2,0:T(8,128)S(1)} %copy-done.5, f32[2,16,16,32,128]{4,2,1,3,0:T(8,128)} %copy.42, f32[2,256,32,128]{3,2,1,0:T(8,128)} %param.7, f32[2,256,512,1]{2,1,3,0:T(8,128)S(1)} %bitcast.272, f32[512,32,128]{2,1,0:T(8,128)} %bitcast.271), kind=kOutput, calls=%fused_computation.3 | convolution fusion | flops 12895387648 | bytes 42991616 | tf_op jit(solution)/shard_map/ab,bmn->amn/dot_general | solution.py:66
  787.4 11.6 %copy.43 = f32[2,256,32,128]{3,2,1,0:T(8,128)} copy(f32[2,256,32,128]{3,1,2,0:T(8,128)} %fusion.1) | data formatting | bytes 16777216 | tf_op jit(solution)/shard_map/add | solution.py:117
  (116 shorter events, 119.2 us)
Async XLA Ops:
  8.3 189.0 %all-to-all-start = ((f32[2,16,16,32,128]{4,3,2,0,1:T(8,128)}), f32[2,16,16,32,128]{4,3,2,0,1:T(8,128)}, u32[]{:S(2)}, u32[]{:S(2)}) async-start(f32[2,16,16,32,128]{4,3,2,0,1:T(8,128)} %copy.40), calls=%async_computation | async-start | bytes 16777216 | tf_op jit(solution)/shard_map/all_to_all | solution.py:85
  46.1 156.8 %copy-start.22 = (s32[256]{0:T(256)S(1)}, s32[256]{0:T(256)}, u32[]{:S(2)}) copy-start(s32[256]{0:T(256)} %param.10) | copy-start | bytes 3076
  46.1 156.8 %copy-start.23 = (f32[32]{0:T(128)S(1)}, f32[32]{0:T(128)}, u32[]{:S(2)}) copy-start(f32[32]{0:T(128)} %param.11) | copy-start | bytes 388
  46.1 157.1 %copy-start.20 = (s32[4096]{0:T(1024)S(1)}, s32[4096]{0:T(1024)}, u32[]{:S(2)}) copy-start(s32[4096]{0:T(1024)} %param.13) | copy-start | bytes 49156
  46.1 157.1 %copy-start.21 = (s32[4096]{0:T(1024)S(1)}, s32[4096]{0:T(1024)}, u32[]{:S(2)}) copy-start(s32[4096]{0:T(1024)} %param.12) | copy-start | bytes 49156
  197.3 187.3 %all-to-all-start.1 = ((f32[2,16,16,32,128]{4,3,2,0,1:T(8,128)}), f32[2,16,16,32,128]{4,3,2,0,1:T(8,128)}, u32[]{:S(2)}, u32[]{:S(2)}) async-start(f32[2,16,16,32,128]{4,3,2,0,1:T(8,128)} %copy.41), calls=%async_computation.1 | async-start | bytes 16777216 | tf_op jit(solution)/shard_map/all_to_all | solution.py:85
  214.9 34.3 %copy-start = (f32[2,16,256,256]{3,2,1,0:T(8,128)}, f32[2,16,256,256]{3,2,1,0:T(8,128)S(1)}, u32[]{:S(2)}) copy-start(f32[2,16,256,256]{3,2,1,0:T(8,128)S(1)} %maximum_dynamic-update-slice_fusion) | copy-start | bytes 25165828
  384.5 7.6 copy-start.1
  392.1 8.9 %copy-start.6 = (f32[16,256,256]{2,1,0:T(8,128)S(1)}, f32[16,256,256]{2,1,0:T(8,128)}, u32[]{:S(2)}) copy-start(f32[16,256,256]{2,1,0:T(8,128)} %fusion.16) | copy-start | bytes 12582916
  392.1 8.9 %copy-start.7 = (f32[16,256,256]{1,2,0:T(8,128)S(1)}, f32[16,256,256]{1,2,0:T(8,128)}, u32[]{:S(2)}) copy-start(f32[16,256,256]{1,2,0:T(8,128)} %fusion.17) | copy-start | bytes 12582916
  392.1 9.8 %copy-start.8 = (f32[16,256,256]{2,1,0:T(8,128)S(1)}, f32[16,256,256]{2,1,0:T(8,128)}, u32[]{:S(2)}) copy-start(f32[16,256,256]{2,1,0:T(8,128)} %fusion.20) | copy-start | bytes 12582916
  401.9 6.7 copy-start.18
  401.9 7.8 copy-start.15
  401.9 7.8 copy-start.16
  401.9 8.9 %copy-start.13 = (f32[2,16,32,128]{3,2,1,0:T(8,128)S(1)}, f32[2,16,32,128]{3,2,1,0:T(8,128)}, u32[]{:S(2)}) copy-start(f32[2,16,32,128]{3,2,1,0:T(8,128)} %get-tuple-element.35) | copy-start | bytes 1572868
  401.9 8.9 %copy-start.14 = (f32[2,16,32,128]{3,2,1,0:T(8,128)S(1)}, f32[2,16,32,128]{3,2,1,0:T(8,128)}, u32[]{:S(2)}) copy-start(f32[2,16,32,128]{3,2,1,0:T(8,128)} %get-tuple-element.36) | copy-start | bytes 1572868
  402.0 10.0 %copy-start.12 = (f32[2,16,32,128]{3,2,1,0:T(8,128)S(1)}, f32[2,16,32,128]{3,2,1,0:T(8,128)}, u32[]{:S(2)}) copy-start(f32[2,16,32,128]{3,2,1,0:T(8,128)} %get-tuple-element.34) | copy-start | bytes 1572868
  435.8 7.8 copy-start.2
  459.1 11.0 %slice-start = ((s8[8388608]{0:T(1024)(128)(4,1)}), s8[4194304]{0:T(1024)(128)(4,1)S(1)}, s32[]{:S(2)}) async-start(s8[8388608]{0:T(1024)(128)(4,1)} %bitcast.269), calls=%async_computation.3 | async-start | bytes 8388608
  474.1 8.9 %copy-start.9 = (f32[16,256,256]{2,1,0:T(8,128)S(1)}, f32[16,256,256]{2,1,0:T(8,128)}, u32[]{:S(2)}) copy-start(f32[16,256,256]{2,1,0:T(8,128)} %fusion.24) | copy-start | bytes 12582916
  474.1 8.9 %copy-start.10 = (f32[16,256,256]{1,2,0:T(8,128)S(1)}, f32[16,256,256]{1,2,0:T(8,128)}, u32[]{:S(2)}) copy-start(f32[16,256,256]{1,2,0:T(8,128)} %fusion.25) | copy-start | bytes 12582916
  474.1 9.8 %copy-start.11 = (f32[16,256,256]{2,1,0:T(8,128)S(1)}, f32[16,256,256]{2,1,0:T(8,128)}, u32[]{:S(2)}) copy-start(f32[16,256,256]{2,1,0:T(8,128)} %fusion.28) | copy-start | bytes 12582916
  540.1 187.4 %all-to-all-start.2 = ((f32[2,16,16,32,128]{4,3,2,0,1:T(8,128)}), f32[2,16,16,32,128]{4,3,2,0,1:T(8,128)}, u32[]{:S(2)}, u32[]{:S(2)}) async-start(f32[2,16,16,32,128]{4,3,2,0,1:T(8,128)} %fusion.44), calls=%async_computation.2 | async-start | bytes 16777216 | tf_op jit(solution)/shard_map/all_to_all | solution.py:101
  727.5 11.8 %copy-start.5 = (f32[1,256,32,128]{3,1,2,0:T(8,128)S(1)}, f32[1,256,32,128]{3,1,2,0:T(8,128)}, u32[]{:S(2)}) copy-start(f32[1,256,32,128]{3,1,2,0:T(8,128)} %get-tuple-element.43) | copy-start | bytes 12582916
  (5 other events, 27.1 us)

commit v4 on v3

--- a/solution.py
+++ b/solution.py
@@ -4,7 +4,7 @@
 from jax.sharding import PartitionSpec as P
 
 time_step = 0.1
-highest = lax.Precision.HIGHEST
+matmul_precision = lax.Precision.HIGH
 
 
 def neg_i(x, scale):
@@ -41,7 +41,7 @@
         lad_a = u_i[:, None] * (sites_i[:, None] == sites_j[None, :]).astype(jnp.float32)
         fh_a = lax.dynamic_slice_in_dim(first_hot, row_start, nrows, 1)
         sh_a = lax.dynamic_slice_in_dim(second_hot, col_start, ncols, 1)
-        pauli_a = u_i[:, None] * jnp.einsum("pi,pj->ij", fh_a, sh_a, precision=highest)
+        pauli_a = u_i[:, None] * jnp.einsum("pi,pj->ij", fh_a, sh_a, precision=matmul_precision)
         left = lax.dynamic_slice_in_dim(onebody, row_start, nrows, 2)
         right = lax.dynamic_slice_in_dim(onebody, col_start, ncols, 2)
         src_a = jnp.stack([
@@ -50,7 +50,7 @@
         ])
 
         lad_k = u_all[:, None] * (site_map[:, None] == site_map[None, :]).astype(jnp.float32)
-        pauli_k = u_all[:, None] * jnp.einsum("pi,pj->ij", first_hot, second_hot, precision=highest)
+        pauli_k = u_all[:, None] * jnp.einsum("pi,pj->ij", first_hot, second_hot, precision=matmul_precision)
         gk = lax.dynamic_slice_in_dim(onebody, k_start, kb, 1)
         gi_r = gk[0][:, :, None]
         gi_i = gk[1][:, :, None]
@@ -63,7 +63,7 @@
         def left_mul(x):
             shp = x.shape
             flat = x.reshape(2 * shp[1], shp[2], shp[3])
-            out = jnp.einsum("ab,bmn->amn", h_big, flat, precision=highest)
+            out = jnp.einsum("ab,bmn->amn", h_big, flat, precision=matmul_precision)
             return out.reshape(shp)
 
         def apply_ij(x):
@@ -71,10 +71,10 @@
             xi = x[1]
 
             def li(hm, xm):
-                return jnp.einsum("ia,kaj->kij", hm, xm, precision=highest)
+                return jnp.einsum("ia,kaj->kij", hm, xm, precision=matmul_precision)
 
             def lj(xm, hm):
-                return jnp.einsum("kia,ja->kij", xm, hm, precision=highest)
+                return jnp.einsum("kia,ja->kij", xm, hm, precision=matmul_precision)
 
             out_re = li(hre, xr) - li(him, xi) + lj(xr, hre) - lj(xi, him)
             out_im = li(hre, xi) + li(him, xr) + lj(xi, hre) + lj(xr, him)

time: 808 us -> 781 us (0.967)
  matrix products: 176 us -> 126 us
  waiting for transfers between devices: 429 us -> 452 us
    dot_general x20, matrix products: 176 us -> 126 us  [the longest x8 45.7 us: li(): return jnp.einsum('ia,kaj->kij', hm, xm, precision=matmul_precision)]
    all_to_all x2, waiting for transfers between devices: 282 us -> 304 us  [to_k(): got = lax.all_to_all(xs, ('row', 'col'), 1, 1, tiled=True)]
  transfers between devices with their start and end apart: 3 -> 3, of which waited for: 3 -> 3; matrix products, arithmetic and copies ran while one was open for 14% -> 12% of each run, Pallas kernels for 0% -> 0%
where the time goes in v4:
time: 781 us; the launch traced here: 771 us
  waiting for transfers between devices  452 us (58%)
  matrix products  126 us (16%)
  local copies, waits for them, and re-layouts  97.3 us (12%)
  other arithmetic  78.2 us (10%)
  starting transfers between devices  17.1 us (2%)
    all_to_all x2, waiting for transfers between devices, to_k(): got = lax.all_to_all(xs, ('row', 'col'), 1, 1, tiled=True)  304 us
    all_to_all x1, waiting for transfers between devices, from_k(): got = lax.all_to_all(ys, ('row', 'col'), 1, 1, tiled=True)  148 us
    dot_general x8, matrix products, li(): return jnp.einsum('ia,kaj->kij', hm, xm, precision=matmul_precision)  45.7 us
    dot_general x2, matrix products, left_mul(): out = jnp.einsum('ab,bmn->amn', h_big, flat, precision=matmul_precision)  42.6 us
    dot_general x8, matrix products, lj(): return jnp.einsum('kia,ja->kij', xm, hm, precision=matmul_precision)  33.8 us
    unnamed x67, local copies, waits for them, and re-layouts  32.6 us
    add x1, other arithmetic, on_device(): w = e + p_k  19.5 us
    sub x1, other arithmetic, on_device(): part_k = neg_i(q, dt) - dt2 * (apply_ij(w) + lad_kb * e)  19.1 us
  transfers between devices with their start and end apart: 3, of which 3 were waited for; matrix products, arithmetic and copies ran while one was open for 12% of the time, Pallas kernels for 0%

profile of v4, /device:TPU:13, one launch (start us, length us, event | category | flops | bytes accessed | tf_op | source)
XLA Modules:
  0.0 770.9 jit_solution(14287119669461876279)
XLA Ops:
  0.0 8.2 %copy.40 = f32[2,16,16,32,128]{4,3,2,0,1:T(8,128)} copy(f32[2,16,16,32,128]{4,3,2,1,0:T(8,128)} %bitcast.265) | data formatting | bytes 16777216 | tf_op jit(solution)/shard_map/reshape | solution.py:84
  8.3 6.7 all-to-all-start
  15.0 12.3 %fusion.6 = f32[512,32,128]{2,0,1:T(8,128)S(1)} fusion(f32[512,32,128]{2,1,0:T(8,128)} %bitcast.266, f32[256,256]{1,0:T(8,128)S(1)} %get-tuple-element.52, f32[256,256]{1,0:T(8,128)S(1)} %get-tuple-element.51, f32[256,256]{1,0:T(8,128)S(1)} %fusion.93), kind=kOutput, calls=%fused_computation.12 | convolution fusion | flops 6443237376 | bytes 17563648 | tf_op jit(solution)/shard_map/ab,bmn->amn/dot_general | solution.py:66
  30.8 8.1 %copy.41 = f32[2,16,16,32,128]{4,3,2,0,1:T(8,128)} copy(f32[2,16,16,32,128]{4,2,1,0,3:T(8,128)S(1)} %bitcast.267) | data formatting | bytes 16777216 | tf_op jit(solution)/shard_map/reshape;reshape | solution.py:84
  38.9 158.4 %all-to-all-done = f32[2,16,16,32,128]{4,3,2,0,1:T(8,128)} async-done(((f32[2,16,16,32,128]{4,3,2,0,1:T(8,128)}), f32[2,16,16,32,128]{4,3,2,0,1:T(8,128)}, u32[]{:S(2)}, u32[]{:S(2)}) %all-to-all-start) | async-done | bytes 8388640 | tf_op jit(solution)/shard_map/all_to_all | solution.py:85
  197.3 5.4 all-to-all-start.1
  210.4 4.4 slice_bitcast_fusion.61
  239.3 145.6 %all-to-all-done.1 = f32[2,16,16,32,128]{4,3,2,0,1:T(8,128)} async-done(((f32[2,16,16,32,128]{4,3,2,0,1:T(8,128)}), f32[2,16,16,32,128]{4,3,2,0,1:T(8,128)}, u32[]{:S(2)}, u32[]{:S(2)}) %all-to-all-start.1) | async-done | bytes 8388640 | tf_op jit(solution)/shard_map/all_to_all | solution.py:85
  384.9 5.8 slice_bitcast_fusion.45
  392.5 9.6 %fusion.15 = f32[1,16,256,256]{3,2,1,0:T(8,128)} fusion(f32[16,256,256]{2,1,0:T(8,128)} %fusion.22, f32[16,256,256]{2,1,0:T(8,128)} %fusion.18, f32[16,256,256]{1,2,0:T(8,128)} %fusion.19, f32[2,16,256,256]{3,2,1,0:T(8,128)S(1)} %copy-done.1, f32[2,256,256]{2,1,0:T(8,128)S(1)} %copy-done.4), kind=kOutput, calls=%fused_computation.35 | convolution fusion | flops 1613758464 | bytes 21233664 | tf_op jit(solution)/shard_map/ia,kaj->kij/dot_general | solution.py:74
  402.1 5.3 fusion.13
  415.2 19.5 %fusion.37 = (f32[2,16,256,256]{3,2,1,0:T(8,128)}, f32[2,16,256,256]{3,2,1,0:T(8,128)}) fusion(f32[2,16,256,256]{3,2,1,0:T(8,128)} %maximum_dynamic-update-slice_fusion.8, f32[1,16,256,256]{3,2,1,0:T(8,128)} %get-tuple-element.56, f32[1,16,256,256]{3,2,1,0:T(8,128)} %get-tuple-element.55, f32[2,16,256,256]{3,2,1,0:T(8,128)} %copy-done, ...), kind=kLoop, calls=%fused_computation.61 | loop fusion | flops 14680064 | bytes 50593792 | tf_op jit(solution)/shard_map/add | solution.py:112
  434.7 6.2 fusion.26
  460.6 4.5 slice_multiply_fusion.1
  465.0 9.6 %fusion.11 = f32[1,16,256,256]{3,2,1,0:T(8,128)} fusion(f32[16,256,256]{2,1,0:T(8,128)} %fusion.30, f32[16,256,256]{2,1,0:T(8,128)} %fusion.26, f32[16,256,256]{1,2,0:T(8,128)} %fusion.27, f32[2,16,256,256]{3,2,1,0:T(8,128)S(1)} %copy-done.2, f32[2,256,256]{2,1,0:T(8,128)S(1)} %copy-done.4), kind=kOutput, calls=%fused_computation.29 | convolution fusion | flops 1613758464 | bytes 21233664 | tf_op jit(solution)/shard_map/ia,kaj->kij/dot_general | solution.py:74
  474.6 5.3 fusion.9
  479.9 19.1 %maximum_subtract_fusion = f32[2,16,256,256]{3,2,1,0:T(8,128)} fusion(f32[1,16,256,256]{3,2,1,0:T(8,128)} %get-tuple-element.10, f32[1,16,256,256]{3,2,1,0:T(8,128)} %get-tuple-element.9, f32[1,16,256,256]{3,2,1,0:T(8,128)} %fusion.9, f32[1,16,256,256]{3,2,1,0:T(8,128)} %fusion.11, f32[256,256]{1,0:T(8,128)S(1)} %compare_select_fusion, ...), kind=kLoop, calls=%fused_computation.5 | loop fusion | flops 18874368 | bytes 50593792 | tf_op jit(solution)/shard_map/sub | solution.py:113
  529.4 5.0 all-to-all-start.2
  541.7 11.7 %add_add_fusion = (f32[2,256,32,128]{3,1,2,0:T(8,128)}, f32[2,256,32,128]{3,1,2,0:T(8,128)S(1)}) fusion(f32[2,256,32,128]{3,2,1,0:T(8,128)} %param.7, f32[2,256,32,128]{3,1,0,2:T(8,128)} %bitcast.268, f32[1,256,32,128]{3,1,2,0:T(8,128)} %get-tuple-element.54, f32[1,256,32,128]{3,1,2,0:T(8,128)S(1)} %get-tuple-element.53, f32[32,128]{1,0:T(8,128)S(1)} %compare_select_fusion.1), kind=kLoop, calls=%fused_computation.14 | loop fusion | flops 10485760 | bytes 41959424 | tf_op jit(solution)/shard_map/add | solution.py:115
  553.3 11.5 %copy.38 = f32[2,256,32,128]{3,2,1,0:T(8,128)} copy(f32[2,256,32,128]{3,1,2,0:T(8,128)} %get-tuple-element.7) | data formatting | bytes 16777216 | tf_op jit(solution)/shard_map/add | solution.py:115
  569.1 147.7 %all-to-all-done.2 = f32[2,16,16,32,128]{4,3,2,0,1:T(8,128)} async-done(((f32[2,16,16,32,128]{4,3,2,0,1:T(8,128)}), f32[2,16,16,32,128]{4,3,2,0,1:T(8,128)}, u32[]{:S(2)}, u32[]{:S(2)}) %all-to-all-start.2) | async-done | bytes 8388640 | tf_op jit(solution)/shard_map/all_to_all | solution.py:101
  716.8 11.8 %copy.42 = f32[2,16,16,32,128]{4,2,1,3,0:T(8,128)} copy(f32[2,16,16,32,128]{4,3,2,0,1:T(8,128)} %all-to-all-done.2) | data formatting | bytes 16777216 | tf_op jit(solution)/shard_map/all_to_all | solution.py:101
  728.6 30.2 %fusion.1 = f32[2,256,32,128]{3,1,2,0:T(8,128)} fusion(f32[1,256,32,128]{3,1,2,0:T(8,128)} %get-tuple-element.44, f32[1,256,32,128]{3,1,2,0:T(8,128)S(1)} %copy-done.5, f32[2,16,16,32,128]{4,2,1,3,0:T(8,128)} %copy.42, f32[2,256,32,128]{3,2,1,0:T(8,128)} %param.7, f32[2,256,512,1]{2,1,3,0:T(8,128)S(1)} %bitcast.272, f32[512,32,128]{2,1,0:T(8,128)} %bitcast.271), kind=kOutput, calls=%fused_computation.3 | convolution fusion | flops 6452936704 | bytes 42991616 | tf_op jit(solution)/shard_map/ab,bmn->amn/dot_general | solution.py:66
  758.8 11.6 %copy.43 = f32[2,256,32,128]{3,2,1,0:T(8,128)} copy(f32[2,256,32,128]{3,1,2,0:T(8,128)} %fusion.1) | data formatting | bytes 16777216 | tf_op jit(solution)/shard_map/add | solution.py:117
  (116 shorter events, 106.7 us)
Async XLA Ops:
  8.2 6.7 copy-start.4
  8.3 189.0 %all-to-all-start = ((f32[2,16,16,32,128]{4,3,2,0,1:T(8,128)}), f32[2,16,16,32,128]{4,3,2,0,1:T(8,128)}, u32[]{:S(2)}, u32[]{:S(2)}) async-start(f32[2,16,16,32,128]{4,3,2,0,1:T(8,128)} %copy.40), calls=%async_computation | async-start | bytes 16777216 | tf_op jit(solution)/shard_map/all_to_all | solution.py:85
  38.9 164.6 %copy-start.22 = (s32[256]{0:T(256)S(1)}, s32[256]{0:T(256)}, u32[]{:S(2)}) copy-start(s32[256]{0:T(256)} %param.10) | copy-start | bytes 3076
  38.9 164.6 %copy-start.23 = (f32[32]{0:T(128)S(1)}, f32[32]{0:T(128)}, u32[]{:S(2)}) copy-start(f32[32]{0:T(128)} %param.11) | copy-start | bytes 388
  38.9 164.8 %copy-start.20 = (s32[4096]{0:T(1024)S(1)}, s32[4096]{0:T(1024)}, u32[]{:S(2)}) copy-start(s32[4096]{0:T(1024)} %param.13) | copy-start | bytes 49156
  38.9 164.8 %copy-start.21 = (s32[4096]{0:T(1024)S(1)}, s32[4096]{0:T(1024)}, u32[]{:S(2)}) copy-start(s32[4096]{0:T(1024)} %param.12) | copy-start | bytes 49156
  197.3 187.6 %all-to-all-start.1 = ((f32[2,16,16,32,128]{4,3,2,0,1:T(8,128)}), f32[2,16,16,32,128]{4,3,2,0,1:T(8,128)}, u32[]{:S(2)}, u32[]{:S(2)}) async-start(f32[2,16,16,32,128]{4,3,2,0,1:T(8,128)} %copy.41), calls=%async_computation.1 | async-start | bytes 16777216 | tf_op jit(solution)/shard_map/all_to_all | solution.py:85
  215.4 19.9 %copy-start = (f32[2,16,256,256]{3,2,1,0:T(8,128)}, f32[2,16,256,256]{3,2,1,0:T(8,128)S(1)}, u32[]{:S(2)}) copy-start(f32[2,16,256,256]{3,2,1,0:T(8,128)S(1)} %maximum_dynamic-update-slice_fusion) | copy-start | bytes 25165828
  384.9 7.6 copy-start.1
  392.4 9.6 %copy-start.6 = (f32[16,256,256]{2,1,0:T(8,128)S(1)}, f32[16,256,256]{2,1,0:T(8,128)}, u32[]{:S(2)}) copy-start(f32[16,256,256]{2,1,0:T(8,128)} %fusion.16) | copy-start | bytes 12582916
  392.5 9.6 %copy-start.7 = (f32[16,256,256]{1,2,0:T(8,128)S(1)}, f32[16,256,256]{1,2,0:T(8,128)}, u32[]{:S(2)}) copy-start(f32[16,256,256]{1,2,0:T(8,128)} %fusion.17) | copy-start | bytes 12582916
  392.5 9.6 %copy-start.8 = (f32[16,256,256]{2,1,0:T(8,128)S(1)}, f32[16,256,256]{2,1,0:T(8,128)}, u32[]{:S(2)}) copy-start(f32[16,256,256]{2,1,0:T(8,128)} %fusion.20) | copy-start | bytes 12582916
  402.1 6.4 copy-start.15
  402.1 6.4 copy-start.16
  402.1 7.5 copy-start.13
  402.1 7.5 copy-start.14
  402.1 8.6 %copy-start.12 = (f32[2,16,32,128]{3,2,1,0:T(8,128)S(1)}, f32[2,16,32,128]{3,2,1,0:T(8,128)}, u32[]{:S(2)}) copy-start(f32[2,16,32,128]{3,2,1,0:T(8,128)} %get-tuple-element.34) | copy-start | bytes 1572868
  434.7 6.2 copy-start.2
  452.6 7.9 %slice-start = ((s8[8388608]{0:T(1024)(128)(4,1)}), s8[4194304]{0:T(1024)(128)(4,1)S(1)}, s32[]{:S(2)}) async-start(s8[8388608]{0:T(1024)(128)(4,1)} %bitcast.269), calls=%async_computation.3 | async-start | bytes 8388608
  465.0 9.6 %copy-start.9 = (f32[16,256,256]{2,1,0:T(8,128)S(1)}, f32[16,256,256]{2,1,0:T(8,128)}, u32[]{:S(2)}) copy-start(f32[16,256,256]{2,1,0:T(8,128)} %fusion.24) | copy-start | bytes 12582916
  465.0 9.6 %copy-start.10 = (f32[16,256,256]{1,2,0:T(8,128)S(1)}, f32[16,256,256]{1,2,0:T(8,128)}, u32[]{:S(2)}) copy-start(f32[16,256,256]{1,2,0:T(8,128)} %fusion.25) | copy-start | bytes 12582916
  465.0 9.6 %copy-start.11 = (f32[16,256,256]{2,1,0:T(8,128)S(1)}, f32[16,256,256]{2,1,0:T(8,128)}, u32[]{:S(2)}) copy-start(f32[16,256,256]{2,1,0:T(8,128)} %fusion.28) | copy-start | bytes 12582916
  529.4 187.4 %all-to-all-start.2 = ((f32[2,16,16,32,128]{4,3,2,0,1:T(8,128)}), f32[2,16,16,32,128]{4,3,2,0,1:T(8,128)}, u32[]{:S(2)}, u32[]{:S(2)}) async-start(f32[2,16,16,32,128]{4,3,2,0,1:T(8,128)} %fusion.44), calls=%async_computation.2 | async-start | bytes 16777216 | tf_op jit(solution)/shard_map/all_to_all | solution.py:101
  716.8 11.8 %copy-start.5 = (f32[1,256,32,128]{3,1,2,0:T(8,128)S(1)}, f32[1,256,32,128]{3,1,2,0:T(8,128)}, u32[]{:S(2)}) copy-start(f32[1,256,32,128]{3,1,2,0:T(8,128)} %get-tuple-element.43) | copy-start | bytes 12582916
  (5 other events, 23.1 us)

commit v5 on v4

--- a/solution.py
+++ b/solution.py
@@ -81,7 +81,8 @@
             return jnp.stack([out_re, out_im])
 
         def to_k(x):
-            xs = x.reshape(2, ndev, kb, nrows, ncols)
+            lead = x.shape[0]
+            xs = x.reshape(lead, ndev, kb, nrows, ncols)
             got = lax.all_to_all(xs, ("row", "col"), 1, 1, tiled=True)
             rows = [
                 jnp.concatenate([got[:, a * ncol + b] for b in range(ncol)], axis=-1)
@@ -98,23 +99,31 @@
                 ],
                 axis=1,
             )
-            got = lax.all_to_all(ys, ("row", "col"), 1, 1, tiled=True)
-            return got.reshape(2, orbs, nrows, ncols)
+            return lax.all_to_all(ys, ("row", "col"), 1, 1, tiled=True)
 
         dt = time_step
         dt2 = 0.5 * time_step * time_step
         g = green
-        g_k = to_k(g)
         p = left_mul(g)
-        p_k = to_k(p)
-        q = apply_ij(g_k) + lad_kb * g_k
-        e = p_k + q + src_k
-        w = e + p_k
-        part_k = neg_i(q, dt) - dt2 * (apply_ij(w) + lad_kb * e)
-        part_k_a = from_k(part_k)
+        gp_k = to_k(jnp.concatenate([g, p]))
         e2 = p + lad_a * g + src_a
         part_a = g + neg_i(p + src_a, dt) - dt2 * left_mul(e2)
-        return part_a + part_k_a
+        gp_k, part_a = lax.optimization_barrier((gp_k, part_a))
+        nchunk = 2
+        kc = kb // nchunk
+        backs = []
+        for h in range(nchunk):
+            sl = slice(h * kc, (h + 1) * kc)
+            g_k = gp_k[:2, sl]
+            p_k = gp_k[2:, sl]
+            src_h = src_k[:, sl]
+            q = apply_ij(g_k) + lad_kb * g_k
+            e = p_k + q + src_h
+            w = e + p_k
+            part_k = neg_i(q, dt) - dt2 * (apply_ij(w) + lad_kb * e)
+            backs.append(from_k(part_k))
+        back = jnp.stack(backs, axis=2).reshape(2, orbs, nrows, ncols)
+        return part_a + back
 
     return on_device
 

time: 781 us -> 786 us (level)
  blocking collectives: 0 us -> 97.2 us
  waiting for transfers between devices: 452 us -> 382 us
  matrix products: 126 us -> 109 us
    all_to_all x0 -> x1, blocking collectives: none -> 97.2 us  [from_k(): return lax.all_to_all(ys, ('row', 'col'), 1, 1, tiled=True)]
    all_to_all x1, waiting for transfers between devices: 148 us -> 72.9 us  [from_k(): return lax.all_to_all(ys, ('row', 'col'), 1, 1, tiled=True)]
    sub x1, other arithmetic: 19.1 us -> 5.91 us  [on_device(): part_k = neg_i(q, dt) - dt2 * (apply_ij(w) + lad_kb * e)]
    all_to_all x1 -> x0, local copies, waits for them, and re-layouts: 11.8 us -> none  [from_k(): got = lax.all_to_all(ys, ('row', 'col'), 1, 1, tiled=True)]
    add x0 -> x1, other arithmetic: none -> 11.2 us  [on_device(): return part_a + back]
    dot_general x8 -> x16, matrix products: 33.8 us -> 22.7 us  [lj(): return jnp.einsum('kia,ja->kij', xm, hm, precision=matmul_precision)]
    all_to_all x2 -> x1, waiting for transfers between devices: 304 us -> 309 us  [to_k(): got = lax.all_to_all(xs, ('row', 'col'), 1, 1, tiled=True)]
    dot_general x8 -> x16, matrix products: 45.7 us -> 41.3 us  [li(): return jnp.einsum('ia,kaj->kij', hm, xm, precision=matmul_precision)]
  transfers between devices with their start and end apart: 3 -> 2, of which waited for: 3 -> 2; matrix products, arithmetic and copies ran while one was open for 12% -> 9% of each run, Pallas kernels for 0% -> 0%
where the time goes in v5:
time: 786 us; the launch traced here: 777 us
  waiting for transfers between devices  382 us (49%)
  matrix products  109 us (14%)
  blocking collectives  97.2 us (12%)
  local copies, waits for them, and re-layouts  93.3 us (12%)
  other arithmetic  83.2 us (11%)
  starting transfers between devices  11.5 us (1%)
    all_to_all x1, waiting for transfers between devices, to_k(): got = lax.all_to_all(xs, ('row', 'col'), 1, 1, tiled=True)  309 us
    all_to_all x1, blocking collectives, from_k(): return lax.all_to_all(ys, ('row', 'col'), 1, 1, tiled=True)  97.2 us
    all_to_all x1, waiting for transfers between devices, from_k(): return lax.all_to_all(ys, ('row', 'col'), 1, 1, tiled=True)  72.9 us
    dot_general x16, matrix products, li(): return jnp.einsum('ia,kaj->kij', hm, xm, precision=matmul_precision)  41.3 us
    dot_general x2, matrix products, left_mul(): out = jnp.einsum('ab,bmn->amn', h_big, flat, precision=matmul_precision)  40.9 us
    unnamed x68, local copies, waits for them, and re-layouts  35.4 us
    dot_general x16, matrix products, lj(): return jnp.einsum('kia,ja->kij', xm, hm, precision=matmul_precision)  22.7 us
    add x1, other arithmetic, on_device(): w = e + p_k  19.3 us
  transfers between devices with their start and end apart: 2, of which 2 were waited for; matrix products, arithmetic and copies ran while one was open for 9% of the time, Pallas kernels for 0%

profile of v5, /device:TPU:13, one launch (start us, length us, event | category | flops | bytes accessed | tf_op | source)
XLA Modules:
  0.0 777.0 jit_solution(17114941829480126514)
XLA Ops:
  10.6 14.1 %fusion.3 = f32[2,256,32,128]{3,1,2,0:T(8,128)} fusion(f32[2,256,512,1]{2,1,3,0:T(8,128)S(1)} %bitcast.412, f32[512,32,128]{2,1,0:T(8,128)} %bitcast.406), kind=kOutput, calls=%fused_computation.10 | convolution fusion | flops 6442450944 | bytes 17825792 | tf_op jit(solution)/shard_map/ab,bmn->amn/dot_general | solution.py:66
  24.8 3.9 subtract_multiply_fusion.1
  28.7 14.9 %add_add_fusion = (f32[2,256,32,128]{3,1,2,0:T(8,128)}, f32[2,256,32,128]{3,1,2,0:T(8,128)}, f32[2,256,32,128]{3,1,2,0:T(8,128)}) fusion(f32[2,256,32,128]{3,1,2,0:T(8,128)} %fusion.3, f32[1,256,32,128]{3,1,2,0:T(8,128)} %get-tuple-element.52, f32[1,256,32,128]{3,1,2,0:T(8,128)S(1)} %get-tuple-element.51, f32[32,128]{1,0:T(8,128)S(1)} %compare_select_fusion.1, ...), kind=kLoop, calls=%fused_computation.14 | loop fusion | flops 10485760 | bytes 50348032 | tf_op jit(solution)/shard_map/add | solution.py:109
  43.7 6.8 pad_maximum_fusion
  50.5 12.3 %copy.30 = f32[4,16,16,32,128]{4,3,2,0,1:T(8,128)} copy(f32[4,16,16,32,128]{4,2,1,3,0:T(8,128)S(1)} %bitcast.409) | data formatting | bytes 33554432 | tf_op jit(solution)/shard_map/reshape | solution.py:85
  62.7 6.6 all-to-all-start
  69.3 11.6 %copy.35 = f32[2,256,32,128]{3,2,1,0:T(8,128)} copy(f32[2,256,32,128]{3,1,2,0:T(8,128)} %get-tuple-element.18) | data formatting | bytes 16777216 | tf_op jit(solution)/shard_map/add | solution.py:109
  84.3 4.1 subtract_multiply_fusion
  88.4 6.8 slice_multiply_fusion.1
  95.2 26.7 %fusion = f32[2,256,32,128]{3,1,2,0:T(8,128)} fusion(f32[1,256,32,128]{3,1,2,0:T(8,128)} %get-tuple-element.38, f32[1,256,32,128]{3,1,2,0:T(8,128)S(1)} %get-tuple-element.37, f32[2,256,512,1]{2,1,3,0:T(8,128)S(1)} %bitcast.413, f32[512,32,128]{2,1,0:T(8,128)} %bitcast.410, f32[2,256,32,128]{3,2,1,0:T(8,128)S(1)} %bitcast.408), kind=kOutput, calls=%fused_computation.3 | convolution fusion | flops 6450839552 | bytes 34603008 | tf_op jit(solution)/shard_map/ab,bmn->amn/dot_general | solution.py:66
  122.0 309.4 %all-to-all-done = f32[4,16,16,32,128]{4,3,2,0,1:T(8,128)} async-done(((f32[4,16,16,32,128]{4,3,2,0,1:T(8,128)}), f32[4,16,16,32,128]{4,3,2,0,1:T(8,128)}, u32[]{:S(2)}, u32[]{:S(2)}) %all-to-all-start) | async-done | bytes 16777248 | tf_op jit(solution)/shard_map/all_to_all | solution.py:86
  431.4 7.1 slice_bitcast_fusion.29
  456.6 3.0 fusion.20
  459.7 4.4 fusion.22
  469.7 19.3 %slice_add_fusion.1 = (f32[2,8,256,256]{3,2,1,0:T(8,128)}, f32[2,8,256,256]{3,2,1,0:T(8,128)}, f32[2,8,256,256]{3,2,1,0:T(8,128)}, f32[2,8,256,256]{3,2,1,0:T(8,...) fusion(f32[4,16,256,256]{3,2,1,0:T(8,128)} %copy-done, f32[1,16,256,256]{3,2,1,0:T(8,128)} %get-tuple-element.54, ...), kind=kLoop, calls=%fused_computation.37 | loop fusion | flops 14680064 | bytes 58982400 | tf_op jit(solution)/shard_map/add | solution.py:122
  515.9 4.3 fusion.40
  529.9 5.9 maximum_subtract_fusion
  547.4 4.9 all-to-all-start.1
  571.9 72.9 %all-to-all-done.1 = f32[2,16,8,32,128]{4,3,2,0,1:T(8,128)} async-done(((f32[2,16,8,32,128]{4,3,2,0,1:T(8,128)}), f32[2,16,8,32,128]{4,3,2,0,1:T(8,128)}, u32[]{:S(2)}, u32[]{:S(2)}) %all-to-all-start.1) | async-done | bytes 4194336 | tf_op jit(solution)/shard_map/all_to_all | solution.py:102
  644.8 97.2 %all_to_all.15 = f32[2,16,8,32,128]{4,3,2,0,1:T(8,128)S(1)} all-to-all(f32[2,16,8,32,128]{4,3,2,0,1:T(8,128)} %fusion.111), channel_id=1, replica_groups=mesh['grp'=2,'row'=8,'col'=2] {'row','col'}, dimensions={1} | all-to-all | bytes 8388608 | tf_op jit(solution)/shard_map/all_to_all | solution.py:102
  741.9 3.6 pad_maximum_fusion.2
  745.6 8.3 %copy.37 = f32[2,16,2,8,32,128]{5,3,2,1,4,0:T(8,128)} copy(f32[2,16,2,8,32,128]{5,4,3,0,1,2:T(8,128)S(1)} %pad_maximum_fusion.2) | data formatting | bytes 16777216 | tf_op jit(solution)/shard_map/stack | solution.py:125
  753.8 11.2 %bitcast_add_fusion = f32[2,256,32,128]{3,1,2,0:T(8,128)} fusion(f32[2,256,32,128]{3,1,2,0:T(8,128)} %fusion, f32[2,16,2,8,32,128]{5,3,2,1,4,0:T(8,128)} %copy.37), kind=kLoop, calls=%fused_computation.7 | loop fusion | flops 2097152 | bytes 25165824 | tf_op jit(solution)/shard_map/add | solution.py:126
  765.0 11.6 %copy.38 = f32[2,256,32,128]{3,2,1,0:T(8,128)} copy(f32[2,256,32,128]{3,1,2,0:T(8,128)} %bitcast_add_fusion) | data formatting | bytes 16777216 | tf_op jit(solution)/shard_map/add | solution.py:126
  (127 shorter events, 105.2 us)
Async XLA Ops:
  62.7 368.7 %all-to-all-start = ((f32[4,16,16,32,128]{4,3,2,0,1:T(8,128)}), f32[4,16,16,32,128]{4,3,2,0,1:T(8,128)}, u32[]{:S(2)}, u32[]{:S(2)}) async-start(f32[4,16,16,32,128]{4,3,2,0,1:T(8,128)} %copy.30), calls=%async_computation | async-start | bytes 33554432 | tf_op jit(solution)/shard_map/all_to_all | solution.py:86
  69.3 12.4 %copy-start.16 = (s32[256]{0:T(256)S(1)}, s32[256]{0:T(256)}, u32[]{:S(2)}) copy-start(s32[256]{0:T(256)} %param.10) | copy-start | bytes 3076
  69.3 12.6 %copy-start.14 = (s32[4096]{0:T(1024)S(1)}, s32[4096]{0:T(1024)}, u32[]{:S(2)}) copy-start(s32[4096]{0:T(1024)} %param.13) | copy-start | bytes 49156
  69.3 12.6 %copy-start.15 = (s32[4096]{0:T(1024)S(1)}, s32[4096]{0:T(1024)}, u32[]{:S(2)}) copy-start(s32[4096]{0:T(1024)} %param.12) | copy-start | bytes 49156
  88.4 6.8 slice-start
  88.4 6.8 slice-start.1
  439.6 1.0 copy-start.1
  440.6 26.2 %copy-start = (f32[4,16,256,256]{3,2,1,0:T(8,128)}, f32[4,16,256,256]{3,2,1,0:T(8,128)S(1)}, u32[]{:S(2)}) copy-start(f32[4,16,256,256]{3,2,1,0:T(8,128)S(1)} %maximum_dynamic-update-slice_fusion) | copy-start | bytes 50331652
  489.0 2.8 copy-start.3
  497.6 3.4 copy-start.2
  506.5 5.0 copy-start.5
  511.5 2.2 copy-start.4
  513.7 1.6 copy-start.12
  513.7 2.2 copy-start.13
  520.2 2.7 copy-start.10
  520.2 2.7 copy-start.11
  523.0 2.7 copy-start.9
  525.6 2.9 copy-start.6
  525.6 4.2 copy-start.7
  547.4 97.4 %all-to-all-start.1 = ((f32[2,16,8,32,128]{4,3,2,0,1:T(8,128)}), f32[2,16,8,32,128]{4,3,2,0,1:T(8,128)}, u32[]{:S(2)}, u32[]{:S(2)}) async-start(f32[2,16,8,32,128]{4,3,2,0,1:T(8,128)} %fusion.127), calls=%async_computation.1 | async-start | bytes 8388608 | tf_op jit(solution)/shard_map/all_to_all | solution.py:102
  552.3 13.7 %copy-start.8 = (f32[2,8,256,256]{3,2,1,0:T(8,128)S(1)}, f32[2,8,256,256]{3,2,1,0:T(8,128)}, u32[]{:S(2)}) copy-start(f32[2,8,256,256]{3,2,1,0:T(8,128)} %get-tuple-element.56) | copy-start | bytes 12582916

commit v6 on v5

--- a/solution.py
+++ b/solution.py
@@ -109,7 +109,7 @@
         e2 = p + lad_a * g + src_a
         part_a = g + neg_i(p + src_a, dt) - dt2 * left_mul(e2)
         gp_k, part_a = lax.optimization_barrier((gp_k, part_a))
-        nchunk = 2
+        nchunk = 1
         kc = kb // nchunk
         backs = []
         for h in range(nchunk):

time: 786 us -> 807 us (1.027)
  blocking collectives: 97.2 us -> 187 us
  waiting for transfers between devices: 382 us -> 309 us
  local copies, waits for them, and re-layouts: 93.3 us -> 75.9 us
  other arithmetic: 83.2 us -> 96.4 us
  matrix products: 109 us -> 122 us
    all_to_all x1, blocking collectives: 97.2 us -> 187 us  [from_k(): return lax.all_to_all(ys, ('row', 'col'), 1, 1, tiled=True)]
    all_to_all x1 -> x0, waiting for transfers between devices: 72.9 us -> none  [from_k(): return lax.all_to_all(ys, ('row', 'col'), 1, 1, tiled=True)]
    unnamed x68 -> x45, local copies, waits for them, and re-layouts: 35.4 us -> 16.9 us
    sub x1, other arithmetic: 5.91 us -> 17.7 us  [on_device(): part_k = neg_i(q, dt) - dt2 * (apply_ij(w) + lad_kb * e)]
    another operation x1 -> x0, local copies, waits for them, and re-layouts: 8.25 us -> none  [on_device(): back = jnp.stack(backs, axis=2).reshape(2, orbs, nrows, ncols)]
    all_to_all x0 -> x1, local copies, waits for them, and re-layouts: none -> 8.25 us  [from_k(): return lax.all_to_all(ys, ('row', 'col'), 1, 1, tiled=True)]
    dot_general x16 -> x8, matrix products: 22.7 us -> 29.6 us  [lj(): return jnp.einsum('kia,ja->kij', xm, hm, precision=matmul_precision)]
    dot_general x16 -> x8, matrix products: 41.3 us -> 48.1 us  [li(): return jnp.einsum('ia,kaj->kij', hm, xm, precision=matmul_precision)]
  transfers between devices with their start and end apart: 2 -> 1, of which waited for: 2 -> 1; matrix products, arithmetic and copies ran while one was open for 9% -> 7% of each run, Pallas kernels for 0% -> 0%
where the time goes in v6:
time: 807 us; the launch traced here: 798 us
  waiting for transfers between devices  309 us (38%)
  blocking collectives  187 us (23%)
  matrix products  122 us (15%)
  other arithmetic  96.4 us (12%)
  local copies, waits for them, and re-layouts  75.9 us (9%)
    all_to_all x1, waiting for transfers between devices, to_k(): got = lax.all_to_all(xs, ('row', 'col'), 1, 1, tiled=True)  309 us
    all_to_all x1, blocking collectives, from_k(): return lax.all_to_all(ys, ('row', 'col'), 1, 1, tiled=True)  187 us
    dot_general x8, matrix products, li(): return jnp.einsum('ia,kaj->kij', hm, xm, precision=matmul_precision)  48.1 us
    dot_general x2, matrix products, left_mul(): out = jnp.einsum('ab,bmn->amn', h_big, flat, precision=matmul_precision)  40.9 us
    dot_general x8, matrix products, lj(): return jnp.einsum('kia,ja->kij', xm, hm, precision=matmul_precision)  29.6 us
    sub x1, other arithmetic, on_device(): part_k = neg_i(q, dt) - dt2 * (apply_ij(w) + lad_kb * e)  17.7 us
    add x1, other arithmetic, on_device(): w = e + p_k  17.4 us
    unnamed x45, local copies, waits for them, and re-layouts  16.9 us
  transfers between devices with their start and end apart: 1, of which 1 were waited for; matrix products, arithmetic and copies ran while one was open for 7% of the time, Pallas kernels for 0%

profile of v6, /device:TPU:13, one launch (start us, length us, event | category | flops | bytes accessed | tf_op | source)
XLA Modules:
  0.0 797.8 jit_solution(10269131665141197239)
XLA Ops:
  10.6 14.1 %fusion.4 = f32[2,256,32,128]{3,1,2,0:T(8,128)} fusion(f32[2,256,512,1]{2,1,3,0:T(8,128)S(1)} %bitcast.245, f32[512,32,128]{2,1,0:T(8,128)} %bitcast.238), kind=kOutput, calls=%fused_computation.12 | convolution fusion | flops 6442450944 | bytes 17825792 | tf_op jit(solution)/shard_map/ab,bmn->amn/dot_general | solution.py:66
  28.7 14.9 %add_add_fusion = (f32[2,256,32,128]{3,1,2,0:T(8,128)}, f32[2,256,32,128]{3,1,2,0:T(8,128)}, f32[2,256,32,128]{3,1,2,0:T(8,128)}) fusion(f32[2,256,32,128]{3,1,2,0:T(8,128)} %fusion.4, f32[1,256,32,128]{3,1,2,0:T(8,128)} %get-tuple-element.43, f32[1,256,32,128]{3,1,2,0:T(8,128)S(1)} %get-tuple-element.42, f32[32,128]{1,0:T(8,128)S(1)} %compare_select_fusion.1, ...), kind=kLoop, calls=%fused_computation.16 | loop fusion | flops 10485760 | bytes 50348032 | tf_op jit(solution)/shard_map/add | solution.py:109
  43.6 6.8 pad_maximum_fusion
  50.4 12.3 %copy.30 = f32[4,16,16,32,128]{4,3,2,0,1:T(8,128)} copy(f32[4,16,16,32,128]{4,2,1,3,0:T(8,128)S(1)} %bitcast.243) | data formatting | bytes 33554432 | tf_op jit(solution)/shard_map/reshape | solution.py:85
  62.7 6.6 all-to-all-start
  69.3 11.6 %copy.35 = f32[2,256,32,128]{3,2,1,0:T(8,128)} copy(f32[2,256,32,128]{3,1,2,0:T(8,128)} %get-tuple-element.11) | data formatting | bytes 16777216 | tf_op jit(solution)/shard_map/add | solution.py:109
  89.1 6.8 slice_multiply_fusion.3
  95.9 26.8 %fusion = f32[2,256,32,128]{3,1,2,0:T(8,128)} fusion(f32[1,256,32,128]{3,1,2,0:T(8,128)} %get-tuple-element.33, f32[1,256,32,128]{3,1,2,0:T(8,128)S(1)} %get-tuple-element.32, f32[2,256,512,1]{2,1,3,0:T(8,128)S(1)} %bitcast.246, f32[512,32,128]{2,1,0:T(8,128)} %bitcast.244, f32[2,256,32,128]{3,2,1,0:T(8,128)S(1)} %bitcast.240), kind=kOutput, calls=%fused_computation.3 | convolution fusion | flops 6450839552 | bytes 34603008 | tf_op jit(solution)/shard_map/ab,bmn->amn/dot_general | solution.py:66
  122.7 308.7 %all-to-all-done = f32[4,16,16,32,128]{4,3,2,0,1:T(8,128)} async-done(((f32[4,16,16,32,128]{4,3,2,0,1:T(8,128)}), f32[4,16,16,32,128]{4,3,2,0,1:T(8,128)}, u32[]{:S(2)}, u32[]{:S(2)}) %all-to-all-start) | async-done | bytes 16777248 | tf_op jit(solution)/shard_map/all_to_all | solution.py:86
  431.4 8.5 %slice_bitcast_fusion.15 = (f32[4,16,32,128]{3,2,1,0:T(8,128)S(1)}, f32[4,16,32,128]{3,2,1,0:T(8,128)S(1)}, f32[4,16,32,128]{3,2,1,0:T(8,128)S(1)}, f32[4,16,32,...) fusion(f32[4,16,16,32,128]{4,3,2,0,1:T(8,128)} %all-to-all-done), kind=kLoop, calls=%fused_computation.88 | loop fusion | bytes 33554432 | tf_op jit(solution)/shard_map/squeeze | solution.py:88
  446.4 4.7 fusion.23
  460.8 4.3 fusion.25
  465.1 8.2 %fusion.16 = f32[1,16,256,256]{3,2,1,0:T(8,128)} fusion(f32[16,256,256]{2,1,0:T(8,128)S(1)} %fusion.21, f32[16,256,256]{2,1,0:T(8,128)} %fusion.29, f32[16,256,256]{1,2,0:T(8,128)} %fusion.23, f32[4,16,256,256]{3,2,1,0:T(8,128)S(1)} %maximum_dynamic-update-slice_fusion, f32[2,256,256]{2,1,0:T(8,128)S(1)} %copy-done.2), kind=kOutput, calls=%fused_computation.36 | convolution fusion | flops 1613758464 | bytes 21233664 | tf_op jit(solution)/shard_map/ia,kaj->kij/dot_general | solution.py:74
  473.3 8.4 %fusion.14 = f32[1,16,256,256]{3,2,1,0:T(8,128)} fusion(f32[16,256,256]{2,1,0:T(8,128)} %fusion.25, f32[16,256,256]{2,1,0:T(8,128)S(1)} %fusion.17, f32[16,256,256]{1,2,0:T(8,128)} %fusion.19, f32[4,16,256,256]{3,2,1,0:T(8,128)S(1)} %maximum_dynamic-update-slice_fusion, f32[2,256,256]{2,1,0:T(8,128)S(1)} %copy-done.2), kind=kOutput, calls=%fused_computation.33 | convolution fusion | flops 1613758464 | bytes 21233664 | tf_op jit(solution)/shard_map/ia,kaj->kij/dot_general | solution.py:74
  481.7 17.4 %slice_add_fusion = (f32[2,16,256,256]{3,2,1,0:T(8,128)}, f32[2,16,256,256]{3,2,1,0:T(8,128)}) fusion(f32[4,16,256,256]{3,2,1,0:T(8,128)} %copy-done, f32[1,16,256,256]{3,2,1,0:T(8,128)} %get-tuple-element.45, f32[1,16,256,256]{3,2,1,0:T(8,128)S(1)} %copy-done.3, f32[256,256]{1,0:T(8,128)S(1)} %copy-done.7, f32[1,16,256,256]{3,2,1,0:T(8,128)} %fusion.14, ...), kind=kLoop, calls=%fused_computation.17 | loop fusion | flops 14680064 | bytes 50593792 | tf_op jit(solution)/shard_map/add | solution.py:122
  499.2 6.1 fusion.35
  524.9 4.2 slice_multiply_fusion.1
  529.1 9.5 %fusion.12 = f32[1,16,256,256]{3,2,1,0:T(8,128)} fusion(f32[16,256,256]{2,1,0:T(8,128)} %fusion.39, f32[16,256,256]{2,1,0:T(8,128)} %fusion.35, f32[16,256,256]{1,2,0:T(8,128)} %fusion.36, f32[2,16,256,256]{3,2,1,0:T(8,128)S(1)} %copy-done.1, f32[2,256,256]{2,1,0:T(8,128)S(1)} %copy-done.2), kind=kOutput, calls=%fused_computation.30 | convolution fusion | flops 1613758464 | bytes 21233664 | tf_op jit(solution)/shard_map/ia,kaj->kij/dot_general | solution.py:74
  538.6 5.2 fusion.10
  543.8 17.7 %maximum_subtract_fusion = f32[2,16,256,256]{3,2,1,0:T(8,128)} fusion(f32[1,16,256,256]{3,2,1,0:T(8,128)} %get-tuple-element.30, f32[1,16,256,256]{3,2,1,0:T(8,128)} %get-tuple-element.29, f32[1,16,256,256]{3,2,1,0:T(8,128)} %fusion.10, f32[1,16,256,256]{3,2,1,0:T(8,128)} %fusion.12, f32[256,256]{1,0:T(8,128)S(1)} %copy-done.7, ...), kind=kLoop, calls=%fused_computation.5 | loop fusion | flops 18874368 | bytes 50593792 | tf_op jit(solution)/shard_map/sub | solution.py:123
  579.2 187.1 %all_to_all.10 = f32[2,16,16,32,128]{4,3,2,0,1:T(8,128)S(1)} all-to-all(f32[2,16,16,32,128]{4,3,2,0,1:T(8,128)S(1)} %fusion.63), channel_id=1, replica_groups=mesh['grp'=2,'row'=8,'col'=2] {'row','col'}, dimensions={1} | all-to-all | bytes 16777216 | tf_op jit(solution)/shard_map/all_to_all | solution.py:102
  766.3 8.3 %copy.37 = f32[2,16,16,32,128]{4,2,1,3,0:T(8,128)} copy(f32[2,16,16,32,128]{4,3,2,0,1:T(8,128)S(1)} %all_to_all.10) | data formatting | bytes 16777216 | tf_op jit(solution)/shard_map/all_to_all | solution.py:102
  774.5 11.2 %bitcast_add_fusion = f32[2,256,32,128]{3,1,2,0:T(8,128)} fusion(f32[2,256,32,128]{3,1,2,0:T(8,128)} %fusion, f32[2,16,16,32,128]{4,2,1,3,0:T(8,128)} %copy.37), kind=kLoop, calls=%fused_computation.9 | loop fusion | flops 2097152 | bytes 25165824 | tf_op jit(solution)/shard_map/add | solution.py:126
  785.7 11.6 %copy.38 = f32[2,256,32,128]{3,2,1,0:T(8,128)} copy(f32[2,256,32,128]{3,1,2,0:T(8,128)} %bitcast_add_fusion) | data formatting | bytes 16777216 | tf_op jit(solution)/shard_map/add | solution.py:126
  (84 shorter events, 76.1 us)
Async XLA Ops:
  62.7 368.7 %all-to-all-start = ((f32[4,16,16,32,128]{4,3,2,0,1:T(8,128)}), f32[4,16,16,32,128]{4,3,2,0,1:T(8,128)}, u32[]{:S(2)}, u32[]{:S(2)}) async-start(f32[4,16,16,32,128]{4,3,2,0,1:T(8,128)} %copy.30), calls=%async_computation | async-start | bytes 33554432 | tf_op jit(solution)/shard_map/all_to_all | solution.py:86
  69.2 12.4 %copy-start.10 = (s32[256]{0:T(256)S(1)}, s32[256]{0:T(256)}, u32[]{:S(2)}) copy-start(s32[256]{0:T(256)} %param.10) | copy-start | bytes 3076
  69.3 13.2 %copy-start.8 = (s32[4096]{0:T(1024)S(1)}, s32[4096]{0:T(1024)}, u32[]{:S(2)}) copy-start(s32[4096]{0:T(1024)} %param.13) | copy-start | bytes 49156
  69.3 13.2 %copy-start.9 = (s32[4096]{0:T(1024)S(1)}, s32[4096]{0:T(1024)}, u32[]{:S(2)}) copy-start(s32[4096]{0:T(1024)} %param.12) | copy-start | bytes 49156
  89.1 6.8 slice-start
  89.1 6.8 slice-start.1
  443.4 1.0 copy-start.2
  444.4 28.9 %copy-start = (f32[4,16,256,256]{3,2,1,0:T(8,128)}, f32[4,16,256,256]{3,2,1,0:T(8,128)S(1)}, u32[]{:S(2)}) copy-start(f32[4,16,256,256]{3,2,1,0:T(8,128)S(1)} %maximum_dynamic-update-slice_fusion) | copy-start | bytes 50331652
  473.3 8.4 %copy-start.3 = (f32[1,16,256,256]{3,2,1,0:T(8,128)S(1)}, f32[1,16,256,256]{3,2,1,0:T(8,128)}, u32[]{:S(2)}) copy-start(f32[1,16,256,256]{3,2,1,0:T(8,128)} %get-tuple-element.44) | copy-start | bytes 12582916
  473.3 8.4 %copy-start.7 = (f32[256,256]{1,0:T(8,128)S(1)}, f32[256,256]{1,0:T(8,128)}, u32[]{:S(2)}) copy-start(f32[256,256]{1,0:T(8,128)} %compare_select_fusion) | copy-start | bytes 786436
  499.2 6.2 copy-start.1
  517.0 7.8 slice-start.2
  521.0 3.9 slice-start.3
  529.0 9.5 %copy-start.4 = (f32[16,256,256]{2,1,0:T(8,128)S(1)}, f32[16,256,256]{2,1,0:T(8,128)}, u32[]{:S(2)}) copy-start(f32[16,256,256]{2,1,0:T(8,128)} %fusion.33) | copy-start | bytes 12582916
  529.0 9.5 %copy-start.5 = (f32[16,256,256]{1,2,0:T(8,128)S(1)}, f32[16,256,256]{1,2,0:T(8,128)}, u32[]{:S(2)}) copy-start(f32[16,256,256]{1,2,0:T(8,128)} %fusion.34) | copy-start | bytes 12582916
  529.0 9.5 %copy-start.6 = (f32[16,256,256]{2,1,0:T(8,128)S(1)}, f32[16,256,256]{2,1,0:T(8,128)}, u32[]{:S(2)}) copy-start(f32[16,256,256]{2,1,0:T(8,128)} %fusion.37) | copy-start | bytes 12582916

commit v7 on v4

--- a/solution.py
+++ b/solution.py
@@ -89,8 +89,8 @@
             ]
             return jnp.concatenate(rows, axis=-2)
 
-        def from_k(y):
-            ys = jnp.stack(
+        def send_k(y):
+            return jnp.stack(
                 [
                     y[:, :, a * nrows:(a + 1) * nrows, b * ncols:(b + 1) * ncols]
                     for a in range(nrow)
@@ -98,6 +98,8 @@
                 ],
                 axis=1,
             )
+
+        def recv_k(ys):
             got = lax.all_to_all(ys, ("row", "col"), 1, 1, tiled=True)
             return got.reshape(2, orbs, nrows, ncols)
 
@@ -111,9 +113,11 @@
         e = p_k + q + src_k
         w = e + p_k
         part_k = neg_i(q, dt) - dt2 * (apply_ij(w) + lad_kb * e)
-        part_k_a = from_k(part_k)
-        e2 = p + lad_a * g + src_a
-        part_a = g + neg_i(p + src_a, dt) - dt2 * left_mul(e2)
+        ys, g2, p2 = lax.optimization_barrier((send_k(part_k), g, p))
+        part_k_a = recv_k(ys)
+        e2 = p2 + lad_a * g2 + src_a
+        part_a = g2 + neg_i(p2 + src_a, dt) - dt2 * left_mul(e2)
+        part_a = lax.optimization_barrier(part_a)
         return part_a + part_k_a
 
     return on_device

time: 781 us -> 751 us (0.962)
  waiting for transfers between devices: 452 us -> 425 us
  other arithmetic: 78.2 us -> 94.7 us
  local copies, waits for them, and re-layouts: 97.3 us -> 81 us
    all_to_all x1, waiting for transfers between devices: 148 us -> 121 us  [recv_k(): got = lax.all_to_all(ys, ('row', 'col'), 1, 1, tiled=True)]
    add x1 -> x2, other arithmetic: 11.7 us -> 25.6 us  [the longest x1 14 us: on_device(): return part_a + part_k_a]
    unnamed x67 -> x71, local copies, waits for them, and re-layouts: 32.6 us -> 23.8 us
  transfers between devices with their start and end apart: 3 -> 3, of which waited for: 3 -> 3; matrix products, arithmetic and copies ran while one was open for 12% -> 16% of each run, Pallas kernels for 0% -> 0%
where the time goes in v7:
time: 751 us; the launch traced here: 742 us
  waiting for transfers between devices  425 us (57%)
  matrix products  122 us (16%)
  other arithmetic  94.7 us (13%)
  local copies, waits for them, and re-layouts  81 us (11%)
  starting transfers between devices  17.4 us (2%)
    all_to_all x2, waiting for transfers between devices, to_k(): got = lax.all_to_all(xs, ('row', 'col'), 1, 1, tiled=True)  304 us
    all_to_all x1, waiting for transfers between devices, recv_k(): got = lax.all_to_all(ys, ('row', 'col'), 1, 1, tiled=True)  121 us
    dot_general x8, matrix products, li(): return jnp.einsum('ia,kaj->kij', hm, xm, precision=matmul_precision)  45.6 us
    dot_general x2, matrix products, left_mul(): out = jnp.einsum('ab,bmn->amn', h_big, flat, precision=matmul_precision)  39.3 us
    dot_general x8, matrix products, lj(): return jnp.einsum('kia,ja->kij', xm, hm, precision=matmul_precision)  33.7 us
    unnamed x71, local copies, waits for them, and re-layouts  23.8 us
    add x1, other arithmetic, on_device(): w = e + p_k  19.5 us
    sub x1, other arithmetic, on_device(): part_k = neg_i(q, dt) - dt2 * (apply_ij(w) + lad_kb * e)  19 us
  transfers between devices with their start and end apart: 3, of which 3 were waited for; matrix products, arithmetic and copies ran while one was open for 16% of the time, Pallas kernels for 0%

profile of v7, /device:TPU:13, one launch (start us, length us, event | category | flops | bytes accessed | tf_op | source)
XLA Modules:
  0.0 741.6 jit_solution(6154003391886153733)
XLA Ops:
  0.0 8.3 %copy.31 = f32[2,16,16,32,128]{4,3,2,0,1:T(8,128)} copy(f32[2,16,16,32,128]{4,3,2,1,0:T(8,128)} %bitcast.264) | data formatting | bytes 16777216 | tf_op jit(solution)/shard_map/reshape | solution.py:84
  8.3 6.7 all-to-all-start
  15.0 12.3 %fusion.5 = f32[512,32,128]{2,0,1:T(8,128)S(1)} fusion(f32[512,32,128]{2,1,0:T(8,128)} %bitcast.265, f32[256,256]{1,0:T(8,128)S(1)} %get-tuple-element.58, f32[256,256]{1,0:T(8,128)S(1)} %get-tuple-element.57, f32[256,256]{1,0:T(8,128)S(1)} %fusion.92), kind=kOutput, calls=%fused_computation.12 | convolution fusion | flops 6443237376 | bytes 17563648 | tf_op jit(solution)/shard_map/ab,bmn->amn/dot_general | solution.py:66
  30.8 8.1 %copy.34 = f32[2,16,16,32,128]{4,3,2,0,1:T(8,128)} copy(f32[2,16,16,32,128]{4,2,1,0,3:T(8,128)S(1)} %bitcast.268) | data formatting | bytes 16777216 | tf_op jit(solution)/shard_map/reshape;reshape | solution.py:84
  38.9 158.4 %all-to-all-done = f32[2,16,16,32,128]{4,3,2,0,1:T(8,128)} async-done(((f32[2,16,16,32,128]{4,3,2,0,1:T(8,128)}), f32[2,16,16,32,128]{4,3,2,0,1:T(8,128)}, u32[]{:S(2)}, u32[]{:S(2)}) %all-to-all-start) | async-done | bytes 8388640 | tf_op jit(solution)/shard_map/all_to_all | solution.py:85
  197.3 5.4 all-to-all-start.1
  239.3 145.6 %all-to-all-done.1 = f32[2,16,16,32,128]{4,3,2,0,1:T(8,128)} async-done(((f32[2,16,16,32,128]{4,3,2,0,1:T(8,128)}), f32[2,16,16,32,128]{4,3,2,0,1:T(8,128)}, u32[]{:S(2)}, u32[]{:S(2)}) %all-to-all-start.1) | async-done | bytes 8388640 | tf_op jit(solution)/shard_map/all_to_all | solution.py:85
  384.9 5.9 slice_bitcast_fusion.45
  392.5 9.6 %fusion.14 = f32[1,16,256,256]{3,2,1,0:T(8,128)} fusion(f32[16,256,256]{2,1,0:T(8,128)} %fusion.21, f32[16,256,256]{2,1,0:T(8,128)} %fusion.17, f32[16,256,256]{1,2,0:T(8,128)} %fusion.18, f32[2,16,256,256]{3,2,1,0:T(8,128)S(1)} %copy-done.1, f32[2,256,256]{2,1,0:T(8,128)S(1)} %copy-done.4), kind=kOutput, calls=%fused_computation.35 | convolution fusion | flops 1613758464 | bytes 21233664 | tf_op jit(solution)/shard_map/ia,kaj->kij/dot_general | solution.py:74
  402.2 5.3 fusion.12
  415.2 19.5 %fusion.36 = (f32[2,16,256,256]{3,2,1,0:T(8,128)}, f32[2,16,256,256]{3,2,1,0:T(8,128)}) fusion(f32[2,16,256,256]{3,2,1,0:T(8,128)} %maximum_dynamic-update-slice_fusion.8, f32[1,16,256,256]{3,2,1,0:T(8,128)} %get-tuple-element.62, f32[1,16,256,256]{3,2,1,0:T(8,128)} %get-tuple-element.61, f32[2,16,256,256]{3,2,1,0:T(8,128)} %copy-done, ...), kind=kLoop, calls=%fused_computation.61 | loop fusion | flops 14680064 | bytes 50593792 | tf_op jit(solution)/shard_map/add | solution.py:114
  434.7 6.2 fusion.25
  464.9 9.5 %fusion.10 = f32[1,16,256,256]{3,2,1,0:T(8,128)} fusion(f32[16,256,256]{2,1,0:T(8,128)} %fusion.29, f32[16,256,256]{2,1,0:T(8,128)} %fusion.25, f32[16,256,256]{1,2,0:T(8,128)} %fusion.26, f32[2,16,256,256]{3,2,1,0:T(8,128)S(1)} %copy-done.2, f32[2,256,256]{2,1,0:T(8,128)S(1)} %copy-done.4), kind=kOutput, calls=%fused_computation.29 | convolution fusion | flops 1613758464 | bytes 21233664 | tf_op jit(solution)/shard_map/ia,kaj->kij/dot_general | solution.py:74
  474.4 5.3 fusion.8
  479.7 19.0 %maximum_subtract_fusion = f32[2,16,256,256]{3,2,1,0:T(8,128)} fusion(f32[1,16,256,256]{3,2,1,0:T(8,128)} %get-tuple-element.18, f32[1,16,256,256]{3,2,1,0:T(8,128)} %get-tuple-element.17, f32[1,16,256,256]{3,2,1,0:T(8,128)} %fusion.8, f32[1,16,256,256]{3,2,1,0:T(8,128)} %fusion.10, f32[256,256]{1,0:T(8,128)S(1)} %compare_select_fusion, ...), kind=kLoop, calls=%fused_computation.1 | loop fusion | flops 18874368 | bytes 50593792 | tf_op jit(solution)/shard_map/sub | solution.py:115
  519.6 5.3 all-to-all-start.2
  532.4 11.6 %add_add_fusion = (f32[2,256,32,128]{3,1,2,0:T(8,128)S(1)}, f32[2,256,32,128]{3,1,2,0:T(8,128)}) fusion(f32[2,256,32,128]{3,2,1,0:T(8,128)} %param.7, f32[2,256,32,128]{3,1,0,2:T(8,128)} %bitcast.269, f32[1,256,32,128]{3,1,2,0:T(8,128)} %get-tuple-element.60, f32[1,256,32,128]{3,1,2,0:T(8,128)S(1)} %get-tuple-element.59, f32[32,128]{1,0:T(8,128)S(1)} %compare_select_fusion.1), kind=kLoop, calls=%fused_computation.14 | loop fusion | flops 10485760 | bytes 41959424 | tf_op jit(solution)/shard_map/add | solution.py:118
  544.0 8.3 %copy.41 = f32[2,256,32,128]{3,2,1,0:T(8,128)} copy(f32[2,256,32,128]{3,1,2,0:T(8,128)S(1)} %get-tuple-element.13) | data formatting | bytes 16777216 | tf_op jit(solution)/shard_map/add | solution.py:118
  552.2 6.8 slice_multiply_fusion.1
  559.0 27.0 %fusion.1 = f32[2,256,32,128]{3,1,2,0:T(8,128)} fusion(f32[1,256,32,128]{3,1,2,0:T(8,128)} %get-tuple-element.16, f32[1,256,32,128]{3,1,2,0:T(8,128)S(1)} %get-tuple-element.15, f32[2,256,32,128]{3,2,1,0:T(8,128)S(1)} %bitcast.267, f32[2,256,512,1]{2,1,3,0:T(8,128)S(1)} %bitcast.274, f32[512,32,128]{2,1,0:T(8,128)} %bitcast.272), kind=kOutput, calls=%fused_computation.7 | convolution fusion | flops 6450839552 | bytes 34603008 | tf_op jit(solution)/shard_map/ab,bmn->amn/dot_general | solution.py:66
  586.0 121.1 %all-to-all-done.2 = f32[2,16,16,32,128]{4,3,2,0,1:T(8,128)} async-done(((f32[2,16,16,32,128]{4,3,2,0,1:T(8,128)}), f32[2,16,16,32,128]{4,3,2,0,1:T(8,128)}, u32[]{:S(2)}, u32[]{:S(2)}) %all-to-all-start.2) | async-done | bytes 8388640 | tf_op jit(solution)/shard_map/all_to_all | solution.py:103
  707.2 8.4 %copy.43 = f32[2,16,16,32,128]{4,3,2,1,0:T(8,128)} copy(f32[2,16,16,32,128]{4,3,2,0,1:T(8,128)} %all-to-all-done.2) | data formatting | bytes 16777216 | tf_op jit(solution)/shard_map/all_to_all | solution.py:103
  715.5 14.0 %copy_add_fusion = f32[2,256,32,128]{3,1,2,0:T(8,128)} fusion(f32[2,256,32,128]{3,1,2,0:T(8,128)} %fusion.1, f32[2,256,32,128]{3,2,1,0:T(8,128)} %bitcast.273), kind=kLoop, calls=%fused_computation.10 | loop fusion | flops 2097152 | bytes 25165824 | tf_op jit(solution)/shard_map/add | solution.py:121
  729.5 11.6 %copy.45 = f32[2,256,32,128]{3,2,1,0:T(8,128)} copy(f32[2,256,32,128]{3,1,2,0:T(8,128)} %copy_add_fusion) | data formatting | bytes 16777216 | tf_op jit(solution)/shard_map/add | solution.py:121
  (122 shorter events, 101.7 us)
Async XLA Ops:
  8.3 6.7 copy-start.4
  8.3 189.0 %all-to-all-start = ((f32[2,16,16,32,128]{4,3,2,0,1:T(8,128)}), f32[2,16,16,32,128]{4,3,2,0,1:T(8,128)}, u32[]{:S(2)}, u32[]{:S(2)}) async-start(f32[2,16,16,32,128]{4,3,2,0,1:T(8,128)} %copy.31), calls=%async_computation | async-start | bytes 16777216 | tf_op jit(solution)/shard_map/all_to_all | solution.py:85
  38.9 164.6 %copy-start.22 = (s32[256]{0:T(256)S(1)}, s32[256]{0:T(256)}, u32[]{:S(2)}) copy-start(s32[256]{0:T(256)} %param.10) | copy-start | bytes 3076
  38.9 164.6 %copy-start.23 = (f32[32]{0:T(128)S(1)}, f32[32]{0:T(128)}, u32[]{:S(2)}) copy-start(f32[32]{0:T(128)} %param.11) | copy-start | bytes 388
  38.9 164.8 %copy-start.20 = (s32[4096]{0:T(1024)S(1)}, s32[4096]{0:T(1024)}, u32[]{:S(2)}) copy-start(s32[4096]{0:T(1024)} %param.13) | copy-start | bytes 49156
  38.9 164.8 %copy-start.21 = (s32[4096]{0:T(1024)S(1)}, s32[4096]{0:T(1024)}, u32[]{:S(2)}) copy-start(s32[4096]{0:T(1024)} %param.12) | copy-start | bytes 49156
  197.3 187.6 %all-to-all-start.1 = ((f32[2,16,16,32,128]{4,3,2,0,1:T(8,128)}), f32[2,16,16,32,128]{4,3,2,0,1:T(8,128)}, u32[]{:S(2)}, u32[]{:S(2)}) async-start(f32[2,16,16,32,128]{4,3,2,0,1:T(8,128)} %copy.34), calls=%async_computation.1 | async-start | bytes 16777216 | tf_op jit(solution)/shard_map/all_to_all | solution.py:85
  215.4 19.9 %copy-start = (f32[2,16,256,256]{3,2,1,0:T(8,128)}, f32[2,16,256,256]{3,2,1,0:T(8,128)S(1)}, u32[]{:S(2)}) copy-start(f32[2,16,256,256]{3,2,1,0:T(8,128)S(1)} %maximum_dynamic-update-slice_fusion) | copy-start | bytes 25165828
  384.9 7.6 %copy-start.1 = (f32[2,16,256,256]{3,2,1,0:T(8,128)S(1)}, f32[2,16,256,256]{3,2,1,0:T(8,128)}, u32[]{:S(2)}) copy-start(f32[2,16,256,256]{3,2,1,0:T(8,128)} %copy-done) | copy-start | bytes 25165828
  392.5 9.6 %copy-start.5 = (f32[16,256,256]{2,1,0:T(8,128)S(1)}, f32[16,256,256]{2,1,0:T(8,128)}, u32[]{:S(2)}) copy-start(f32[16,256,256]{2,1,0:T(8,128)} %fusion.15) | copy-start | bytes 12582916
  392.5 9.6 %copy-start.6 = (f32[16,256,256]{1,2,0:T(8,128)S(1)}, f32[16,256,256]{1,2,0:T(8,128)}, u32[]{:S(2)}) copy-start(f32[16,256,256]{1,2,0:T(8,128)} %fusion.16) | copy-start | bytes 12582916
  392.5 9.6 %copy-start.7 = (f32[16,256,256]{2,1,0:T(8,128)S(1)}, f32[16,256,256]{2,1,0:T(8,128)}, u32[]{:S(2)}) copy-start(f32[16,256,256]{2,1,0:T(8,128)} %fusion.19) | copy-start | bytes 12582916
  402.1 6.4 copy-start.15
  402.1 6.4 copy-start.16
  402.2 7.5 %copy-start.13 = (f32[2,16,32,128]{3,2,1,0:T(8,128)S(1)}, f32[2,16,32,128]{3,2,1,0:T(8,128)}, u32[]{:S(2)}) copy-start(f32[2,16,32,128]{3,2,1,0:T(8,128)} %get-tuple-element.43) | copy-start | bytes 1572868
  402.2 7.5 %copy-start.14 = (f32[2,16,32,128]{3,2,1,0:T(8,128)S(1)}, f32[2,16,32,128]{3,2,1,0:T(8,128)}, u32[]{:S(2)}) copy-start(f32[2,16,32,128]{3,2,1,0:T(8,128)} %get-tuple-element.44) | copy-start | bytes 1572868
  402.2 8.6 %copy-start.12 = (f32[2,16,32,128]{3,2,1,0:T(8,128)S(1)}, f32[2,16,32,128]{3,2,1,0:T(8,128)}, u32[]{:S(2)}) copy-start(f32[2,16,32,128]{3,2,1,0:T(8,128)} %get-tuple-element.42) | copy-start | bytes 1572868
  452.5 7.9 %slice-start.2 = ((s8[8388608]{0:T(1024)(128)(4,1)}), s8[4194304]{0:T(1024)(128)(4,1)S(1)}, s32[]{:S(2)}) async-start(s8[8388608]{0:T(1024)(128)(4,1)} %bitcast.270), calls=%async_computation.5 | async-start | bytes 8388608
  464.9 9.6 %copy-start.8 = (f32[16,256,256]{2,1,0:T(8,128)S(1)}, f32[16,256,256]{2,1,0:T(8,128)}, u32[]{:S(2)}) copy-start(f32[16,256,256]{2,1,0:T(8,128)} %fusion.23) | copy-start | bytes 12582916
  464.9 9.6 %copy-start.9 = (f32[16,256,256]{1,2,0:T(8,128)S(1)}, f32[16,256,256]{1,2,0:T(8,128)}, u32[]{:S(2)}) copy-start(f32[16,256,256]{1,2,0:T(8,128)} %fusion.24) | copy-start | bytes 12582916
  464.9 9.6 %copy-start.10 = (f32[16,256,256]{2,1,0:T(8,128)S(1)}, f32[16,256,256]{2,1,0:T(8,128)}, u32[]{:S(2)}) copy-start(f32[16,256,256]{2,1,0:T(8,128)} %fusion.27) | copy-start | bytes 12582916
  519.6 187.5 %all-to-all-start.2 = ((f32[2,16,16,32,128]{4,3,2,0,1:T(8,128)}), f32[2,16,16,32,128]{4,3,2,0,1:T(8,128)}, u32[]{:S(2)}, u32[]{:S(2)}) async-start(f32[2,16,16,32,128]{4,3,2,0,1:T(8,128)} %copy-done.11), calls=%async_computation.2 | async-start | bytes 16777216 | tf_op jit(solution)/shard_map/all_to_all | solution.py:103
  552.2 6.8 slice-start
  552.2 6.8 slice-start.1
  (7 other events, 32.9 us)

commit v8 on v7

--- a/solution.py
+++ b/solution.py
@@ -110,9 +110,9 @@
         p = left_mul(g)
         p_k = to_k(p)
         q = apply_ij(g_k) + lad_kb * g_k
+        pre = apply_ij(q + src_k)
         e = p_k + q + src_k
-        w = e + p_k
-        part_k = neg_i(q, dt) - dt2 * (apply_ij(w) + lad_kb * e)
+        part_k = neg_i(q, dt) - dt2 * (apply_ij(p_k + p_k) + pre + lad_kb * e)
         ys, g2, p2 = lax.optimization_barrier((send_k(part_k), g, p))
         part_k_a = recv_k(ys)
         e2 = p2 + lad_a * g2 + src_a

time: 751 us -> 758 us (level)
  waiting for transfers between devices: 425 us -> 380 us
  matrix products: 122 us -> 159 us
  starting transfers between devices: 17.4 us -> 27.1 us
    all_to_all x2, waiting for transfers between devices: 304 us -> 259 us  [to_k(): got = lax.all_to_all(xs, ('row', 'col'), 1, 1, tiled=True)]
    dot_general x8 -> x12, matrix products: 45.6 us -> 68.5 us  [li(): return jnp.einsum('ia,kaj->kij', hm, xm, precision=matmul_precision)]
    dot_general x8 -> x12, matrix products: 33.7 us -> 47.2 us  [lj(): return jnp.einsum('kia,ja->kij', xm, hm, precision=matmul_precision)]
    all_to_all x2, starting transfers between devices: 12.1 us -> 22.1 us  [to_k(): got = lax.all_to_all(xs, ('row', 'col'), 1, 1, tiled=True)]
    add x1 -> x2, other arithmetic: 19.5 us -> 20.7 us  [the longest x1 10.5 us: on_device(): part_k = neg_i(q, dt) - dt2 * (apply_ij(p_k + p_k) + pre + lad_kb * e)]
    unnamed x71 -> x73, local copies, waits for them, and re-layouts: 23.8 us -> 23.2 us
  transfers between devices with their start and end apart: 3 -> 3, of which waited for: 3 -> 3; matrix products, arithmetic and copies ran while one was open for 16% -> 22% of each run, Pallas kernels for 0% -> 0%
where the time goes in v8:
time: 758 us; the launch traced here: 749 us
  waiting for transfers between devices  380 us (50%)
  matrix products  159 us (21%)
  other arithmetic  101 us (13%)
  local copies, waits for them, and re-layouts  80.6 us (11%)
  starting transfers between devices  27.1 us (4%)
    all_to_all x2, waiting for transfers between devices, to_k(): got = lax.all_to_all(xs, ('row', 'col'), 1, 1, tiled=True)  259 us
    all_to_all x1, waiting for transfers between devices, recv_k(): got = lax.all_to_all(ys, ('row', 'col'), 1, 1, tiled=True)  121 us
    dot_general x12, matrix products, li(): return jnp.einsum('ia,kaj->kij', hm, xm, precision=matmul_precision)  68.5 us
    dot_general x12, matrix products, lj(): return jnp.einsum('kia,ja->kij', xm, hm, precision=matmul_precision)  47.2 us
    dot_general x2, matrix products, left_mul(): out = jnp.einsum('ab,bmn->amn', h_big, flat, precision=matmul_precision)  39.6 us
    unnamed x73, local copies, waits for them, and re-layouts  23.2 us
    all_to_all x2, starting transfers between devices, to_k(): got = lax.all_to_all(xs, ('row', 'col'), 1, 1, tiled=True)  22.1 us
    sub x1, other arithmetic, on_device(): part_k = neg_i(q, dt) - dt2 * (apply_ij(p_k + p_k) + pre + lad_kb * e)  22 us
  transfers between devices with their start and end apart: 3, of which 3 were waited for; matrix products, arithmetic and copies ran while one was open for 22% of the time, Pallas kernels for 0%

profile of v8, /device:TPU:13, one launch (start us, length us, event | category | flops | bytes accessed | tf_op | source)
XLA Modules:
  0.0 748.5 jit_solution(17009245693703980661)
XLA Ops:
  0.0 8.2 %copy.31 = f32[2,16,16,32,128]{4,3,2,0,1:T(8,128)} copy(f32[2,16,16,32,128]{4,3,2,1,0:T(8,128)} %bitcast.314) | data formatting | bytes 16777216 | tf_op jit(solution)/shard_map/reshape | solution.py:84
  8.2 6.7 all-to-all-start
  15.0 12.6 %fusion.6 = f32[512,32,128]{2,0,1:T(8,128)S(1)} fusion(f32[512,32,128]{2,1,0:T(8,128)} %bitcast.315, f32[256,256]{1,0:T(8,128)S(1)} %get-tuple-element.56, f32[256,256]{1,0:T(8,128)S(1)} %get-tuple-element.55, f32[256,256]{1,0:T(8,128)S(1)} %fusion.121), kind=kOutput, calls=%fused_computation.13 | convolution fusion | flops 6443237376 | bytes 17563648 | tf_op jit(solution)/shard_map/ab,bmn->amn/dot_general | solution.py:66
  31.0 8.1 %copy.34 = f32[2,16,16,32,128]{4,3,2,0,1:T(8,128)} copy(f32[2,16,16,32,128]{4,2,1,0,3:T(8,128)S(1)} %bitcast.318) | data formatting | bytes 16777216 | tf_op jit(solution)/shard_map/reshape;reshape | solution.py:84
  39.2 158.1 %all-to-all-done = f32[2,16,16,32,128]{4,3,2,0,1:T(8,128)} async-done(((f32[2,16,16,32,128]{4,3,2,0,1:T(8,128)}), f32[2,16,16,32,128]{4,3,2,0,1:T(8,128)}, u32[]{:S(2)}, u32[]{:S(2)}) %all-to-all-start) | async-done | bytes 8388640 | tf_op jit(solution)/shard_map/all_to_all | solution.py:85
  197.3 15.4 %all-to-all-start.1 = ((f32[2,16,16,32,128]{4,3,2,0,1:T(8,128)}), f32[2,16,16,32,128]{4,3,2,0,1:T(8,128)}, u32[]{:S(2)}, u32[]{:S(2)}) async-start(f32[2,16,16,32,128]{4,3,2,0,1:T(8,128)} %copy.34), calls=%async_computation.1 | async-start | bytes 16777216 | tf_op jit(solution)/shard_map/all_to_all | solution.py:85
  243.6 9.3 %fusion.20 = f32[1,16,256,256]{3,2,1,0:T(8,128)} fusion(f32[16,256,256]{2,1,0:T(8,128)} %fusion.27, f32[16,256,256]{2,1,0:T(8,128)} %fusion.23, f32[16,256,256]{1,2,0:T(8,128)} %fusion.24, f32[2,16,256,256]{3,2,1,0:T(8,128)S(1)} %maximum_dynamic-update-slice_fusion, f32[2,256,256]{2,1,0:T(8,128)S(1)} %copy-done.2), kind=kOutput, calls=%fused_computation.45 | convolution fusion | flops 1613758464 | bytes 21233664 | tf_op jit(solution)/shard_map/ia,kaj->kij/dot_general | solution.py:74
  258.0 10.3 %fusion.8 = (f32[2,16,256,256]{3,2,1,0:T(8,128)}, f32[2,16,256,256]{3,2,1,0:T(8,128)}) fusion(f32[1,16,256,256]{3,2,1,0:T(8,128)} %get-tuple-element.62, f32[1,16,256,256]{3,2,1,0:T(8,128)S(1)} %get-tuple-element.61, f32[2,16,256,256]{3,2,1,0:T(8,128)S(1)} %maximum_dynamic-update-slice_fusion, f32[256,256]{1,0:T(8,128)S(1)} %compare_select_fusion, ...), kind=kLoop, calls=%fused_computation.17 | loop fusion | flops 10485760 | bytes 42205184 | tf_op jit(solution)/shard_map/add | solution.py:113
  268.2 6.2 fusion.39
  294.0 100.9 %all-to-all-done.1 = f32[2,16,16,32,128]{4,3,2,0,1:T(8,128)} async-done(((f32[2,16,16,32,128]{4,3,2,0,1:T(8,128)}), f32[2,16,16,32,128]{4,3,2,0,1:T(8,128)}, u32[]{:S(2)}, u32[]{:S(2)}) %all-to-all-start.1) | async-done | bytes 8388640 | tf_op jit(solution)/shard_map/all_to_all | solution.py:85
  407.7 10.5 %add.124 = f32[2,16,256,256]{3,2,1,0:T(8,128)} add(f32[2,16,256,256]{3,2,1,0:T(8,128)} %maximum_dynamic-update-slice_fusion.8, f32[2,16,256,256]{3,2,1,0:T(8,128)} %maximum_dynamic-update-slice_fusion.8) | non-fusion elementwise | flops 2097152 | bytes 25165824 | tf_op jit(solution)/shard_map/add | solution.py:115
  444.2 8.0 %slice_multiply_fusion.3 = (f32[1,16,256,256]{3,2,1,0:T(8,128)}, f32[1,16,256,256]{3,2,1,0:T(8,128)}) fusion(f32[2,16,256,256]{3,2,1,0:T(8,128)} %get-tuple-element.12), kind=kLoop, calls=%fused_computation.25 | loop fusion | flops 2097152 | bytes 16777216 | tf_op jit(solution)/shard_map/mul | solution.py:11
  452.3 9.5 %fusion.12 = f32[1,16,256,256]{3,2,1,0:T(8,128)} fusion(f32[16,256,256]{2,1,0:T(8,128)} %fusion.43, f32[16,256,256]{2,1,0:T(8,128)} %fusion.39, f32[16,256,256]{1,2,0:T(8,128)} %fusion.40, f32[2,16,256,256]{3,2,1,0:T(8,128)S(1)} %bitcast.313, f32[2,256,256]{2,1,0:T(8,128)S(1)} %copy-done.2), kind=kOutput, calls=%fused_computation.33 | convolution fusion | flops 1613758464 | bytes 21233664 | tf_op jit(solution)/shard_map/ia,kaj->kij/dot_general | solution.py:74
  461.8 7.2 fusion.10
  469.0 9.5 %fusion.16 = f32[1,16,256,256]{3,2,1,0:T(8,128)} fusion(f32[16,256,256]{2,1,0:T(8,128)} %fusion.35, f32[16,256,256]{2,1,0:T(8,128)} %fusion.31, f32[16,256,256]{1,2,0:T(8,128)} %fusion.32, f32[2,16,256,256]{3,2,1,0:T(8,128)S(1)} %copy-done.1, f32[2,256,256]{2,1,0:T(8,128)S(1)} %copy-done.2), kind=kOutput, calls=%fused_computation.39 | convolution fusion | flops 1613758464 | bytes 21233664 | tf_op jit(solution)/shard_map/ia,kaj->kij/dot_general | solution.py:74
  484.0 22.0 %maximum_subtract_fusion = f32[2,16,256,256]{3,2,1,0:T(8,128)} fusion(f32[1,16,256,256]{3,2,1,0:T(8,128)} %get-tuple-element.34, f32[1,16,256,256]{3,2,1,0:T(8,128)} %get-tuple-element.33, f32[1,16,256,256]{3,2,1,0:T(8,128)} %fusion.14, f32[1,16,256,256]{3,2,1,0:T(8,128)} %fusion.16, f32[1,16,256,256]{3,2,1,0:T(8,128)} %fusion.10, ...), kind=kLoop, calls=%fused_computation.1 | loop fusion | flops 23068672 | bytes 58982400 | tf_op jit(solution)/shard_map/sub | solution.py:115
  539.3 11.6 %add_add_fusion = (f32[2,256,32,128]{3,1,2,0:T(8,128)S(1)}, f32[2,256,32,128]{3,1,2,0:T(8,128)}) fusion(f32[2,256,32,128]{3,2,1,0:T(8,128)} %param.7, f32[2,256,32,128]{3,1,0,2:T(8,128)} %bitcast.319, f32[1,256,32,128]{3,1,2,0:T(8,128)} %get-tuple-element.60, f32[1,256,32,128]{3,1,2,0:T(8,128)S(1)} %get-tuple-element.59, f32[32,128]{1,0:T(8,128)S(1)} %compare_select_fusion.1), kind=kLoop, calls=%fused_computation.15 | loop fusion | flops 10485760 | bytes 41959424 | tf_op jit(solution)/shard_map/add | solution.py:118
  550.9 8.3 %copy.41 = f32[2,256,32,128]{3,2,1,0:T(8,128)} copy(f32[2,256,32,128]{3,1,2,0:T(8,128)S(1)} %get-tuple-element.13) | data formatting | bytes 16777216 | tf_op jit(solution)/shard_map/add | solution.py:118
  559.1 6.8 slice_multiply_fusion.1
  565.9 27.1 %fusion.2 = f32[2,256,32,128]{3,1,2,0:T(8,128)} fusion(f32[1,256,32,128]{3,1,2,0:T(8,128)} %get-tuple-element.16, f32[1,256,32,128]{3,1,2,0:T(8,128)S(1)} %get-tuple-element.15, f32[2,256,32,128]{3,2,1,0:T(8,128)S(1)} %bitcast.317, f32[2,256,512,1]{2,1,3,0:T(8,128)S(1)} %bitcast.322, f32[512,32,128]{2,1,0:T(8,128)} %bitcast.320), kind=kOutput, calls=%fused_computation.8 | convolution fusion | flops 6450839552 | bytes 34603008 | tf_op jit(solution)/shard_map/ab,bmn->amn/dot_general | solution.py:66
  593.0 121.3 %all-to-all-done.2 = f32[2,16,16,32,128]{4,3,2,0,1:T(8,128)} async-done(((f32[2,16,16,32,128]{4,3,2,0,1:T(8,128)}), f32[2,16,16,32,128]{4,3,2,0,1:T(8,128)}, u32[]{:S(2)}, u32[]{:S(2)}) %all-to-all-start.2) | async-done | bytes 8388640 | tf_op jit(solution)/shard_map/all_to_all | solution.py:103
  714.3 8.4 %copy.43 = f32[2,16,16,32,128]{4,3,2,1,0:T(8,128)} copy(f32[2,16,16,32,128]{4,3,2,0,1:T(8,128)} %all-to-all-done.2) | data formatting | bytes 16777216 | tf_op jit(solution)/shard_map/all_to_all | solution.py:103
  722.7 14.0 %copy_add_fusion = f32[2,256,32,128]{3,1,2,0:T(8,128)} fusion(f32[2,256,32,128]{3,1,2,0:T(8,128)} %fusion.2, f32[2,256,32,128]{3,2,1,0:T(8,128)} %bitcast.321), kind=kLoop, calls=%fused_computation.11 | loop fusion | flops 2097152 | bytes 25165824 | tf_op jit(solution)/shard_map/add | solution.py:121
  736.7 11.6 %copy.45 = f32[2,256,32,128]{3,2,1,0:T(8,128)} copy(f32[2,256,32,128]{3,1,2,0:T(8,128)} %copy_add_fusion) | data formatting | bytes 16777216 | tf_op jit(solution)/shard_map/add | solution.py:121
  (133 shorter events, 136.3 us)
Async XLA Ops:
  8.2 6.7 copy-start.2
  8.2 189.0 %all-to-all-start = ((f32[2,16,16,32,128]{4,3,2,0,1:T(8,128)}), f32[2,16,16,32,128]{4,3,2,0,1:T(8,128)}, u32[]{:S(2)}, u32[]{:S(2)}) async-start(f32[2,16,16,32,128]{4,3,2,0,1:T(8,128)} %copy.31), calls=%async_computation | async-start | bytes 16777216 | tf_op jit(solution)/shard_map/all_to_all | solution.py:85
  14.9 12.6 %copy-start.11 = (f32[256,256]{1,0:T(8,128)}, f32[256,256]{1,0:T(8,128)S(1)}, u32[]{:S(2)}) copy-start(f32[256,256]{1,0:T(8,128)S(1)} %fusion.121) | copy-start | bytes 786436
  15.0 12.6 %copy-start.13 = (f32[256,256]{1,0:T(8,128)}, f32[256,256]{1,0:T(8,128)S(1)}, u32[]{:S(2)}) copy-start(f32[256,256]{1,0:T(8,128)S(1)} %get-tuple-element.55) | copy-start | bytes 786436
  15.0 12.6 %copy-start.15 = (f32[256,256]{1,0:T(8,128)}, f32[256,256]{1,0:T(8,128)S(1)}, u32[]{:S(2)}) copy-start(f32[256,256]{1,0:T(8,128)S(1)} %get-tuple-element.56) | copy-start | bytes 786436
  39.1 174.3 %copy-start.22 = (s32[256]{0:T(256)S(1)}, s32[256]{0:T(256)}, u32[]{:S(2)}) copy-start(s32[256]{0:T(256)} %param.10) | copy-start | bytes 3076
  39.1 174.3 %copy-start.24 = (f32[32]{0:T(128)S(1)}, f32[32]{0:T(128)}, u32[]{:S(2)}) copy-start(f32[32]{0:T(128)} %param.11) | copy-start | bytes 388
  39.2 174.5 %copy-start.18 = (s32[4096]{0:T(1024)S(1)}, s32[4096]{0:T(1024)}, u32[]{:S(2)}) copy-start(s32[4096]{0:T(1024)} %param.13) | copy-start | bytes 49156
  39.2 174.5 %copy-start.20 = (s32[4096]{0:T(1024)S(1)}, s32[4096]{0:T(1024)}, u32[]{:S(2)}) copy-start(s32[4096]{0:T(1024)} %param.12) | copy-start | bytes 49156
  197.3 197.6 %all-to-all-start.1 = ((f32[2,16,16,32,128]{4,3,2,0,1:T(8,128)}), f32[2,16,16,32,128]{4,3,2,0,1:T(8,128)}, u32[]{:S(2)}, u32[]{:S(2)}) async-start(f32[2,16,16,32,128]{4,3,2,0,1:T(8,128)} %copy.34), calls=%async_computation.1 | async-start | bytes 16777216 | tf_op jit(solution)/shard_map/all_to_all | solution.py:85
  219.3 38.7 %copy-start.4 = (f32[1,16,256,256]{3,2,1,0:T(8,128)}, f32[1,16,256,256]{3,2,1,0:T(8,128)S(1)}, u32[]{:S(2)}) copy-start(f32[1,16,256,256]{3,2,1,0:T(8,128)S(1)} %get-tuple-element.61) | copy-start | bytes 12582916
  268.2 6.2 copy-start
  418.2 6.2 copy-start.1
  440.4 11.8 %slice-start = ((s8[8388608]{0:T(1024)(128)(4,1)}), s8[4194304]{0:T(1024)(128)(4,1)S(1)}, s32[]{:S(2)}) async-start(s8[8388608]{0:T(1024)(128)(4,1)} %bitcast.312), calls=%async_computation.3 | async-start | bytes 8388608
  444.2 8.0 %slice-start.1 = ((s8[8388608]{0:T(1024)(128)(4,1)}), s8[4194304]{0:T(1024)(128)(4,1)S(1)}, s32[]{:S(2)}) async-start(s8[8388608]{0:T(1024)(128)(4,1)} %bitcast.312), calls=%async_computation.4 | async-start | bytes 8388608
  452.3 9.5 %copy-start.5 = (f32[16,256,256]{2,1,0:T(8,128)S(1)}, f32[16,256,256]{2,1,0:T(8,128)}, u32[]{:S(2)}) copy-start(f32[16,256,256]{2,1,0:T(8,128)} %fusion.37) | copy-start | bytes 12582916
  452.3 9.5 %copy-start.6 = (f32[16,256,256]{1,2,0:T(8,128)S(1)}, f32[16,256,256]{1,2,0:T(8,128)}, u32[]{:S(2)}) copy-start(f32[16,256,256]{1,2,0:T(8,128)} %fusion.38) | copy-start | bytes 12582916
  469.0 9.5 %copy-start.7 = (f32[16,256,256]{2,1,0:T(8,128)S(1)}, f32[16,256,256]{2,1,0:T(8,128)}, u32[]{:S(2)}) copy-start(f32[16,256,256]{2,1,0:T(8,128)} %fusion.29) | copy-start | bytes 12582916
  469.0 9.5 %copy-start.8 = (f32[16,256,256]{1,2,0:T(8,128)S(1)}, f32[16,256,256]{1,2,0:T(8,128)}, u32[]{:S(2)}) copy-start(f32[16,256,256]{1,2,0:T(8,128)} %fusion.30) | copy-start | bytes 12582916
  469.0 9.5 %copy-start.9 = (f32[16,256,256]{2,1,0:T(8,128)S(1)}, f32[16,256,256]{2,1,0:T(8,128)}, u32[]{:S(2)}) copy-start(f32[16,256,256]{2,1,0:T(8,128)} %fusion.33) | copy-start | bytes 12582916
  526.9 5.7 copy-start.19
  526.9 187.4 %all-to-all-start.2 = ((f32[2,16,16,32,128]{4,3,2,0,1:T(8,128)}), f32[2,16,16,32,128]{4,3,2,0,1:T(8,128)}, u32[]{:S(2)}, u32[]{:S(2)}) async-start(f32[2,16,16,32,128]{4,3,2,0,1:T(8,128)} %copy-done.10), calls=%async_computation.2 | async-start | bytes 16777216 | tf_op jit(solution)/shard_map/all_to_all | solution.py:103
  559.1 6.8 slice-start.2
  559.1 6.8 slice-start.3
  (8 other events, 39.6 us)

commit v9 on v7

--- a/solution.py
+++ b/solution.py
@@ -2,6 +2,7 @@
 import jax.numpy as jnp
 from jax import lax
 from jax.sharding import PartitionSpec as P
+from jax.experimental.layout import Layout, with_layout_constraint
 
 time_step = 0.1
 matmul_precision = lax.Precision.HIGH
@@ -117,7 +118,7 @@
         part_k_a = recv_k(ys)
         e2 = p2 + lad_a * g2 + src_a
         part_a = g2 + neg_i(p2 + src_a, dt) - dt2 * left_mul(e2)
-        part_a = lax.optimization_barrier(part_a)
+        part_a = lax.optimization_barrier(with_layout_constraint(part_a, Layout((0, 1, 2, 3))))
         return part_a + part_k_a
 
     return on_device

time: 751 us -> 736 us (0.980)
  matrix products: 122 us -> 112 us
  other arithmetic: 94.7 us -> 104 us
  local copies, waits for them, and re-layouts: 81 us -> 72.7 us
    add x2 -> x0, local copies, waits for them, and re-layouts: 19.9 us -> none  [the longest x1 11.6 us: on_device(): return part_a + part_k_a]
    sub x0 -> x1, other arithmetic: none -> 12.6 us  [on_device(): part_a = g2 + neg_i(p2 + src_a, dt) - dt2 * left_mul(e2)]
    all_to_all x2, waiting for transfers between devices: 304 us -> 292 us  [to_k(): got = lax.all_to_all(xs, ('row', 'col'), 1, 1, tiled=True)]
    dot_general x0 -> x1, local copies, waits for them, and re-layouts: none -> 11.5 us  [left_mul(): out = jnp.einsum('ab,bmn->amn', h_big, flat, precision=matmul_precision)]
    dot_general x2, matrix products: 39.3 us -> 29 us  [left_mul(): out = jnp.einsum('ab,bmn->amn', h_big, flat, precision=matmul_precision)]
  transfers between devices with their start and end apart: 3 -> 3, of which waited for: 3 -> 3; matrix products, arithmetic and copies ran while one was open for 16% -> 17% of each run, Pallas kernels for 0% -> 0%
where the time goes in v9:
time: 736 us; the launch traced here: 727 us
  waiting for transfers between devices  420 us (57%)
  matrix products  112 us (15%)
  other arithmetic  104 us (14%)
  local copies, waits for them, and re-layouts  72.7 us (10%)
  starting transfers between devices  17.6 us (2%)
    all_to_all x2, waiting for transfers between devices, to_k(): got = lax.all_to_all(xs, ('row', 'col'), 1, 1, tiled=True)  292 us
    all_to_all x1, waiting for transfers between devices, recv_k(): got = lax.all_to_all(ys, ('row', 'col'), 1, 1, tiled=True)  127 us
    dot_general x8, matrix products, li(): return jnp.einsum('ia,kaj->kij', hm, xm, precision=matmul_precision)  45.9 us
    dot_general x8, matrix products, lj(): return jnp.einsum('kia,ja->kij', xm, hm, precision=matmul_precision)  33.8 us
    dot_general x2, matrix products, left_mul(): out = jnp.einsum('ab,bmn->amn', h_big, flat, precision=matmul_precision)  29 us
    unnamed x71, local copies, waits for them, and re-layouts  23.9 us
    add x1, other arithmetic, on_device(): w = e + p_k  19.7 us
    sub x1, other arithmetic, on_device(): part_k = neg_i(q, dt) - dt2 * (apply_ij(w) + lad_kb * e)  19.1 us
  transfers between devices with their start and end apart: 3, of which 3 were waited for; matrix products, arithmetic and copies ran while one was open for 17% of the time, Pallas kernels for 0%

profile of v9, /device:TPU:13, one launch (start us, length us, event | category | flops | bytes accessed | tf_op | source)
XLA Modules:
  0.0 727.1 jit_solution(8856661316238084825)
XLA Ops:
  0.0 8.3 %copy.21 = f32[2,16,16,32,128]{4,3,2,0,1:T(8,128)} copy(f32[2,16,16,32,128]{4,3,2,1,0:T(8,128)} %bitcast.262) | data formatting | bytes 16777216 | tf_op jit(solution)/shard_map/reshape | solution.py:85
  8.3 6.7 all-to-all-start
  15.0 12.3 %fusion.5 = f32[512,32,128]{2,0,1:T(8,128)S(1)} fusion(f32[512,32,128]{2,1,0:T(8,128)} %bitcast.263, f32[256,256]{1,0:T(8,128)S(1)} %get-tuple-element.60, f32[256,256]{1,0:T(8,128)S(1)} %get-tuple-element.59, f32[256,256]{1,0:T(8,128)S(1)} %fusion.91), kind=kOutput, calls=%fused_computation.12 | convolution fusion | flops 6443237376 | bytes 17563648 | tf_op jit(solution)/shard_map/ab,bmn->amn/dot_general | solution.py:67
  30.8 8.1 %copy.24 = f32[2,16,16,32,128]{4,3,2,0,1:T(8,128)} copy(f32[2,16,16,32,128]{4,2,1,0,3:T(8,128)S(1)} %bitcast.266) | data formatting | bytes 16777216 | tf_op jit(solution)/shard_map/reshape;reshape | solution.py:85
  38.9 158.4 %all-to-all-done = f32[2,16,16,32,128]{4,3,2,0,1:T(8,128)} async-done(((f32[2,16,16,32,128]{4,3,2,0,1:T(8,128)}), f32[2,16,16,32,128]{4,3,2,0,1:T(8,128)}, u32[]{:S(2)}, u32[]{:S(2)}) %all-to-all-start) | async-done | bytes 8388640 | tf_op jit(solution)/shard_map/all_to_all | solution.py:86
  197.3 5.5 all-to-all-start.1
  202.9 11.5 %copy.25 = f32[512,32,128]{2,1,0:T(8,128)} copy(f32[512,32,128]{2,0,1:T(8,128)} %copy-done.3) | data formatting | bytes 16777216 | tf_op jit(solution)/shard_map/ab,bmn->amn/dot_general | solution.py:67
  251.3 133.7 %all-to-all-done.1 = f32[2,16,16,32,128]{4,3,2,0,1:T(8,128)} async-done(((f32[2,16,16,32,128]{4,3,2,0,1:T(8,128)}), f32[2,16,16,32,128]{4,3,2,0,1:T(8,128)}, u32[]{:S(2)}, u32[]{:S(2)}) %all-to-all-start.1) | async-done | bytes 8388640 | tf_op jit(solution)/shard_map/all_to_all | solution.py:86
  385.0 5.9 slice_bitcast_fusion.45
  392.6 9.6 %fusion.15 = f32[1,16,256,256]{3,2,1,0:T(8,128)} fusion(f32[16,256,256]{2,1,0:T(8,128)} %fusion.22, f32[16,256,256]{2,1,0:T(8,128)} %fusion.18, f32[16,256,256]{1,2,0:T(8,128)} %fusion.19, f32[2,16,256,256]{3,2,1,0:T(8,128)S(1)} %copy-done.1, f32[2,256,256]{2,1,0:T(8,128)S(1)} %copy-done.4), kind=kOutput, calls=%fused_computation.35 | convolution fusion | flops 1613758464 | bytes 21233664 | tf_op jit(solution)/shard_map/ia,kaj->kij/dot_general | solution.py:75
  402.2 5.3 fusion.13
  414.8 19.7 %fusion.35 = (f32[2,16,256,256]{3,2,1,0:T(8,128)}, f32[2,16,256,256]{3,2,1,0:T(8,128)}) fusion(f32[2,16,256,256]{3,2,1,0:T(8,128)} %maximum_dynamic-update-slice_fusion.8, f32[1,16,256,256]{3,2,1,0:T(8,128)} %get-tuple-element.62, f32[1,16,256,256]{3,2,1,0:T(8,128)} %get-tuple-element.61, f32[2,16,256,256]{3,2,1,0:T(8,128)} %copy-done, ...), kind=kLoop, calls=%fused_computation.61 | loop fusion | flops 14680064 | bytes 50593792 | tf_op jit(solution)/shard_map/add | solution.py:115
  434.5 6.2 fusion.26
  464.5 9.6 %fusion.11 = f32[1,16,256,256]{3,2,1,0:T(8,128)} fusion(f32[16,256,256]{2,1,0:T(8,128)} %fusion.30, f32[16,256,256]{2,1,0:T(8,128)} %fusion.26, f32[16,256,256]{1,2,0:T(8,128)} %fusion.27, f32[2,16,256,256]{3,2,1,0:T(8,128)S(1)} %copy-done.2, f32[2,256,256]{2,1,0:T(8,128)S(1)} %copy-done.4), kind=kOutput, calls=%fused_computation.29 | convolution fusion | flops 1613758464 | bytes 21233664 | tf_op jit(solution)/shard_map/ia,kaj->kij/dot_general | solution.py:75
  474.1 5.3 fusion.9
  479.4 19.1 %maximum_subtract_fusion = f32[2,16,256,256]{3,2,1,0:T(8,128)} fusion(f32[1,16,256,256]{3,2,1,0:T(8,128)} %get-tuple-element.18, f32[1,16,256,256]{3,2,1,0:T(8,128)} %get-tuple-element.17, f32[1,16,256,256]{3,2,1,0:T(8,128)} %fusion.9, f32[1,16,256,256]{3,2,1,0:T(8,128)} %fusion.11, f32[256,256]{1,0:T(8,128)S(1)} %compare_select_fusion, ...), kind=kLoop, calls=%fused_computation.1 | loop fusion | flops 18874368 | bytes 50593792 | tf_op jit(solution)/shard_map/sub | solution.py:116
  519.4 5.4 all-to-all-start.2
  532.0 11.6 %add_add_fusion = (f32[2,256,32,128]{3,2,1,0:T(8,128)S(1)}, f32[2,256,32,128]{3,2,1,0:T(8,128)}) fusion(f32[2,256,32,128]{3,2,1,0:T(8,128)} %bitcast.269, f32[2,256,32,128]{3,2,1,0:T(8,128)} %param.7, f32[1,256,32,128]{3,2,1,0:T(8,128)} %get-tuple-element.52, f32[1,256,32,128]{3,2,1,0:T(8,128)S(1)} %get-tuple-element.51, f32[32,128]{1,0:T(8,128)S(1)} %compare_select_fusion.1), kind=kLoop, calls=%fused_computation.14 | loop fusion | flops 10485760 | bytes 41959424 | tf_op jit(solution)/shard_map/add | solution.py:119
  543.7 6.7 slice_multiply_fusion.1
  550.4 16.6 %fusion.2 = f32[2,256,32,128]{3,1,2,0:T(8,128)} fusion(f32[2,256,512,1]{2,1,3,0:T(8,128)S(1)} %bitcast.272, f32[512,32,128]{2,1,0:T(8,128)S(1)} %bitcast.270), kind=kOutput, calls=%fused_computation.8 | convolution fusion | flops 6442450944 | bytes 17825792 | tf_op jit(solution)/shard_map/ab,bmn->amn/dot_general | solution.py:67
  567.0 12.6 %fusion.1 = f32[2,256,32,128]{3,2,1,0:T(8,128)} fusion(f32[2,256,32,128]{3,2,1,0:T(8,128)S(1)} %bitcast.265, f32[1,256,32,128]{3,2,1,0:T(8,128)} %get-tuple-element.16, f32[1,256,32,128]{3,2,1,0:T(8,128)S(1)} %get-tuple-element.15, f32[2,256,32,128]{3,1,2,0:T(8,128)} %fusion.2), kind=kLoop, calls=%fused_computation.7 | loop fusion | flops 8388608 | bytes 33554432 | tf_op jit(solution)/shard_map/sub | solution.py:120
  579.6 127.4 %all-to-all-done.2 = f32[2,16,16,32,128]{4,3,2,0,1:T(8,128)} async-done(((f32[2,16,16,32,128]{4,3,2,0,1:T(8,128)}), f32[2,16,16,32,128]{4,3,2,0,1:T(8,128)}, u32[]{:S(2)}, u32[]{:S(2)}) %all-to-all-start.2) | async-done | bytes 8388640 | tf_op jit(solution)/shard_map/all_to_all | solution.py:104
  707.0 8.4 %copy.28 = f32[2,16,16,32,128]{4,3,2,1,0:T(8,128)} copy(f32[2,16,16,32,128]{4,3,2,0,1:T(8,128)} %all-to-all-done.2) | data formatting | bytes 16777216 | tf_op jit(solution)/shard_map/all_to_all | solution.py:104
  715.4 11.3 %add.122 = f32[2,256,32,128]{3,2,1,0:T(8,128)} add(f32[2,256,32,128]{3,2,1,0:T(8,128)} %fusion.1, f32[2,256,32,128]{3,2,1,0:T(8,128)} %bitcast.271) | non-fusion elementwise | flops 2097152 | bytes 25165824 | tf_op jit(solution)/shard_map/add | solution.py:122
  (120 shorter events, 101.1 us)
Async XLA Ops:
  8.3 6.7 copy-start.4
  8.3 189.0 %all-to-all-start = ((f32[2,16,16,32,128]{4,3,2,0,1:T(8,128)}), f32[2,16,16,32,128]{4,3,2,0,1:T(8,128)}, u32[]{:S(2)}, u32[]{:S(2)}) async-start(f32[2,16,16,32,128]{4,3,2,0,1:T(8,128)} %copy.21), calls=%async_computation | async-start | bytes 16777216 | tf_op jit(solution)/shard_map/all_to_all | solution.py:86
  197.3 187.7 %all-to-all-start.1 = ((f32[2,16,16,32,128]{4,3,2,0,1:T(8,128)}), f32[2,16,16,32,128]{4,3,2,0,1:T(8,128)}, u32[]{:S(2)}, u32[]{:S(2)}) async-start(f32[2,16,16,32,128]{4,3,2,0,1:T(8,128)} %copy.24), calls=%async_computation.1 | async-start | bytes 16777216 | tf_op jit(solution)/shard_map/all_to_all | solution.py:86
  202.8 12.3 %copy-start.22 = (s32[256]{0:T(256)S(1)}, s32[256]{0:T(256)}, u32[]{:S(2)}) copy-start(s32[256]{0:T(256)} %param.10) | copy-start | bytes 3076
  202.8 12.3 %copy-start.23 = (f32[32]{0:T(128)S(1)}, f32[32]{0:T(128)}, u32[]{:S(2)}) copy-start(f32[32]{0:T(128)} %param.11) | copy-start | bytes 388
  202.9 12.5 %copy-start.20 = (s32[4096]{0:T(1024)S(1)}, s32[4096]{0:T(1024)}, u32[]{:S(2)}) copy-start(s32[4096]{0:T(1024)} %param.13) | copy-start | bytes 49156
  202.9 12.5 %copy-start.21 = (s32[4096]{0:T(1024)S(1)}, s32[4096]{0:T(1024)}, u32[]{:S(2)}) copy-start(s32[4096]{0:T(1024)} %param.12) | copy-start | bytes 49156
  227.2 20.0 %copy-start = (f32[2,16,256,256]{3,2,1,0:T(8,128)}, f32[2,16,256,256]{3,2,1,0:T(8,128)S(1)}, u32[]{:S(2)}) copy-start(f32[2,16,256,256]{3,2,1,0:T(8,128)S(1)} %maximum_dynamic-update-slice_fusion) | copy-start | bytes 25165828
  385.0 7.6 %copy-start.1 = (f32[2,16,256,256]{3,2,1,0:T(8,128)S(1)}, f32[2,16,256,256]{3,2,1,0:T(8,128)}, u32[]{:S(2)}) copy-start(f32[2,16,256,256]{3,2,1,0:T(8,128)} %copy-done) | copy-start | bytes 25165828
  392.6 9.6 %copy-start.5 = (f32[16,256,256]{2,1,0:T(8,128)S(1)}, f32[16,256,256]{2,1,0:T(8,128)}, u32[]{:S(2)}) copy-start(f32[16,256,256]{2,1,0:T(8,128)} %fusion.16) | copy-start | bytes 12582916
  392.6 9.6 %copy-start.6 = (f32[16,256,256]{1,2,0:T(8,128)S(1)}, f32[16,256,256]{1,2,0:T(8,128)}, u32[]{:S(2)}) copy-start(f32[16,256,256]{1,2,0:T(8,128)} %fusion.17) | copy-start | bytes 12582916
  392.6 9.6 %copy-start.7 = (f32[16,256,256]{2,1,0:T(8,128)S(1)}, f32[16,256,256]{2,1,0:T(8,128)}, u32[]{:S(2)}) copy-start(f32[16,256,256]{2,1,0:T(8,128)} %fusion.20) | copy-start | bytes 12582916
  402.2 6.4 copy-start.15
  402.2 6.4 copy-start.16
  402.2 7.4 %copy-start.13 = (f32[2,16,32,128]{3,2,1,0:T(8,128)S(1)}, f32[2,16,32,128]{3,2,1,0:T(8,128)}, u32[]{:S(2)}) copy-start(f32[2,16,32,128]{3,2,1,0:T(8,128)} %get-tuple-element.43) | copy-start | bytes 1572868
  402.2 7.4 %copy-start.14 = (f32[2,16,32,128]{3,2,1,0:T(8,128)S(1)}, f32[2,16,32,128]{3,2,1,0:T(8,128)}, u32[]{:S(2)}) copy-start(f32[2,16,32,128]{3,2,1,0:T(8,128)} %get-tuple-element.44) | copy-start | bytes 1572868
  402.2 8.4 %copy-start.12 = (f32[2,16,32,128]{3,2,1,0:T(8,128)S(1)}, f32[2,16,32,128]{3,2,1,0:T(8,128)}, u32[]{:S(2)}) copy-start(f32[2,16,32,128]{3,2,1,0:T(8,128)} %get-tuple-element.42) | copy-start | bytes 1572868
  452.4 7.9 %slice-start.2 = ((s8[8388608]{0:T(1024)(128)(4,1)}), s8[4194304]{0:T(1024)(128)(4,1)S(1)}, s32[]{:S(2)}) async-start(s8[8388608]{0:T(1024)(128)(4,1)} %bitcast.267), calls=%async_computation.5 | async-start | bytes 8388608
  464.5 9.6 %copy-start.8 = (f32[16,256,256]{2,1,0:T(8,128)S(1)}, f32[16,256,256]{2,1,0:T(8,128)}, u32[]{:S(2)}) copy-start(f32[16,256,256]{2,1,0:T(8,128)} %fusion.24) | copy-start | bytes 12582916
  464.5 9.6 %copy-start.9 = (f32[16,256,256]{1,2,0:T(8,128)S(1)}, f32[16,256,256]{1,2,0:T(8,128)}, u32[]{:S(2)}) copy-start(f32[16,256,256]{1,2,0:T(8,128)} %fusion.25) | copy-start | bytes 12582916
  464.5 9.6 %copy-start.10 = (f32[16,256,256]{2,1,0:T(8,128)S(1)}, f32[16,256,256]{2,1,0:T(8,128)}, u32[]{:S(2)}) copy-start(f32[16,256,256]{2,1,0:T(8,128)} %fusion.28) | copy-start | bytes 12582916
  519.4 187.6 %all-to-all-start.2 = ((f32[2,16,16,32,128]{4,3,2,0,1:T(8,128)}), f32[2,16,16,32,128]{4,3,2,0,1:T(8,128)}, u32[]{:S(2)}, u32[]{:S(2)}) async-start(f32[2,16,16,32,128]{4,3,2,0,1:T(8,128)} %copy-done.11), calls=%async_computation.2 | async-start | bytes 16777216 | tf_op jit(solution)/shard_map/all_to_all | solution.py:104
  543.7 23.4 %slice-start = ((s8[8388608]{0:T(1024)(128)(4,1)}), s8[4194304]{0:T(1024)(128)(4,1)S(1)}, s32[]{:S(2)}) async-start(s8[8388608]{0:T(1024)(128)(4,1)} %bitcast.264), calls=%async_computation.3 | async-start | bytes 8388608
  550.4 16.6 %slice-start.1 = ((s8[8388608]{0:T(1024)(128)(4,1)}), s8[4194304]{0:T(1024)(128)(4,1)S(1)}, s32[]{:S(2)}) async-start(s8[8388608]{0:T(1024)(128)(4,1)} %bitcast.264), calls=%async_computation.4 | async-start | bytes 8388608
  (7 other events, 33.0 us)

commit v10 on v9

--- a/solution.py
+++ b/solution.py
@@ -113,8 +113,17 @@
         q = apply_ij(g_k) + lad_kb * g_k
         e = p_k + q + src_k
         w = e + p_k
-        part_k = neg_i(q, dt) - dt2 * (apply_ij(w) + lad_kb * e)
-        ys, g2, p2 = lax.optimization_barrier((send_k(part_k), g, p))
+        aw = apply_ij(w)
+
+        def blk(x, a, b):
+            return x[..., a * nrows:(a + 1) * nrows, b * ncols:(b + 1) * ncols]
+
+        blocks = [
+            neg_i(blk(q, a, b), dt) - dt2 * (blk(aw, a, b) + blk(lad_kb, a, b) * blk(e, a, b))
+            for a in range(nrow)
+            for b in range(ncol)
+        ]
+        ys, g2, p2 = lax.optimization_barrier((jnp.stack(blocks, axis=1), g, p))
         part_k_a = recv_k(ys)
         e2 = p2 + lad_a * g2 + src_a
         part_a = g2 + neg_i(p2 + src_a, dt) - dt2 * left_mul(e2)

time: 736 us -> 715 us (0.971)
  local copies, waits for them, and re-layouts: 72.7 us -> 55.7 us
    sub x1 -> x0, other arithmetic: 19.1 us -> none  [on_device(): part_k = neg_i(q, dt) - dt2 * (apply_ij(w) + lad_kb * e)]
    unnamed x16 -> x31, other arithmetic: 7.8 us -> 26.5 us
    unnamed x71 -> x112, local copies, waits for them, and re-layouts: 23.9 us -> 7.35 us
  transfers between devices with their start and end apart: 3 -> 3, of which waited for: 3 -> 3; matrix products, arithmetic and copies ran while one was open for 17% -> 18% of each run, Pallas kernels for 0% -> 0%
where the time goes in v10:
time: 715 us; the launch traced here: 706 us
  waiting for transfers between devices  418 us (58%)
  matrix products  108 us (15%)
  other arithmetic  105 us (15%)
  local copies, waits for them, and re-layouts  55.7 us (8%)
  starting transfers between devices  17.6 us (2%)
    all_to_all x2, waiting for transfers between devices, to_k(): got = lax.all_to_all(xs, ('row', 'col'), 1, 1, tiled=True)  291 us
    all_to_all x1, waiting for transfers between devices, recv_k(): got = lax.all_to_all(ys, ('row', 'col'), 1, 1, tiled=True)  127 us
    dot_general x8, matrix products, li(): return jnp.einsum('ia,kaj->kij', hm, xm, precision=matmul_precision)  42.7 us
    dot_general x8, matrix products, lj(): return jnp.einsum('kia,ja->kij', xm, hm, precision=matmul_precision)  32.1 us
    dot_general x2, matrix products, left_mul(): out = jnp.einsum('ab,bmn->amn', h_big, flat, precision=matmul_precision)  29.2 us
    unnamed x31, other arithmetic  26.5 us
    add x1, other arithmetic, on_device(): w = e + p_k  20.6 us
  transfers between devices with their start and end apart: 3, of which 3 were waited for; matrix products, arithmetic and copies ran while one was open for 18% of the time, Pallas kernels for 0%

profile of v10, /device:TPU:13, one launch (start us, length us, event | category | flops | bytes accessed | tf_op | source)
XLA Modules:
  0.0 705.8 jit_solution(6336057990040252589)
XLA Ops:
  0.0 8.3 %copy.21 = f32[2,16,16,32,128]{4,3,2,0,1:T(8,128)} copy(f32[2,16,16,32,128]{4,3,2,1,0:T(8,128)} %bitcast.294) | data formatting | bytes 16777216 | tf_op jit(solution)/shard_map/reshape | solution.py:85
  8.3 6.7 all-to-all-start
  15.1 12.6 %fusion.4 = f32[512,32,128]{2,0,1:T(8,128)S(1)} fusion(f32[512,32,128]{2,1,0:T(8,128)} %bitcast.295, f32[256,256]{1,0:T(8,128)S(1)} %get-tuple-element.91, f32[256,256]{1,0:T(8,128)S(1)} %get-tuple-element.90, f32[256,256]{1,0:T(8,128)S(1)} %fusion.138), kind=kOutput, calls=%fused_computation.39 | convolution fusion | flops 6443237376 | bytes 17563648 | tf_op jit(solution)/shard_map/ab,bmn->amn/dot_general | solution.py:67
  31.1 8.1 %copy.24 = f32[2,16,16,32,128]{4,3,2,0,1:T(8,128)} copy(f32[2,16,16,32,128]{4,2,1,0,3:T(8,128)S(1)} %bitcast.298) | data formatting | bytes 16777216 | tf_op jit(solution)/shard_map/reshape;reshape | solution.py:85
  39.2 158.1 %all-to-all-done = f32[2,16,16,32,128]{4,3,2,0,1:T(8,128)} async-done(((f32[2,16,16,32,128]{4,3,2,0,1:T(8,128)}), f32[2,16,16,32,128]{4,3,2,0,1:T(8,128)}, u32[]{:S(2)}, u32[]{:S(2)}) %all-to-all-start) | async-done | bytes 8388640 | tf_op jit(solution)/shard_map/all_to_all | solution.py:86
  197.4 5.5 all-to-all-start.1
  202.9 11.6 %copy.25 = f32[512,32,128]{2,1,0:T(8,128)} copy(f32[512,32,128]{2,0,1:T(8,128)} %copy-done.3) | data formatting | bytes 16777216 | tf_op jit(solution)/shard_map/ab,bmn->amn/dot_general | solution.py:67
  223.0 4.4 slice_bitcast_fusion.45
  228.1 4.4 fusion.17
  252.3 132.8 %all-to-all-done.1 = f32[2,16,16,32,128]{4,3,2,0,1:T(8,128)} async-done(((f32[2,16,16,32,128]{4,3,2,0,1:T(8,128)}), f32[2,16,16,32,128]{4,3,2,0,1:T(8,128)}, u32[]{:S(2)}, u32[]{:S(2)}) %all-to-all-start.1) | async-done | bytes 8388640 | tf_op jit(solution)/shard_map/all_to_all | solution.py:86
  385.1 5.8 slice_bitcast_fusion.29
  391.9 9.5 %fusion.14 = f32[1,16,256,256]{3,2,1,0:T(8,128)} fusion(f32[16,256,256]{2,1,0:T(8,128)} %fusion.21, f32[16,256,256]{2,1,0:T(8,128)} %fusion.17, f32[16,256,256]{1,2,0:T(8,128)} %fusion.18, f32[2,16,256,256]{3,2,1,0:T(8,128)S(1)} %copy-done.1, f32[2,256,256]{2,1,0:T(8,128)S(1)} %copy-done.4), kind=kOutput, calls=%fused_computation.60 | convolution fusion | flops 1613758464 | bytes 21233664 | tf_op jit(solution)/shard_map/ia,kaj->kij/dot_general | solution.py:75
  401.5 5.4 fusion.12
  414.2 20.6 %fusion.139 = (f32[2,16,256,256]{3,2,1,0:T(8,128)}, f32[2,16,256,256]{3,2,1,0:T(8,128)}, f32[2,16,256,256]{3,2,1,0:T(8,128)}) fusion(f32[2,16,256,256]{3,2,1,0:T(8,128)} %maximum_dynamic-update-slice_fusion.8, f32[1,16,256,256]{3,2,1,0:T(8,128)} %get-tuple-element.93, f32[1,16,256,256]{3,2,1,0:T(8,128)} %get-tuple-element.92, ...), kind=kLoop, calls=%fused_computation.330 | loop fusion | flops 14680064 | bytes 58982400 | tf_op jit(solution)/shard_map/add | solution.py:115
  462.6 6.5 fusion.10
  469.1 5.2 fusion.8
  498.1 5.4 all-to-all-start.2
  510.8 11.6 %add_add_fusion = (f32[2,256,32,128]{3,2,1,0:T(8,128)S(1)}, f32[2,256,32,128]{3,2,1,0:T(8,128)}) fusion(f32[2,256,32,128]{3,2,1,0:T(8,128)} %bitcast.299, f32[2,256,32,128]{3,2,1,0:T(8,128)} %param.7, f32[1,256,32,128]{3,2,1,0:T(8,128)} %get-tuple-element.83, f32[1,256,32,128]{3,2,1,0:T(8,128)S(1)} %get-tuple-element.82, f32[32,128]{1,0:T(8,128)S(1)} %compare_select_fusion.2), kind=kLoop, calls=%fused_computation.41 | loop fusion | flops 10485760 | bytes 41959424 | tf_op jit(solution)/shard_map/add | solution.py:128
  522.4 6.8 slice_multiply_fusion.1
  529.2 16.6 %fusion.1 = f32[2,256,32,128]{3,1,2,0:T(8,128)} fusion(f32[2,256,512,1]{2,1,3,0:T(8,128)S(1)} %bitcast.304, f32[512,32,128]{2,1,0:T(8,128)S(1)} %bitcast.302), kind=kOutput, calls=%fused_computation.35 | convolution fusion | flops 6442450944 | bytes 17825792 | tf_op jit(solution)/shard_map/ab,bmn->amn/dot_general | solution.py:67
  545.9 12.6 %fusion = f32[2,256,32,128]{3,2,1,0:T(8,128)} fusion(f32[2,256,32,128]{3,2,1,0:T(8,128)S(1)} %bitcast.297, f32[1,256,32,128]{3,2,1,0:T(8,128)} %get-tuple-element.17, f32[1,256,32,128]{3,2,1,0:T(8,128)S(1)} %get-tuple-element.16, f32[2,256,32,128]{3,1,2,0:T(8,128)} %fusion.1), kind=kLoop, calls=%fused_computation.34 | loop fusion | flops 8388608 | bytes 33554432 | tf_op jit(solution)/shard_map/sub | solution.py:129
  558.5 127.2 %all-to-all-done.2 = f32[2,16,16,32,128]{4,3,2,0,1:T(8,128)} async-done(((f32[2,16,16,32,128]{4,3,2,0,1:T(8,128)}), f32[2,16,16,32,128]{4,3,2,0,1:T(8,128)}, u32[]{:S(2)}, u32[]{:S(2)}) %all-to-all-start.2) | async-done | bytes 8388640 | tf_op jit(solution)/shard_map/all_to_all | solution.py:104
  685.7 8.4 %copy.28 = f32[2,16,16,32,128]{4,3,2,1,0:T(8,128)} copy(f32[2,16,16,32,128]{4,3,2,0,1:T(8,128)} %all-to-all-done.2) | data formatting | bytes 16777216 | tf_op jit(solution)/shard_map/all_to_all | solution.py:104
  694.1 11.3 %add.182 = f32[2,256,32,128]{3,2,1,0:T(8,128)} add(f32[2,256,32,128]{3,2,1,0:T(8,128)} %fusion, f32[2,256,32,128]{3,2,1,0:T(8,128)} %bitcast.303) | non-fusion elementwise | flops 2097152 | bytes 25165824 | tf_op jit(solution)/shard_map/add | solution.py:131
  (178 shorter events, 99.0 us)
Async XLA Ops:
  8.3 6.7 copy-start.4
  8.3 189.0 %all-to-all-start = ((f32[2,16,16,32,128]{4,3,2,0,1:T(8,128)}), f32[2,16,16,32,128]{4,3,2,0,1:T(8,128)}, u32[]{:S(2)}, u32[]{:S(2)}) async-start(f32[2,16,16,32,128]{4,3,2,0,1:T(8,128)} %copy.21), calls=%async_computation | async-start | bytes 16777216 | tf_op jit(solution)/shard_map/all_to_all | solution.py:86
  15.0 12.6 %copy-start.11 = (f32[256,256]{1,0:T(8,128)}, f32[256,256]{1,0:T(8,128)S(1)}, u32[]{:S(2)}) copy-start(f32[256,256]{1,0:T(8,128)S(1)} %fusion.138) | copy-start | bytes 786436
  15.1 12.6 %copy-start.13 = (f32[256,256]{1,0:T(8,128)}, f32[256,256]{1,0:T(8,128)S(1)}, u32[]{:S(2)}) copy-start(f32[256,256]{1,0:T(8,128)S(1)} %get-tuple-element.90) | copy-start | bytes 786436
  15.1 12.6 %copy-start.15 = (f32[256,256]{1,0:T(8,128)}, f32[256,256]{1,0:T(8,128)S(1)}, u32[]{:S(2)}) copy-start(f32[256,256]{1,0:T(8,128)S(1)} %get-tuple-element.91) | copy-start | bytes 786436
  197.4 187.7 %all-to-all-start.1 = ((f32[2,16,16,32,128]{4,3,2,0,1:T(8,128)}), f32[2,16,16,32,128]{4,3,2,0,1:T(8,128)}, u32[]{:S(2)}, u32[]{:S(2)}) async-start(f32[2,16,16,32,128]{4,3,2,0,1:T(8,128)} %copy.24), calls=%async_computation.1 | async-start | bytes 16777216 | tf_op jit(solution)/shard_map/all_to_all | solution.py:86
  202.9 12.4 %copy-start.43 = (s32[256]{0:T(256)S(1)}, s32[256]{0:T(256)}, u32[]{:S(2)}) copy-start(s32[256]{0:T(256)} %param.10) | copy-start | bytes 3076
  202.9 12.4 %copy-start.51 = (f32[32]{0:T(128)S(1)}, f32[32]{0:T(128)}, u32[]{:S(2)}) copy-start(f32[32]{0:T(128)} %param.11) | copy-start | bytes 388
  202.9 13.4 %copy-start.45 = (s32[4096]{0:T(1024)S(1)}, s32[4096]{0:T(1024)}, u32[]{:S(2)}) copy-start(s32[4096]{0:T(1024)} %param.13) | copy-start | bytes 49156
  202.9 13.4 %copy-start.47 = (s32[4096]{0:T(1024)S(1)}, s32[4096]{0:T(1024)}, u32[]{:S(2)}) copy-start(s32[4096]{0:T(1024)} %param.12) | copy-start | bytes 49156
  215.4 12.1 %copy-start.49 = (f32[256]{0:T(256)}, f32[256]{0:T(256)S(1)}, u32[]{:S(2)}) copy-start(f32[256]{0:T(256)S(1)} %select_reduce_fusion) | copy-start | bytes 3076
  228.1 20.2 %copy-start = (f32[2,16,256,256]{3,2,1,0:T(8,128)}, f32[2,16,256,256]{3,2,1,0:T(8,128)S(1)}, u32[]{:S(2)}) copy-start(f32[2,16,256,256]{3,2,1,0:T(8,128)S(1)} %maximum_dynamic-update-slice_fusion) | copy-start | bytes 25165828
  385.1 6.8 copy-start.1
  391.9 9.6 %copy-start.7 = (f32[16,256,256]{2,1,0:T(8,128)S(1)}, f32[16,256,256]{2,1,0:T(8,128)}, u32[]{:S(2)}) copy-start(f32[16,256,256]{2,1,0:T(8,128)} %fusion.15) | copy-start | bytes 12582916
  391.9 9.6 %copy-start.8 = (f32[16,256,256]{1,2,0:T(8,128)S(1)}, f32[16,256,256]{1,2,0:T(8,128)}, u32[]{:S(2)}) copy-start(f32[16,256,256]{1,2,0:T(8,128)} %fusion.16) | copy-start | bytes 12582916
  391.9 9.6 %copy-start.9 = (f32[16,256,256]{2,1,0:T(8,128)S(1)}, f32[16,256,256]{2,1,0:T(8,128)}, u32[]{:S(2)}) copy-start(f32[16,256,256]{2,1,0:T(8,128)} %fusion.19) | copy-start | bytes 12582916
  401.5 6.4 copy-start.18
  401.5 7.5 %copy-start.17 = (f32[2,16,32,128]{3,2,1,0:T(8,128)S(1)}, f32[2,16,32,128]{3,2,1,0:T(8,128)}, u32[]{:S(2)}) copy-start(f32[2,16,32,128]{3,2,1,0:T(8,128)} %get-tuple-element.75) | copy-start | bytes 1572868
  451.2 7.9 %slice-start.2 = ((s8[8388608]{0:T(1024)(128)(4,1)}), s8[4194304]{0:T(1024)(128)(4,1)S(1)}, s32[]{:S(2)}) async-start(s8[8388608]{0:T(1024)(128)(4,1)} %bitcast.300), calls=%async_computation.5 | async-start | bytes 8388608
  462.6 6.5 copy-start.5
  462.6 6.5 copy-start.6
  498.1 187.6 %all-to-all-start.2 = ((f32[2,16,16,32,128]{4,3,2,0,1:T(8,128)}), f32[2,16,16,32,128]{4,3,2,0,1:T(8,128)}, u32[]{:S(2)}, u32[]{:S(2)}) async-start(f32[2,16,16,32,128]{4,3,2,0,1:T(8,128)} %copy-done.10), calls=%async_computation.2 | async-start | bytes 16777216 | tf_op jit(solution)/shard_map/all_to_all | solution.py:104
  522.4 23.4 %slice-start = ((s8[8388608]{0:T(1024)(128)(4,1)}), s8[4194304]{0:T(1024)(128)(4,1)S(1)}, s32[]{:S(2)}) async-start(s8[8388608]{0:T(1024)(128)(4,1)} %bitcast.296), calls=%async_computation.3 | async-start | bytes 8388608
  529.2 16.6 %slice-start.1 = ((s8[8388608]{0:T(1024)(128)(4,1)}), s8[4194304]{0:T(1024)(128)(4,1)S(1)}, s32[]{:S(2)}) async-start(s8[8388608]{0:T(1024)(128)(4,1)} %bitcast.296), calls=%async_computation.4 | async-start | bytes 8388608
  (35 other events, 130.9 us)

commit v11 on v10

--- a/solution.py
+++ b/solution.py
@@ -109,10 +109,24 @@
         g = green
         g_k = to_k(g)
         p = left_mul(g)
-        p_k = to_k(p)
+        p_got = lax.all_to_all(p.reshape(2, ndev, kb, nrows, ncols), ("row", "col"), 1, 1, tiled=True)
         q = apply_ij(g_k) + lad_kb * g_k
-        e = p_k + q + src_k
-        w = e + p_k
+
+        def pblk(a, b):
+            return p_got[:, a * ncol + b]
+
+        def sub(x, a, b):
+            return x[..., a * nrows:(a + 1) * nrows, b * ncols:(b + 1) * ncols]
+
+        def e_blk(a, b):
+            return pblk(a, b) + sub(q, a, b) + sub(src_k, a, b)
+
+        def assemble(f):
+            rows = [jnp.concatenate([f(a, b) for b in range(ncol)], axis=-1) for a in range(nrow)]
+            return jnp.concatenate(rows, axis=-2)
+
+        e = assemble(e_blk)
+        w = assemble(lambda a, b: e_blk(a, b) + pblk(a, b))
         aw = apply_ij(w)
 
         def blk(x, a, b):

time: 715 us -> 670 us (0.937)
  other arithmetic: 105 us -> 78.8 us
  matrix products: 108 us -> 96.1 us
  waiting for transfers between devices: 418 us -> 408 us
    all_to_all x2 -> x1, waiting for transfers between devices: 291 us -> 158 us  [to_k(): got = lax.all_to_all(xs, ('row', 'col'), 1, 1, tiled=True)]
    all_to_all x0 -> x1, waiting for transfers between devices: none -> 123 us  [on_device(): lax.all_to_all(p.reshape(2, ndev, kb, nrows, ncols), ('row', 'col'), 1, 1...]
    unnamed x31 -> x30, other arithmetic: 26.5 us -> 4.57 us
    unnamed x112 -> x138, local copies, waits for them, and re-layouts: 7.35 us -> 15.8 us
    add x1 -> x5, other arithmetic: 20.6 us -> 17.5 us  [the longest x4 13.1 us: on_device(): w = assemble(lambda a, b: e_blk(a, b) + pblk(a, b))]
  transfers between devices with their start and end apart: 3 -> 3, of which waited for: 3 -> 3; matrix products, arithmetic and copies ran while one was open for 18% -> 20% of each run, Pallas kernels for 0% -> 0%
where the time goes in v11:
time: 670 us; the launch traced here: 661 us
  waiting for transfers between devices  408 us (61%)
  matrix products  96.1 us (14%)
  other arithmetic  78.8 us (12%)
  local copies, waits for them, and re-layouts  58.6 us (9%)
  starting transfers between devices  17.6 us (3%)
    all_to_all x1, waiting for transfers between devices, to_k(): got = lax.all_to_all(xs, ('row', 'col'), 1, 1, tiled=True)  158 us
    all_to_all x1, waiting for transfers between devices, recv_k(): got = lax.all_to_all(ys, ('row', 'col'), 1, 1, tiled=True)  127 us
    all_to_all x1, waiting for transfers between devices, on_device(): lax.all_to_all(p.reshape(2, ndev, kb, nrows, ncols), ('row', 'col'), 1, 1...  123 us
    dot_general x8, matrix products, li(): return jnp.einsum('ia,kaj->kij', hm, xm, precision=matmul_precision)  37.7 us
    dot_general x2, matrix products, left_mul(): out = jnp.einsum('ab,bmn->amn', h_big, flat, precision=matmul_precision)  29.2 us
    dot_general x8, matrix products, lj(): return jnp.einsum('kia,ja->kij', xm, hm, precision=matmul_precision)  25.5 us
    unnamed x138, local copies, waits for them, and re-layouts  15.8 us
  transfers between devices with their start and end apart: 3, of which 3 were waited for; matrix products, arithmetic and copies ran while one was open for 20% of the time, Pallas kernels for 0%

profile of v11, /device:TPU:13, one launch (start us, length us, event | category | flops | bytes accessed | tf_op | source)
XLA Modules:
  0.0 660.5 jit_solution(6458869900286910789)
XLA Ops:
  0.0 8.3 %copy.21 = f32[2,16,16,32,128]{4,3,2,0,1:T(8,128)} copy(f32[2,16,16,32,128]{4,3,2,1,0:T(8,128)} %bitcast.374) | data formatting | bytes 16777216 | tf_op jit(solution)/shard_map/reshape | solution.py:85
  8.3 6.7 %all-to-all-start = ((f32[2,16,16,32,128]{4,3,2,0,1:T(8,128)}), f32[2,16,16,32,128]{4,3,2,0,1:T(8,128)}, u32[]{:S(2)}, u32[]{:S(2)}) async-start(f32[2,16,16,32,128]{4,3,2,0,1:T(8,128)} %copy.21), calls=%async_computation | async-start | bytes 16777216 | tf_op jit(solution)/shard_map/all_to_all | solution.py:86
  15.1 12.6 %fusion.4 = f32[512,32,128]{2,0,1:T(8,128)S(1)} fusion(f32[512,32,128]{2,1,0:T(8,128)} %bitcast.375, f32[256,256]{1,0:T(8,128)S(1)} %get-tuple-element.128, f32[256,256]{1,0:T(8,128)S(1)} %get-tuple-element.127, f32[256,256]{1,0:T(8,128)S(1)} %fusion.185), kind=kOutput, calls=%fused_computation.68 | convolution fusion | flops 6443237376 | bytes 17563648 | tf_op jit(solution)/shard_map/ab,bmn->amn/dot_general | solution.py:67
  31.1 8.2 %copy.24 = f32[2,16,16,32,128]{4,3,2,0,1:T(8,128)} copy(f32[2,16,16,32,128]{4,2,1,0,3:T(8,128)S(1)} %bitcast.378) | data formatting | bytes 16777216 | tf_op jit(solution)/shard_map/reshape;reshape | solution.py:112
  39.3 158.0 %all-to-all-done = f32[2,16,16,32,128]{4,3,2,0,1:T(8,128)} async-done(((f32[2,16,16,32,128]{4,3,2,0,1:T(8,128)}), f32[2,16,16,32,128]{4,3,2,0,1:T(8,128)}, u32[]{:S(2)}, u32[]{:S(2)}) %all-to-all-start) | async-done | bytes 8388640 | tf_op jit(solution)/shard_map/all_to_all | solution.py:86
  197.4 5.5 all-to-all-start.1
  202.9 11.6 %copy.25 = f32[512,32,128]{2,1,0:T(8,128)} copy(f32[512,32,128]{2,0,1:T(8,128)} %copy-done.2) | data formatting | bytes 16777216 | tf_op jit(solution)/shard_map/ab,bmn->amn/dot_general | solution.py:67
  218.8 4.2 subtract_multiply_fusion.1
  223.1 4.4 slice_bitcast_fusion.45
  246.2 6.4 fusion.14
  252.6 5.2 fusion.12
  257.8 4.4 maximum_add_fusion
  262.2 122.9 %all-to-all-done.1 = f32[2,16,16,32,128]{4,3,2,0,1:T(8,128)} async-done(((f32[2,16,16,32,128]{4,3,2,0,1:T(8,128)}), f32[2,16,16,32,128]{4,3,2,0,1:T(8,128)}, u32[]{:S(2)}, u32[]{:S(2)}) %all-to-all-start.1) | async-done | bytes 8388640 | tf_op jit(solution)/shard_map/all_to_all | solution.py:112
  385.1 5.0 fusion.138
  428.1 6.5 fusion.10
  434.6 5.2 fusion.8
  452.9 5.4 all-to-all-start.2
  465.6 11.6 %add_add_fusion = (f32[2,256,32,128]{3,2,1,0:T(8,128)S(1)}, f32[2,256,32,128]{3,2,1,0:T(8,128)}) fusion(f32[2,256,32,128]{3,2,1,0:T(8,128)} %bitcast.379, f32[2,256,32,128]{3,2,1,0:T(8,128)} %param.7, f32[1,256,32,128]{3,2,1,0:T(8,128)} %get-tuple-element.120, f32[1,256,32,128]{3,2,1,0:T(8,128)S(1)} %get-tuple-element.119, f32[32,128]{1,0:T(8,128)S(1)} %compare_select_fusion.2), kind=kLoop, calls=%fused_computation.70 | loop fusion | flops 10485760 | bytes 41959424 | tf_op jit(solution)/shard_map/add | solution.py:142
  477.2 6.8 %slice_multiply_fusion.1 = (f32[1,256,32,128]{3,2,1,0:T(8,128)S(1)}, f32[1,256,32,128]{3,2,1,0:T(8,128)}) fusion(f32[2,256,32,128]{3,2,1,0:T(8,128)} %get-tuple-element.68), kind=kLoop, calls=%fused_computation.73 | loop fusion | flops 2097152 | bytes 16777216 | tf_op jit(solution)/shard_map/mul | solution.py:12
  484.0 16.6 %fusion.1 = f32[2,256,32,128]{3,1,2,0:T(8,128)} fusion(f32[2,256,512,1]{2,1,3,0:T(8,128)S(1)} %bitcast.382, f32[512,32,128]{2,1,0:T(8,128)S(1)} %bitcast.380), kind=kOutput, calls=%fused_computation.64 | convolution fusion | flops 6442450944 | bytes 17825792 | tf_op jit(solution)/shard_map/ab,bmn->amn/dot_general | solution.py:67
  500.6 12.7 %fusion = f32[2,256,32,128]{3,2,1,0:T(8,128)} fusion(f32[2,256,32,128]{3,2,1,0:T(8,128)S(1)} %bitcast.377, f32[1,256,32,128]{3,2,1,0:T(8,128)} %get-tuple-element.70, f32[1,256,32,128]{3,2,1,0:T(8,128)S(1)} %get-tuple-element.69, f32[2,256,32,128]{3,1,2,0:T(8,128)} %fusion.1), kind=kLoop, calls=%fused_computation.63 | loop fusion | flops 8388608 | bytes 33554432 | tf_op jit(solution)/shard_map/sub | solution.py:143
  513.3 127.2 %all-to-all-done.2 = f32[2,16,16,32,128]{4,3,2,0,1:T(8,128)} async-done(((f32[2,16,16,32,128]{4,3,2,0,1:T(8,128)}), f32[2,16,16,32,128]{4,3,2,0,1:T(8,128)}, u32[]{:S(2)}, u32[]{:S(2)}) %all-to-all-start.2) | async-done | bytes 8388640 | tf_op jit(solution)/shard_map/all_to_all | solution.py:104
  640.5 8.4 %copy.28 = f32[2,16,16,32,128]{4,3,2,1,0:T(8,128)} copy(f32[2,16,16,32,128]{4,3,2,0,1:T(8,128)} %all-to-all-done.2) | data formatting | bytes 16777216 | tf_op jit(solution)/shard_map/all_to_all | solution.py:104
  648.9 11.3 %add.394 = f32[2,256,32,128]{3,2,1,0:T(8,128)} add(f32[2,256,32,128]{3,2,1,0:T(8,128)} %fusion, f32[2,256,32,128]{3,2,1,0:T(8,128)} %bitcast.381) | non-fusion elementwise | flops 2097152 | bytes 25165824 | tf_op jit(solution)/shard_map/add | solution.py:145
  (206 shorter events, 84.0 us)
Async XLA Ops:
  8.3 6.7 %copy-start.4 = (f32[2,256,256]{2,1,0:T(8,128)S(1)}, f32[2,256,256]{2,1,0:T(8,128)}, u32[]{:S(2)}) copy-start(f32[2,256,256]{2,1,0:T(8,128)} %param.8) | copy-start | bytes 1572868
  8.3 189.0 %all-to-all-start = ((f32[2,16,16,32,128]{4,3,2,0,1:T(8,128)}), f32[2,16,16,32,128]{4,3,2,0,1:T(8,128)}, u32[]{:S(2)}, u32[]{:S(2)}) async-start(f32[2,16,16,32,128]{4,3,2,0,1:T(8,128)} %copy.21), calls=%async_computation | async-start | bytes 16777216 | tf_op jit(solution)/shard_map/all_to_all | solution.py:86
  15.1 12.6 %copy-start.8 = (f32[256,256]{1,0:T(8,128)}, f32[256,256]{1,0:T(8,128)S(1)}, u32[]{:S(2)}) copy-start(f32[256,256]{1,0:T(8,128)S(1)} %fusion.185) | copy-start | bytes 786436
  15.1 12.6 %copy-start.10 = (f32[256,256]{1,0:T(8,128)}, f32[256,256]{1,0:T(8,128)S(1)}, u32[]{:S(2)}) copy-start(f32[256,256]{1,0:T(8,128)S(1)} %get-tuple-element.127) | copy-start | bytes 786436
  15.1 12.6 %copy-start.12 = (f32[256,256]{1,0:T(8,128)}, f32[256,256]{1,0:T(8,128)S(1)}, u32[]{:S(2)}) copy-start(f32[256,256]{1,0:T(8,128)S(1)} %get-tuple-element.128) | copy-start | bytes 786436
  197.4 187.7 %all-to-all-start.1 = ((f32[2,16,16,32,128]{4,3,2,0,1:T(8,128)}), f32[2,16,16,32,128]{4,3,2,0,1:T(8,128)}, u32[]{:S(2)}, u32[]{:S(2)}) async-start(f32[2,16,16,32,128]{4,3,2,0,1:T(8,128)} %copy.24), calls=%async_computation.1 | async-start | bytes 16777216 | tf_op jit(solution)/shard_map/all_to_all | solution.py:112
  202.9 12.4 %copy-start.58 = (s32[256]{0:T(256)S(1)}, s32[256]{0:T(256)}, u32[]{:S(2)}) copy-start(s32[256]{0:T(256)} %param.10) | copy-start | bytes 3076
  202.9 12.4 %copy-start.66 = (f32[32]{0:T(128)S(1)}, f32[32]{0:T(128)}, u32[]{:S(2)}) copy-start(f32[32]{0:T(128)} %param.11) | copy-start | bytes 388
  202.9 13.4 %copy-start.60 = (s32[4096]{0:T(1024)S(1)}, s32[4096]{0:T(1024)}, u32[]{:S(2)}) copy-start(s32[4096]{0:T(1024)} %param.13) | copy-start | bytes 49156
  202.9 13.4 %copy-start.62 = (s32[4096]{0:T(1024)S(1)}, s32[4096]{0:T(1024)}, u32[]{:S(2)}) copy-start(s32[4096]{0:T(1024)} %param.12) | copy-start | bytes 49156
  215.4 12.1 %copy-start.64 = (f32[256]{0:T(256)}, f32[256]{0:T(256)S(1)}, u32[]{:S(2)}) copy-start(f32[256]{0:T(256)S(1)} %select_reduce_fusion) | copy-start | bytes 3076
  385.1 6.2 copy-start.1
  385.1 8.5 %copy-start.3 = (f32[2,16,256,256]{3,2,1,0:T(8,128)S(1)}, f32[2,16,256,256]{3,2,1,0:T(8,128)}, u32[]{:S(2)}) copy-start(f32[2,16,256,256]{3,2,1,0:T(8,128)} %maximum_add_fusion) | copy-start | bytes 25165828
  428.1 6.5 copy-start.5
  428.1 6.6 copy-start.6
  452.8 5.7 copy-start.50
  452.8 5.9 copy-start.9
  452.8 5.9 copy-start.11
  452.9 5.9 copy-start.13
  452.9 6.0 copy-start.61
  452.9 6.0 copy-start.63
  452.9 187.6 %all-to-all-start.2 = ((f32[2,16,16,32,128]{4,3,2,0,1:T(8,128)}), f32[2,16,16,32,128]{4,3,2,0,1:T(8,128)}, u32[]{:S(2)}, u32[]{:S(2)}) async-start(f32[2,16,16,32,128]{4,3,2,0,1:T(8,128)} %copy-done.7), calls=%async_computation.2 | async-start | bytes 16777216 | tf_op jit(solution)/shard_map/all_to_all | solution.py:104
  477.2 23.4 %slice-start = ((s8[8388608]{0:T(1024)(128)(4,1)}), s8[4194304]{0:T(1024)(128)(4,1)S(1)}, s32[]{:S(2)}) async-start(s8[8388608]{0:T(1024)(128)(4,1)} %bitcast.376), calls=%async_computation.3 | async-start | bytes 8388608
  484.0 16.6 %slice-start.1 = ((s8[8388608]{0:T(1024)(128)(4,1)}), s8[4194304]{0:T(1024)(128)(4,1)S(1)}, s32[]{:S(2)}) async-start(s8[8388608]{0:T(1024)(128)(4,1)} %bitcast.376), calls=%async_computation.4 | async-start | bytes 8388608
  (48 other events, 79.9 us)

commit v12 on v11

--- a/solution.py
+++ b/solution.py
@@ -100,10 +100,6 @@
                 axis=1,
             )
 
-        def recv_k(ys):
-            got = lax.all_to_all(ys, ("row", "col"), 1, 1, tiled=True)
-            return got.reshape(2, orbs, nrows, ncols)
-
         dt = time_step
         dt2 = 0.5 * time_step * time_step
         g = green
@@ -138,11 +134,13 @@
             for b in range(ncol)
         ]
         ys, g2, p2 = lax.optimization_barrier((jnp.stack(blocks, axis=1), g, p))
-        part_k_a = recv_k(ys)
+        back = lax.all_to_all(ys, ("row", "col"), 1, 1, tiled=True)
         e2 = p2 + lad_a * g2 + src_a
         part_a = g2 + neg_i(p2 + src_a, dt) - dt2 * left_mul(e2)
         part_a = lax.optimization_barrier(with_layout_constraint(part_a, Layout((0, 1, 2, 3))))
-        return part_a + part_k_a
+        return jnp.concatenate(
+            [part_a[:, d * kb:(d + 1) * kb] + back[:, d] for d in range(ndev)], axis=1
+        )
 
     return on_device
 

time: 670 us -> 674 us (level)
  other arithmetic: 78.8 us -> 87.8 us
    unnamed x30 -> x45, other arithmetic: 4.57 us -> 22.8 us
    add x1 -> x0, other arithmetic: 11.3 us -> none  [on_device(): return part_a + part_k_a]
    all_to_all x1 -> x0, local copies, waits for them, and re-layouts: 8.37 us -> none  [recv_k(): got = lax.all_to_all(ys, ('row', 'col'), 1, 1, tiled=True)]
    unnamed x138 -> x142, local copies, waits for them, and re-layouts: 15.8 us -> 19.2 us
where the time goes in v12:
time: 674 us; the launch traced here: 665 us
  waiting for transfers between devices  408 us (61%)
  matrix products  96.2 us (14%)
  other arithmetic  87.8 us (13%)
  local copies, waits for them, and re-layouts  53.5 us (8%)
  starting transfers between devices  17.6 us (3%)
    all_to_all x1, waiting for transfers between devices, to_k(): got = lax.all_to_all(xs, ('row', 'col'), 1, 1, tiled=True)  158 us
    all_to_all x1, waiting for transfers between devices, on_device(): back = lax.all_to_all(ys, ('row', 'col'), 1, 1, tiled=True)  127 us
    all_to_all x1, waiting for transfers between devices, on_device(): lax.all_to_all(p.reshape(2, ndev, kb, nrows, ncols), ('row', 'col'), 1, 1...  123 us
    dot_general x8, matrix products, li(): return jnp.einsum('ia,kaj->kij', hm, xm, precision=matmul_precision)  37.8 us
    dot_general x2, matrix products, left_mul(): out = jnp.einsum('ab,bmn->amn', h_big, flat, precision=matmul_precision)  29.3 us
    dot_general x8, matrix products, lj(): return jnp.einsum('kia,ja->kij', xm, hm, precision=matmul_precision)  25.4 us
    unnamed x45, other arithmetic  22.8 us
    unnamed x142, local copies, waits for them, and re-layouts  19.2 us
  transfers between devices with their start and end apart: 3, of which 3 were waited for; matrix products, arithmetic and copies ran while one was open for 20% of the time, Pallas kernels for 0%

profile of v12, /device:TPU:13, one launch (start us, length us, event | category | flops | bytes accessed | tf_op | source)
XLA Modules:
  0.0 664.6 jit_solution(17207173696100379640)
XLA Ops:
  0.0 8.4 %copy.19 = f32[2,16,16,32,128]{4,3,2,0,1:T(8,128)} copy(f32[2,16,16,32,128]{4,3,2,1,0:T(8,128)} %bitcast.469) | data formatting | bytes 16777216 | tf_op jit(solution)/shard_map/reshape | solution.py:85
  8.4 6.7 %all-to-all-start = ((f32[2,16,16,32,128]{4,3,2,0,1:T(8,128)}), f32[2,16,16,32,128]{4,3,2,0,1:T(8,128)}, u32[]{:S(2)}, u32[]{:S(2)}) async-start(f32[2,16,16,32,128]{4,3,2,0,1:T(8,128)} %copy.19), calls=%async_computation | async-start | bytes 16777216 | tf_op jit(solution)/shard_map/all_to_all | solution.py:86
  15.2 12.6 %fusion.4 = f32[512,32,128]{2,0,1:T(8,128)S(1)} fusion(f32[512,32,128]{2,1,0:T(8,128)} %bitcast.470, f32[256,256]{1,0:T(8,128)S(1)} %get-tuple-element.128, f32[256,256]{1,0:T(8,128)S(1)} %get-tuple-element.127, f32[256,256]{1,0:T(8,128)S(1)} %fusion.217), kind=kOutput, calls=%fused_computation.68 | convolution fusion | flops 6443237376 | bytes 17563648 | tf_op jit(solution)/shard_map/ab,bmn->amn/dot_general | solution.py:67
  31.1 8.1 %copy.22 = f32[2,16,16,32,128]{4,3,2,0,1:T(8,128)} copy(f32[2,16,16,32,128]{4,2,1,0,3:T(8,128)S(1)} %bitcast.473) | data formatting | bytes 16777216 | tf_op jit(solution)/shard_map/reshape;reshape | solution.py:108
  39.2 158.2 %all-to-all-done = f32[2,16,16,32,128]{4,3,2,0,1:T(8,128)} async-done(((f32[2,16,16,32,128]{4,3,2,0,1:T(8,128)}), f32[2,16,16,32,128]{4,3,2,0,1:T(8,128)}, u32[]{:S(2)}, u32[]{:S(2)}) %all-to-all-start) | async-done | bytes 8388640 | tf_op jit(solution)/shard_map/all_to_all | solution.py:86
  197.4 5.5 all-to-all-start.1
  203.0 11.6 %copy.23 = f32[512,32,128]{2,1,0:T(8,128)} copy(f32[512,32,128]{2,0,1:T(8,128)} %copy-done.2) | data formatting | bytes 16777216 | tf_op jit(solution)/shard_map/ab,bmn->amn/dot_general | solution.py:67
  218.9 4.3 subtract_multiply_fusion.1
  223.1 4.4 slice_bitcast_fusion.61
  242.2 4.1 fusion.19
  246.2 6.4 fusion.14
  252.6 5.2 fusion.12
  257.9 4.4 maximum_add_fusion
  262.3 122.9 %all-to-all-done.1 = f32[2,16,16,32,128]{4,3,2,0,1:T(8,128)} async-done(((f32[2,16,16,32,128]{4,3,2,0,1:T(8,128)}), f32[2,16,16,32,128]{4,3,2,0,1:T(8,128)}, u32[]{:S(2)}, u32[]{:S(2)}) %all-to-all-start.1) | async-done | bytes 8388640 | tf_op jit(solution)/shard_map/all_to_all | solution.py:108
  385.1 5.0 fusion.170
  415.9 4.2 fusion.24
  428.1 6.5 fusion.10
  434.6 5.2 fusion.8
  452.9 5.4 all-to-all-start.2
  465.6 11.8 %add_add_fusion = (f32[2,256,32,128]{3,2,1,0:T(8,128)S(1)}, f32[2,256,32,128]{3,2,1,0:T(8,128)}) fusion(f32[2,256,32,128]{3,2,1,0:T(8,128)} %bitcast.474, f32[2,256,32,128]{3,2,1,0:T(8,128)} %param.7, f32[1,256,32,128]{3,2,1,0:T(8,128)} %get-tuple-element.120, f32[1,256,32,128]{3,2,1,0:T(8,128)S(1)} %get-tuple-element.119, f32[32,128]{1,0:T(8,128)S(1)} %compare_select_fusion.2), kind=kLoop, calls=%fused_computation.70 | loop fusion | flops 10485760 | bytes 41959424 | tf_op jit(solution)/shard_map/add | solution.py:138
  477.3 6.8 %slice_multiply_fusion.1 = (f32[1,256,32,128]{3,2,1,0:T(8,128)S(1)}, f32[1,256,32,128]{3,2,1,0:T(8,128)}) fusion(f32[2,256,32,128]{3,2,1,0:T(8,128)} %get-tuple-element.68), kind=kLoop, calls=%fused_computation.73 | loop fusion | flops 2097152 | bytes 16777216 | tf_op jit(solution)/shard_map/mul | solution.py:12
  484.1 16.7 %fusion.1 = f32[2,256,32,128]{3,1,2,0:T(8,128)} fusion(f32[2,256,512,1]{2,1,3,0:T(8,128)S(1)} %bitcast.476, f32[512,32,128]{2,1,0:T(8,128)S(1)} %bitcast.475), kind=kOutput, calls=%fused_computation.64 | convolution fusion | flops 6442450944 | bytes 17825792 | tf_op jit(solution)/shard_map/ab,bmn->amn/dot_general | solution.py:67
  500.9 12.7 %fusion = f32[2,256,32,128]{3,2,1,0:T(8,128)} fusion(f32[2,256,32,128]{3,2,1,0:T(8,128)S(1)} %bitcast.472, f32[1,256,32,128]{3,2,1,0:T(8,128)} %get-tuple-element.70, f32[1,256,32,128]{3,2,1,0:T(8,128)S(1)} %get-tuple-element.69, f32[2,256,32,128]{3,1,2,0:T(8,128)} %fusion.1), kind=kLoop, calls=%fused_computation.63 | loop fusion | flops 8388608 | bytes 33554432 | tf_op jit(solution)/shard_map/sub | solution.py:139
  513.5 127.0 %all-to-all-done.2 = f32[2,16,16,32,128]{4,3,2,0,1:T(8,128)} async-done(((f32[2,16,16,32,128]{4,3,2,0,1:T(8,128)}), f32[2,16,16,32,128]{4,3,2,0,1:T(8,128)}, u32[]{:S(2)}, u32[]{:S(2)}) %all-to-all-start.2) | async-done | bytes 8388640 | tf_op jit(solution)/shard_map/all_to_all | solution.py:137
  (224 shorter events, 99.3 us)
Async XLA Ops:
  8.4 6.7 %copy-start.4 = (f32[2,256,256]{2,1,0:T(8,128)S(1)}, f32[2,256,256]{2,1,0:T(8,128)}, u32[]{:S(2)}) copy-start(f32[2,256,256]{2,1,0:T(8,128)} %param.8) | copy-start | bytes 1572868
  8.4 189.0 %all-to-all-start = ((f32[2,16,16,32,128]{4,3,2,0,1:T(8,128)}), f32[2,16,16,32,128]{4,3,2,0,1:T(8,128)}, u32[]{:S(2)}, u32[]{:S(2)}) async-start(f32[2,16,16,32,128]{4,3,2,0,1:T(8,128)} %copy.19), calls=%async_computation | async-start | bytes 16777216 | tf_op jit(solution)/shard_map/all_to_all | solution.py:86
  15.1 12.6 %copy-start.9 = (f32[256,256]{1,0:T(8,128)}, f32[256,256]{1,0:T(8,128)S(1)}, u32[]{:S(2)}) copy-start(f32[256,256]{1,0:T(8,128)S(1)} %fusion.217) | copy-start | bytes 786436
  15.1 12.6 %copy-start.11 = (f32[256,256]{1,0:T(8,128)}, f32[256,256]{1,0:T(8,128)S(1)}, u32[]{:S(2)}) copy-start(f32[256,256]{1,0:T(8,128)S(1)} %get-tuple-element.127) | copy-start | bytes 786436
  15.2 12.6 %copy-start.13 = (f32[256,256]{1,0:T(8,128)}, f32[256,256]{1,0:T(8,128)S(1)}, u32[]{:S(2)}) copy-start(f32[256,256]{1,0:T(8,128)S(1)} %get-tuple-element.128) | copy-start | bytes 786436
  197.4 187.7 %all-to-all-start.1 = ((f32[2,16,16,32,128]{4,3,2,0,1:T(8,128)}), f32[2,16,16,32,128]{4,3,2,0,1:T(8,128)}, u32[]{:S(2)}, u32[]{:S(2)}) async-start(f32[2,16,16,32,128]{4,3,2,0,1:T(8,128)} %copy.22), calls=%async_computation.1 | async-start | bytes 16777216 | tf_op jit(solution)/shard_map/all_to_all | solution.py:108
  202.9 12.4 %copy-start.60 = (s32[256]{0:T(256)S(1)}, s32[256]{0:T(256)}, u32[]{:S(2)}) copy-start(s32[256]{0:T(256)} %param.10) | copy-start | bytes 3076
  203.0 12.4 %copy-start.68 = (f32[32]{0:T(128)S(1)}, f32[32]{0:T(128)}, u32[]{:S(2)}) copy-start(f32[32]{0:T(128)} %param.11) | copy-start | bytes 388
  203.0 13.4 %copy-start.62 = (s32[4096]{0:T(1024)S(1)}, s32[4096]{0:T(1024)}, u32[]{:S(2)}) copy-start(s32[4096]{0:T(1024)} %param.12) | copy-start | bytes 49156
  203.0 13.4 %copy-start.64 = (s32[4096]{0:T(1024)S(1)}, s32[4096]{0:T(1024)}, u32[]{:S(2)}) copy-start(s32[4096]{0:T(1024)} %param.13) | copy-start | bytes 49156
  215.4 12.2 %copy-start.66 = (f32[256]{0:T(256)}, f32[256]{0:T(256)S(1)}, u32[]{:S(2)}) copy-start(f32[256]{0:T(256)S(1)} %select_reduce_fusion) | copy-start | bytes 3076
  385.1 6.2 copy-start.1
  385.1 8.5 %copy-start.3 = (f32[2,16,256,256]{3,2,1,0:T(8,128)S(1)}, f32[2,16,256,256]{3,2,1,0:T(8,128)}, u32[]{:S(2)}) copy-start(f32[2,16,256,256]{3,2,1,0:T(8,128)} %maximum_add_fusion) | copy-start | bytes 25165828
  428.1 6.5 copy-start.6
  428.1 6.6 copy-start.7
  452.9 5.9 copy-start.10
  452.9 5.9 copy-start.12
  452.9 5.9 copy-start.14
  452.9 6.0 copy-start.63
  452.9 6.0 copy-start.65
  452.9 187.6 %all-to-all-start.2 = ((f32[2,16,16,32,128]{4,3,2,0,1:T(8,128)}), f32[2,16,16,32,128]{4,3,2,0,1:T(8,128)}, u32[]{:S(2)}, u32[]{:S(2)}) async-start(f32[2,16,16,32,128]{4,3,2,0,1:T(8,128)} %copy-done.8), calls=%async_computation.2 | async-start | bytes 16777216 | tf_op jit(solution)/shard_map/all_to_all | solution.py:137
  477.3 23.5 %slice-start = ((s8[8388608]{0:T(1024)(128)(4,1)}), s8[4194304]{0:T(1024)(128)(4,1)S(1)}, s32[]{:S(2)}) async-start(s8[8388608]{0:T(1024)(128)(4,1)} %bitcast.471), calls=%async_computation.3 | async-start | bytes 8388608
  484.1 16.7 %slice-start.1 = ((s8[8388608]{0:T(1024)(128)(4,1)}), s8[4194304]{0:T(1024)(128)(4,1)S(1)}, s32[]{:S(2)}) async-start(s8[8388608]{0:T(1024)(128)(4,1)} %bitcast.471), calls=%async_computation.4 | async-start | bytes 8388608
  640.5 8.2 %copy-start.5 = (f32[2,256,32,128]{3,2,1,0:T(8,128)S(1)}, f32[2,256,32,128]{3,2,1,0:T(8,128)}, u32[]{:S(2)}) copy-start(f32[2,256,32,128]{3,2,1,0:T(8,128)} %fusion) | copy-start | bytes 25165828
  (50 other events, 89.0 us)

commit v13 on v11

--- a/solution.py
+++ b/solution.py
@@ -126,8 +126,9 @@
             return jnp.concatenate(rows, axis=-2)
 
         e = assemble(e_blk)
-        w = assemble(lambda a, b: e_blk(a, b) + pblk(a, b))
-        aw = apply_ij(w)
+        pre = apply_ij(q + src_k)
+        p2k = assemble(lambda a, b: pblk(a, b) + pblk(a, b))
+        aw = apply_ij(p2k) + pre
 
         def blk(x, a, b):
             return x[..., a * nrows:(a + 1) * nrows, b * ncols:(b + 1) * ncols]

time: 670 us -> 711 us (1.061)
  matrix products: 96.1 us -> 158 us
  waiting for transfers between devices: 408 us -> 365 us
  other arithmetic: 78.8 us -> 102 us
    all_to_all x1, waiting for transfers between devices: 123 us -> 79.7 us  [on_device(): lax.all_to_all(p.reshape(2, ndev, kb, nrows, ncols), ('row', 'col'), 1, 1...]
    dot_general x8 -> x12, matrix products: 37.7 us -> 77.8 us  [li(): return jnp.einsum('ia,kaj->kij', hm, xm, precision=matmul_precision)]
    dot_general x8 -> x12, matrix products: 25.5 us -> 47.7 us  [lj(): return jnp.einsum('kia,ja->kij', xm, hm, precision=matmul_precision)]
    unnamed x30 -> x32, other arithmetic: 4.57 us -> 24.2 us
    add x5 -> x3, other arithmetic: 17.5 us -> 22.5 us  [the longest x1 11.1 us: on_device(): pre = apply_ij(q + src_k)]
    unnamed x138 -> x112, local copies, waits for them, and re-layouts: 15.8 us -> 12.4 us
  transfers between devices with their start and end apart: 3 -> 3, of which waited for: 3 -> 3; matrix products, arithmetic and copies ran while one was open for 20% -> 25% of each run, Pallas kernels for 0% -> 0%
where the time goes in v13:
time: 711 us; the launch traced here: 701 us
  waiting for transfers between devices  365 us (51%)
  matrix products  158 us (22%)
  other arithmetic  102 us (14%)
  local copies, waits for them, and re-layouts  57.8 us (8%)
  starting transfers between devices  17 us (2%)
    all_to_all x1, waiting for transfers between devices, to_k(): got = lax.all_to_all(xs, ('row', 'col'), 1, 1, tiled=True)  158 us
    all_to_all x1, waiting for transfers between devices, recv_k(): got = lax.all_to_all(ys, ('row', 'col'), 1, 1, tiled=True)  128 us
    all_to_all x1, waiting for transfers between devices, on_device(): lax.all_to_all(p.reshape(2, ndev, kb, nrows, ncols), ('row', 'col'), 1, 1...  79.7 us
    dot_general x12, matrix products, li(): return jnp.einsum('ia,kaj->kij', hm, xm, precision=matmul_precision)  77.8 us
    dot_general x12, matrix products, lj(): return jnp.einsum('kia,ja->kij', xm, hm, precision=matmul_precision)  47.7 us
    dot_general x2, matrix products, left_mul(): out = jnp.einsum('ab,bmn->amn', h_big, flat, precision=matmul_precision)  29.2 us
    unnamed x32, other arithmetic  24.2 us
  transfers between devices with their start and end apart: 3, of which 3 were waited for; matrix products, arithmetic and copies ran while one was open for 25% of the time, Pallas kernels for 0%

profile of v13, /device:TPU:13, one launch (start us, length us, event | category | flops | bytes accessed | tf_op | source)
XLA Modules:
  0.0 701.2 jit_solution(1177590823909112114)
XLA Ops:
  0.0 8.3 %copy.21 = f32[2,16,16,32,128]{4,3,2,0,1:T(8,128)} copy(f32[2,16,16,32,128]{4,3,2,1,0:T(8,128)} %bitcast.408) | data formatting | bytes 16777216 | tf_op jit(solution)/shard_map/reshape | solution.py:85
  8.3 6.7 all-to-all-start
  15.1 12.6 %fusion.5 = f32[512,32,128]{2,0,1:T(8,128)S(1)} fusion(f32[512,32,128]{2,1,0:T(8,128)} %bitcast.409, f32[256,256]{1,0:T(8,128)S(1)} %get-tuple-element.90, f32[256,256]{1,0:T(8,128)S(1)} %get-tuple-element.89, f32[256,256]{1,0:T(8,128)S(1)} %fusion.214), kind=kOutput, calls=%fused_computation.43 | convolution fusion | flops 6443237376 | bytes 17563648 | tf_op jit(solution)/shard_map/ab,bmn->amn/dot_general | solution.py:67
  31.1 8.1 %copy.24 = f32[2,16,16,32,128]{4,3,2,0,1:T(8,128)} copy(f32[2,16,16,32,128]{4,2,1,0,3:T(8,128)S(1)} %bitcast.412) | data formatting | bytes 16777216 | tf_op jit(solution)/shard_map/reshape;reshape | solution.py:112
  39.2 158.1 %all-to-all-done = f32[2,16,16,32,128]{4,3,2,0,1:T(8,128)} async-done(((f32[2,16,16,32,128]{4,3,2,0,1:T(8,128)}), f32[2,16,16,32,128]{4,3,2,0,1:T(8,128)}, u32[]{:S(2)}, u32[]{:S(2)}) %all-to-all-start) | async-done | bytes 8388640 | tf_op jit(solution)/shard_map/all_to_all | solution.py:86
  202.7 11.6 %copy.25 = f32[512,32,128]{2,1,0:T(8,128)} copy(f32[512,32,128]{2,0,1:T(8,128)} %copy-done.7) | data formatting | bytes 16777216 | tf_op jit(solution)/shard_map/ab,bmn->amn/dot_general | solution.py:67
  220.4 7.3 %slice_bitcast_fusion.59 = (f32[2,16,32,128]{3,2,1,0:T(8,128)S(1)}, f32[2,16,32,128]{3,2,1,0:T(8,128)S(1)}, f32[2,16,32,128]{3,2,1,0:T(8,128)S(1)}, f32[2,16,32,...) fusion(f32[2,16,16,32,128]{4,3,2,0,1:T(8,128)} %all-to-all-done), kind=kLoop, calls=%fused_computation.271 | loop fusion | bytes 16777216 | tf_op jit(solution)/shard_map/squeeze | solution.py:88
  250.6 9.4 %fusion.19 = f32[1,16,256,256]{3,2,1,0:T(8,128)} fusion(f32[16,256,256]{2,1,0:T(8,128)} %fusion.26, f32[16,256,256]{2,1,0:T(8,128)} %fusion.22, f32[16,256,256]{1,2,0:T(8,128)} %fusion.23, f32[2,16,256,256]{3,2,1,0:T(8,128)S(1)} %maximum_dynamic-update-slice_fusion, f32[2,256,256]{2,1,0:T(8,128)S(1)} %copy-done.6), kind=kOutput, calls=%fused_computation.72 | convolution fusion | flops 1613758464 | bytes 21233664 | tf_op jit(solution)/shard_map/ia,kaj->kij/dot_general | solution.py:75
  260.0 8.2 %fusion.17 = f32[1,16,256,256]{3,2,1,0:T(8,128)} fusion(f32[16,256,256]{2,1,0:T(8,128)S(1)} %fusion.20, f32[16,256,256]{2,1,0:T(8,128)} %fusion.24, f32[16,256,256]{1,2,0:T(8,128)} %fusion.21, f32[2,16,256,256]{3,2,1,0:T(8,128)S(1)} %maximum_dynamic-update-slice_fusion, f32[2,256,256]{2,1,0:T(8,128)S(1)} %copy-done.6), kind=kOutput, calls=%fused_computation.69 | convolution fusion | flops 1613758464 | bytes 21233664 | tf_op jit(solution)/shard_map/ia,kaj->kij/dot_general | solution.py:75
  268.3 11.1 %fusion = (f32[2,16,256,256]{3,2,1,0:T(8,128)}, f32[2,16,256,256]{3,2,1,0:T(8,128)}) fusion(f32[1,16,256,256]{3,2,1,0:T(8,128)S(1)} %get-tuple-element.92, f32[1,16,256,256]{3,2,1,0:T(8,128)S(1)} %get-tuple-element.91, f32[2,16,256,256]{3,2,1,0:T(8,128)} %copy-done.4, f32[256,256]{1,0:T(8,128)S(1)} %compare_select_fusion.1, f32[1,16,256,256]{3,2,1,0:T(8,128)} %fusion.17, ...), kind=kLoop, calls=%fused_computation.33 | loop fusion | flops 10485760 | bytes 42205184 | tf_op jit(solution)/shard_map/add | solution.py:129
  279.4 6.2 fusion.38
  305.1 79.7 %all-to-all-done.1 = f32[2,16,16,32,128]{4,3,2,0,1:T(8,128)} async-done(((f32[2,16,16,32,128]{4,3,2,0,1:T(8,128)}), f32[2,16,16,32,128]{4,3,2,0,1:T(8,128)}, u32[]{:S(2)}, u32[]{:S(2)}) %all-to-all-start.1) | async-done | bytes 8388640 | tf_op jit(solution)/shard_map/all_to_all | solution.py:112
  419.2 9.3 %fusion.11 = f32[1,16,256,256]{3,2,1,0:T(8,128)} fusion(f32[16,256,256]{2,1,0:T(8,128)} %fusion.42, f32[16,256,256]{2,1,0:T(8,128)} %fusion.38, f32[16,256,256]{1,2,0:T(8,128)} %fusion.39, f32[2,16,256,256]{3,2,1,0:T(8,128)S(1)} %bitcast.407, f32[2,256,256]{2,1,0:T(8,128)S(1)} %copy-done.6), kind=kOutput, calls=%fused_computation.60 | convolution fusion | flops 1613758464 | bytes 21233664 | tf_op jit(solution)/shard_map/ia,kaj->kij/dot_general | solution.py:75
  428.5 9.4 %fusion.9 = f32[1,16,256,256]{3,2,1,0:T(8,128)} fusion(f32[16,256,256]{2,1,0:T(8,128)} %fusion.36, f32[16,256,256]{2,1,0:T(8,128)} %fusion.40, f32[16,256,256]{1,2,0:T(8,128)} %fusion.37, f32[2,16,256,256]{3,2,1,0:T(8,128)S(1)} %bitcast.407, f32[2,256,256]{2,1,0:T(8,128)S(1)} %copy-done.6), kind=kOutput, calls=%fused_computation.57 | convolution fusion | flops 1613758464 | bytes 21233664 | tf_op jit(solution)/shard_map/ia,kaj->kij/dot_general | solution.py:75
  437.9 9.7 %fusion.15 = f32[1,16,256,256]{3,2,1,0:T(8,128)} fusion(f32[16,256,256]{2,1,0:T(8,128)} %fusion.34, f32[16,256,256]{2,1,0:T(8,128)} %fusion.30, f32[16,256,256]{1,2,0:T(8,128)} %fusion.31, f32[2,16,256,256]{3,2,1,0:T(8,128)S(1)} %maximum_dynamic-update-slice_fusion.8, f32[2,256,256]{2,1,0:T(8,128)S(1)} %copy-done.6), kind=kOutput, calls=%fused_computation.66 | convolution fusion | flops 1613758464 | bytes 21233664 | tf_op jit(solution)/shard_map/ia,kaj->kij/dot_general | solution.py:75
  447.6 7.5 %fusion.13 = f32[1,16,256,256]{3,2,1,0:T(8,128)} fusion(f32[16,256,256]{2,1,0:T(8,128)S(1)} %copy-done.9, f32[16,256,256]{2,1,0:T(8,128)} %fusion.32, f32[16,256,256]{1,2,0:T(8,128)S(1)} %copy-done.10, f32[2,16,256,256]{3,2,1,0:T(8,128)S(1)} %maximum_dynamic-update-slice_fusion.8, f32[2,256,256]{2,1,0:T(8,128)S(1)} %copy-done.6), kind=kOutput, calls=%fused_computation.63 | convolution fusion | flops 1613758464 | bytes 21233664 | tf_op jit(solution)/shard_map/ia,kaj->kij/dot_general | solution.py:75
  455.1 6.6 maximum_add_fusion.1
  506.3 11.6 %add_add_fusion = (f32[2,256,32,128]{3,2,1,0:T(8,128)S(1)}, f32[2,256,32,128]{3,2,1,0:T(8,128)}) fusion(f32[2,256,32,128]{3,2,1,0:T(8,128)} %bitcast.415, f32[2,256,32,128]{3,2,1,0:T(8,128)} %param.7, f32[1,256,32,128]{3,2,1,0:T(8,128)} %get-tuple-element.82, f32[1,256,32,128]{3,2,1,0:T(8,128)S(1)} %get-tuple-element.81, f32[32,128]{1,0:T(8,128)S(1)} %compare_select_fusion.2), kind=kLoop, calls=%fused_computation.45 | loop fusion | flops 10485760 | bytes 41959424 | tf_op jit(solution)/shard_map/add | solution.py:143
  518.0 6.8 slice_multiply_fusion.1
  524.8 16.6 %fusion.2 = f32[2,256,32,128]{3,1,2,0:T(8,128)} fusion(f32[2,256,512,1]{2,1,3,0:T(8,128)S(1)} %bitcast.418, f32[512,32,128]{2,1,0:T(8,128)S(1)} %bitcast.416), kind=kOutput, calls=%fused_computation.39 | convolution fusion | flops 6442450944 | bytes 17825792 | tf_op jit(solution)/shard_map/ab,bmn->amn/dot_general | solution.py:67
  541.4 12.5 %fusion.1 = f32[2,256,32,128]{3,2,1,0:T(8,128)} fusion(f32[2,256,32,128]{3,2,1,0:T(8,128)S(1)} %bitcast.411, f32[1,256,32,128]{3,2,1,0:T(8,128)} %get-tuple-element.16, f32[1,256,32,128]{3,2,1,0:T(8,128)S(1)} %get-tuple-element.15, f32[2,256,32,128]{3,1,2,0:T(8,128)} %fusion.2), kind=kLoop, calls=%fused_computation.38 | loop fusion | flops 8388608 | bytes 33554432 | tf_op jit(solution)/shard_map/sub | solution.py:144
  553.9 127.5 %all-to-all-done.2 = f32[2,16,16,32,128]{4,3,2,0,1:T(8,128)} async-done(((f32[2,16,16,32,128]{4,3,2,0,1:T(8,128)}), f32[2,16,16,32,128]{4,3,2,0,1:T(8,128)}, u32[]{:S(2)}, u32[]{:S(2)}) %all-to-all-start.2) | async-done | bytes 8388640 | tf_op jit(solution)/shard_map/all_to_all | solution.py:104
  681.4 8.4 %copy.28 = f32[2,16,16,32,128]{4,3,2,1,0:T(8,128)} copy(f32[2,16,16,32,128]{4,3,2,0,1:T(8,128)} %all-to-all-done.2) | data formatting | bytes 16777216 | tf_op jit(solution)/shard_map/all_to_all | solution.py:104
  689.8 11.3 %add.390 = f32[2,256,32,128]{3,2,1,0:T(8,128)} add(f32[2,256,32,128]{3,2,1,0:T(8,128)} %fusion.1, f32[2,256,32,128]{3,2,1,0:T(8,128)} %bitcast.417) | non-fusion elementwise | flops 2097152 | bytes 25165824 | tf_op jit(solution)/shard_map/add | solution.py:146
  (188 shorter events, 135.7 us)
Async XLA Ops:
  8.3 6.7 copy-start.6
  8.3 189.0 %all-to-all-start = ((f32[2,16,16,32,128]{4,3,2,0,1:T(8,128)}), f32[2,16,16,32,128]{4,3,2,0,1:T(8,128)}, u32[]{:S(2)}, u32[]{:S(2)}) async-start(f32[2,16,16,32,128]{4,3,2,0,1:T(8,128)} %copy.21), calls=%async_computation | async-start | bytes 16777216 | tf_op jit(solution)/shard_map/all_to_all | solution.py:86
  15.0 12.6 %copy-start.12 = (f32[256,256]{1,0:T(8,128)}, f32[256,256]{1,0:T(8,128)S(1)}, u32[]{:S(2)}) copy-start(f32[256,256]{1,0:T(8,128)S(1)} %fusion.214) | copy-start | bytes 786436
  15.1 12.6 %copy-start.14 = (f32[256,256]{1,0:T(8,128)}, f32[256,256]{1,0:T(8,128)S(1)}, u32[]{:S(2)}) copy-start(f32[256,256]{1,0:T(8,128)S(1)} %get-tuple-element.89) | copy-start | bytes 786436
  15.1 12.6 %copy-start.16 = (f32[256,256]{1,0:T(8,128)}, f32[256,256]{1,0:T(8,128)S(1)}, u32[]{:S(2)}) copy-start(f32[256,256]{1,0:T(8,128)S(1)} %get-tuple-element.90) | copy-start | bytes 786436
  197.3 187.5 %all-to-all-start.1 = ((f32[2,16,16,32,128]{4,3,2,0,1:T(8,128)}), f32[2,16,16,32,128]{4,3,2,0,1:T(8,128)}, u32[]{:S(2)}, u32[]{:S(2)}) async-start(f32[2,16,16,32,128]{4,3,2,0,1:T(8,128)} %copy.24), calls=%async_computation.1 | async-start | bytes 16777216 | tf_op jit(solution)/shard_map/all_to_all | solution.py:112
  202.6 12.4 %copy-start.41 = (s32[256]{0:T(256)S(1)}, s32[256]{0:T(256)}, u32[]{:S(2)}) copy-start(s32[256]{0:T(256)} %param.10) | copy-start | bytes 3076
  202.6 12.4 %copy-start.49 = (f32[32]{0:T(128)S(1)}, f32[32]{0:T(128)}, u32[]{:S(2)}) copy-start(f32[32]{0:T(128)} %param.11) | copy-start | bytes 388
  202.7 13.4 %copy-start.43 = (s32[4096]{0:T(1024)S(1)}, s32[4096]{0:T(1024)}, u32[]{:S(2)}) copy-start(s32[4096]{0:T(1024)} %param.13) | copy-start | bytes 49156
  202.7 13.4 %copy-start.45 = (s32[4096]{0:T(1024)S(1)}, s32[4096]{0:T(1024)}, u32[]{:S(2)}) copy-start(s32[4096]{0:T(1024)} %param.12) | copy-start | bytes 49156
  220.4 47.9 %copy-start = (f32[1,16,256,256]{3,2,1,0:T(8,128)}, f32[1,16,256,256]{3,2,1,0:T(8,128)S(1)}, u32[]{:S(2)}) copy-start(f32[1,16,256,256]{3,2,1,0:T(8,128)S(1)} %get-tuple-element.91) | copy-start | bytes 12582916
  220.4 47.9 %copy-start.2 = (f32[1,16,256,256]{3,2,1,0:T(8,128)}, f32[1,16,256,256]{3,2,1,0:T(8,128)S(1)}, u32[]{:S(2)}) copy-start(f32[1,16,256,256]{3,2,1,0:T(8,128)S(1)} %get-tuple-element.92) | copy-start | bytes 12582916
  228.3 31.7 %copy-start.4 = (f32[2,16,256,256]{3,2,1,0:T(8,128)}, f32[2,16,256,256]{3,2,1,0:T(8,128)S(1)}, u32[]{:S(2)}) copy-start(f32[2,16,256,256]{3,2,1,0:T(8,128)S(1)} %maximum_dynamic-update-slice_fusion) | copy-start | bytes 25165828
  406.1 8.1 %slice-start.4 = ((s8[8388608]{0:T(1024)(128)(4,1)}), s8[4194304]{0:T(1024)(128)(4,1)S(1)}, s32[]{:S(2)}) async-start(s8[8388608]{0:T(1024)(128)(4,1)} %bitcast.413), calls=%async_computation.7 | async-start | bytes 8388608
  437.9 9.7 %copy-start.9 = (f32[16,256,256]{2,1,0:T(8,128)S(1)}, f32[16,256,256]{2,1,0:T(8,128)}, u32[]{:S(2)}) copy-start(f32[16,256,256]{2,1,0:T(8,128)} %fusion.28) | copy-start | bytes 12582916
  437.9 9.7 %copy-start.10 = (f32[16,256,256]{1,2,0:T(8,128)S(1)}, f32[16,256,256]{1,2,0:T(8,128)}, u32[]{:S(2)}) copy-start(f32[16,256,256]{1,2,0:T(8,128)} %fusion.29) | copy-start | bytes 12582916
  455.1 7.0 %copy-start.1 = (f32[1,16,256,256]{3,2,1,0:T(8,128)S(1)}, f32[1,16,256,256]{3,2,1,0:T(8,128)}, u32[]{:S(2)}) copy-start(f32[1,16,256,256]{3,2,1,0:T(8,128)} %copy-done) | copy-start | bytes 12582916
  455.1 9.9 %copy-start.3 = (f32[1,16,256,256]{3,2,1,0:T(8,128)S(1)}, f32[1,16,256,256]{3,2,1,0:T(8,128)}, u32[]{:S(2)}) copy-start(f32[1,16,256,256]{3,2,1,0:T(8,128)} %copy-done.2) | copy-start | bytes 12582916
  455.1 10.0 %copy-start.31 = (f32[1,16,32,128]{3,2,1,0:T(8,128)S(1)}, f32[1,16,32,128]{3,2,1,0:T(8,128)}, u32[]{:S(2)}) copy-start(f32[1,16,32,128]{3,2,1,0:T(8,128)} %get-tuple-element.47) | copy-start | bytes 786436
  455.1 10.3 %copy-start.32 = (f32[1,16,32,128]{3,2,1,0:T(8,128)S(1)}, f32[1,16,32,128]{3,2,1,0:T(8,128)}, u32[]{:S(2)}) copy-start(f32[1,16,32,128]{3,2,1,0:T(8,128)} %get-tuple-element.48) | copy-start | bytes 786436
  461.8 10.8 %copy-start.8 = (f32[2,16,256,256]{3,2,1,0:T(8,128)}, f32[2,16,256,256]{3,2,1,0:T(8,128)S(1)}, u32[]{:S(2)}) copy-start(f32[2,16,256,256]{3,2,1,0:T(8,128)S(1)} %maximum_add_fusion.1) | copy-start | bytes 25165828
  494.1 187.4 %all-to-all-start.2 = ((f32[2,16,16,32,128]{4,3,2,0,1:T(8,128)}), f32[2,16,16,32,128]{4,3,2,0,1:T(8,128)}, u32[]{:S(2)}, u32[]{:S(2)}) async-start(f32[2,16,16,32,128]{4,3,2,0,1:T(8,128)} %copy-done.11), calls=%async_computation.2 | async-start | bytes 16777216 | tf_op jit(solution)/shard_map/all_to_all | solution.py:104
  518.0 23.4 %slice-start.2 = ((s8[8388608]{0:T(1024)(128)(4,1)}), s8[4194304]{0:T(1024)(128)(4,1)S(1)}, s32[]{:S(2)}) async-start(s8[8388608]{0:T(1024)(128)(4,1)} %bitcast.410), calls=%async_computation.5 | async-start | bytes 8388608
  524.8 16.6 %slice-start.3 = ((s8[8388608]{0:T(1024)(128)(4,1)}), s8[4194304]{0:T(1024)(128)(4,1)S(1)}, s32[]{:S(2)}) async-start(s8[8388608]{0:T(1024)(128)(4,1)} %bitcast.410), calls=%async_computation.6 | async-start | bytes 8388608
  (35 other events, 135.3 us)
